TPU v7x, 256 devices: a whole 4x4x8 slice. The times are simulated.
256 devices in a mesh: tile: 16 (over z_lo, y), visit: 16 (over z_hi, x, core).
Axes of the slice: x: 4, y: 4, z: 8 (z_hi: 2, z_lo: 4; z = z_hi * 4 + z_lo), core: 2. Of those that a mesh axis runs over, the one named last changes fastest.
Arguments:
- template: float32 [2048, 2048], P('tile', 'visit'), may hold values from -6 to 6
- row_taps: float32 [16, 21], replicated, may hold values from -1 to 1
- col_taps: float32 [16, 21], replicated, may hold values from -1 to 1
- coeffs: float32 [16, 16, 6], P('visit'), may hold values from -2 to 2
- visits: float32 [16, 2048, 2048], P('visit', 'tile'), may hold values from -6 to 6
- boxes: int32 [16, 2], replicated, may hold values from 0 to 2048, as said below
Outputs:
- difference: float32 [16, 2048, 2048], P('visit', 'tile')
Inputs may be any that keep to these rules, and one draw needn't show every extreme that they name: boxes[v, 0] is the first column and boxes[v, 1] the number of columns of visit v's box, which lies within the 2048 columns; boxes[v, 1] is at least 512, and some visit covers all 2048 columns.
All inputs are finite; a program needn't handle non-finite values.
Results may differ from a plain program's by a relative error of at most 0.0003.
Values sent between devices are 32-bit elements; how exact they have to be, the bound alone decides.
No kernel may reach another device: no remote copies, remote signals or barrier semaphores. Data moves between devices by JAX's collectives and lax.ppermute only.
A program may use at most 128 MiB of HBM per device.

v0:
```python
import jax
import jax.numpy as jnp
from jax import lax
from jax.sharding import PartitionSpec as P


def extended_2(cells, sides, width):
    for axis, dim in sides:
        count = lax.axis_size(axis)
        ends = count - 1
        head = lax.slice_in_dim(cells, 0, width, axis=dim)
        tail = lax.slice_in_dim(cells, cells.shape[dim] - width, cells.shape[dim], axis=dim)
        cells = jnp.concatenate(
            [
                lax.ppermute(tail, axis, [(i, (i + 1) % count) for i in range(ends)]),
                cells,
                lax.ppermute(head, axis, [((i + 1) % count, i) for i in range(ends)]),
            ],
            axis=dim,
        )
    return cells


def coordinate(first, count, total):
    return 2.0 * ((first + jnp.arange(count)).astype(jnp.float32) + 0.5) / total - 1.0


def surface_terms(y_coord, x_coord):
    y_grid = y_coord[:, None] * jnp.ones_like(x_coord)[None, :]
    x_grid = jnp.ones_like(y_coord)[:, None] * x_coord[None, :]
    return jnp.stack(
        [jnp.ones_like(x_grid), x_grid, y_grid, x_grid * x_grid, x_grid * y_grid, y_grid * y_grid]
    )


def separable(padded, row_taps, col_taps, tile_rows, span):
    passed = jnp.zeros((row_taps.shape[0], tile_rows, padded.shape[1]), jnp.float32)
    for offset in range(row_taps.shape[1]):
        passed = (
            passed + row_taps[:, offset, None, None] * padded[None, offset : offset + tile_rows, :]
        )
    images = jnp.zeros((row_taps.shape[0], tile_rows, span), jnp.float32)
    for offset in range(col_taps.shape[1]):
        images = images + col_taps[:, offset, None, None] * passed[:, :, offset : offset + span]
    return images


def combine(coef, images, y_coord, first_col, full_width):
    terms = surface_terms(y_coord, coordinate(first_col, images.shape[2], full_width))
    weighted = jnp.einsum("vkt,krc->vtrc", coef, images, precision=lax.Precision.HIGHEST)
    return jnp.sum(weighted * terms[None], axis=1)


def local(template, row_taps, col_taps, coeffs, visits, boxes):
    half = row_taps.shape[1] // 2
    tile_rows, columns = template.shape
    full_width = columns * lax.axis_size("visit")
    total_rows = tile_rows * lax.axis_size("tile")
    y_coord = coordinate(lax.axis_index("tile") * tile_rows, tile_rows, total_rows)
    visit_count = visits.shape[0]
    extended = extended_2(template, (("tile", 0), ("visit", 1)), half)
    basis = separable(extended, row_taps, col_taps, tile_rows, columns)
    model = combine(
        coeffs,
        lax.all_gather(basis, "visit", axis=2, tiled=True),
        y_coord,
        jnp.int32(0),
        full_width,
    )
    local_boxes = lax.dynamic_slice_in_dim(
        boxes, lax.axis_index("visit") * visit_count, visit_count, 0
    )
    column_index = jnp.arange(full_width)
    inside = (column_index[None, :] >= local_boxes[:, 0:1]) & (
        column_index[None, :] < local_boxes[:, 0:1] + local_boxes[:, 1:2]
    )
    return jnp.where(inside[:, None, :], visits - model, jnp.float32(0.0))


def solution(mesh):
    placed = (P("tile", "visit"), P(), P(), P("visit", None, None), P("visit", "tile", None), P())
    return jax.shard_map(
        local, mesh=mesh, in_specs=placed, out_specs=P("visit", "tile", None), check_vma=False
    )
```

profile of v0, /device:TPU:1, one launch (start us, length us, event | category | flops | bytes accessed | tf_op | source)
XLA Modules:
  0.0 257.7 jit_solution(8569968261775360518)
XLA Ops:
  6.5 0.0 copy-start
  6.5 0.0 all-gather.2.cloned.1.call-start
  6.5 0.7 fusion.30
  7.3 1.3 collective-permute-start.1
  8.6 4.6 %collective-permute-start = (f32[10,128]{1,0:T(8,128)S(1)}, f32[10,128]{1,0:T(8,128)S(1)}, u32[]{:S(2)}, u32[]{:S(2)}) collective-permute-start(f32[10,128]{1,0:T(8,128)S(1)} %get-tuple-element.70), channel_id=1, source_target_pairs={{0,16},{16,32},{32,48},{48,64},{64,80},{80,96},{96,112},{112,128},... | collective-permute-start | bytes 15368 | tf_op jit(solution)/shard_map/ppermute | solution.py:15
  13.2 1.9 slice_reduce_fusion.40
  15.1 1.9 slice_reduce_fusion.41
  17.1 1.0 slice_reduce_fusion.21
  18.0 0.0 collective-permute-done.1
  18.0 0.0 collective-permute-done
  18.1 0.9 pad_maximum_fusion.1
  18.9 0.1 fusion.29
  19.0 5.0 %collective-permute-start.3 = (f32[148,10]{1,0:T(8,128)S(1)}, f32[148,10]{1,0:T(8,128)S(1)}, u32[]{:S(2)}, u32[]{:S(2)}) collective-permute-start(f32[148,10]{1,0:T(8,128)S(1)} %get-tuple-element.69), channel_id=1, source_target_pairs={{1,0},{2,1},{3,2},{4,3},{5,4},{6,5},{7,6},{8,7},{9,8},{10,9},{11,1... | collective-permute-start | bytes 17768 | tf_op jit(solution)/shard_map/ppermute | solution.py:17
  24.0 1.9 collective-permute-start.2
  25.9 1.0 slice_reduce_fusion.1
  26.9 0.0 collective-permute-done.3
  26.9 0.5 collective-permute-done.2
  27.4 1.0 pad_maximum_fusion
  28.3 0.2 fusion.27
  28.6 2.9 %multiply_add_fusion = f32[16,128,148]{2,0,1:T(8,128)S(1)} fusion(f32[128,148]{1,0:T(8,128)S(1)} %get-tuple-element.48, f32[16]{0:T(128)S(1)} %get-tuple-element.46, f32[128,148]{1,0:T(8,128)S(1)} %get-tuple-element.49, f32[16]{0:T(128)S(1)} %get-tuple-element.45, f32[128,148]{1,0:T(8,128)S(1)} %get-tuple-element.50, f32[16]{0:T(128)S(1)} %get-tuple-element.27, ...), kind=kLoop, calls=%fused_computation.2 | loop fusion | flops 12427264 | bytes 2805056 | tf_op jit(solution)/shard_map/add | solution.py:40
  31.5 6.5 %fusion.1 = f32[16,128,128]{2,0,1:T(8,128)} fusion(f32[16,128,148]{2,0,1:T(8,128)S(1)} %multiply_add_fusion, f32[16]{0:T(128)S(1)} %get-tuple-element.25, f32[16]{0:T(128)S(1)} %get-tuple-element.24, f32[16]{0:T(128)S(1)} %get-tuple-element.6, f32[16]{0:T(128)S(1)} %get-tuple-element.7, f32[16]{0:T(128)S(1)} %get-tuple-element.8, f32[16]{0:T(128)S(1)} %get-tuple-element.9, ...), kind=kLoop, calls=%fused_computation.4 | loop fusion | flops 10747904 | bytes 23070016 | tf_op jit(solution)/shard_map/add | solution.py:44
  38.0 0.0 all-gather.2.cloned.1.call-update
  38.0 0.0 copy-done
  38.0 0.1 constant_dynamic-slice_fusion
  38.1 0.6 fusion.31
  40.1 0.6 broadcast_multiply_fusion
  40.7 0.5 stack.18
  41.2 0.6 stack.19
  41.8 1.5 stack.20
  43.4 1.6 stack.21
  44.9 1.5 stack_broadcast_in_dim.3
  46.5 0.0 copy-start.2
  46.5 20.1 %stack.22 = f32[6,128,2048]{2,0,1:T(8,128)} concatenate(f32[1,128,2048]{2,0,1:T(1,128)} %stack_broadcast_in_dim.3, f32[1,128,2048]{2,0,1:T(1,128)S(1)} %stack.18, f32[1,128,2048]{2,0,1:T(1,128)S(1)} %stack.19, f32[1,128,2048]{2,0,1:T(1,128)} %stack.20, f32[1,128,2048]{2,0,1:T(1,128)S(1)} %broadcast_multiply_fusion, f32[1,128,2048]{2,0,1:T(1,128)} %stack.21), dimensions={0} | concatenate | bytes 12582912 | tf_op jit(solution)/shard_map/stack | solution.py:31
  66.6 0.7 fusion.22
  67.3 0.0 copy-start.1
  67.3 165.3 %all-gather.2.cloned.1.call-done = f32[16,128,2048]{2,0,1:T(8,128)} async-done(((f32[16,128,128]{2,0,1:T(8,128)}), f32[16,128,2048]{2,0,1:T(8,128)}) %all-gather.2.cloned.1.call-update) | async-done | bytes 16777232 | tf_op jit(solution)/shard_map/all_gather | solution.py:65
  232.6 0.0 copy-done.2
  232.6 17.1 %fusion = f32[128,2048]{1,0:T(8,128)S(1)} fusion(f32[6,128,2048]{2,0,1:T(8,128)} %stack.22, f32[16,128,2048]{2,0,1:T(8,128)} %all-gather.2.cloned.1.call-done, f32[1,16,6]{1,0,2:T(1,128)S(1)} %copy-done.2), kind=kOutput, calls=%fused_computation.1 | convolution fusion | flops 304873472 | bytes 24117632 | tf_op jit(solution)/shard_map/vkt,krc->vtrc/dot_general | solution.py:50
  249.7 0.0 copy-done.1
  249.7 1.1 fusion.21
  (4 shorter events, 0.0 us)
Async XLA Ops:
  6.5 31.5 %copy-start = (s32[16,2]{0,1:T(2,128)S(1)}, s32[16,2]{0,1:T(2,128)}, u32[]{:S(2)}) copy-start(s32[16,2]{0,1:T(2,128)} %param.11) | copy-start | bytes 388
  6.5 226.0 %all-gather.2.cloned.1.call-start = ((), (), s32[]{:S(2)}) async-start(), calls=%async_computation | async-start | bytes 17825792 | tf_op jit(solution)/shard_map/all_gather | solution.py:65
  7.3 10.8 %collective-permute-start.1 = (f32[10,128]{1,0:T(8,128)S(1)}, f32[10,128]{1,0:T(8,128)S(1)}, u32[]{:S(2)}, u32[]{:S(2)}) collective-permute-start(f32[10,128]{1,0:T(8,128)S(1)} %get-tuple-element.71), channel_id=1, source_target_pairs={{16,0},{32,16},{48,32},{64,48},{80,64},{96,80},{112,96},{128,112},... | collective-permute-start | bytes 15368 | tf_op jit(solution)/shard_map/ppermute | solution.py:17
  8.6 9.5 %collective-permute-start = (f32[10,128]{1,0:T(8,128)S(1)}, f32[10,128]{1,0:T(8,128)S(1)}, u32[]{:S(2)}, u32[]{:S(2)}) collective-permute-start(f32[10,128]{1,0:T(8,128)S(1)} %get-tuple-element.70), channel_id=1, source_target_pairs={{0,16},{16,32},{32,48},{48,64},{64,80},{80,96},{96,112},{112,128},... | collective-permute-start | bytes 15368 | tf_op jit(solution)/shard_map/ppermute | solution.py:15
  19.0 7.9 %collective-permute-start.3 = (f32[148,10]{1,0:T(8,128)S(1)}, f32[148,10]{1,0:T(8,128)S(1)}, u32[]{:S(2)}, u32[]{:S(2)}) collective-permute-start(f32[148,10]{1,0:T(8,128)S(1)} %get-tuple-element.69), channel_id=1, source_target_pairs={{1,0},{2,1},{3,2},{4,3},{5,4},{6,5},{7,6},{8,7},{9,8},{10,9},{11,1... | collective-permute-start | bytes 17768 | tf_op jit(solution)/shard_map/ppermute | solution.py:17
  24.0 3.4 %collective-permute-start.2 = (f32[148,10]{1,0:T(8,128)S(1)}, f32[148,10]{1,0:T(8,128)S(1)}, u32[]{:S(2)}, u32[]{:S(2)}) collective-permute-start(f32[148,10]{1,0:T(8,128)S(1)} %get-tuple-element.68), channel_id=1, source_target_pairs={{0,1},{1,2},{2,3},{3,4},{4,5},{5,6},{6,7},{7,8},{8,9},{9,10},{10,1... | collective-permute-start | bytes 17768 | tf_op jit(solution)/shard_map/ppermute | solution.py:15
  46.5 186.1 %copy-start.2 = (f32[1,16,6]{1,0,2:T(1,128)S(1)}, f32[1,16,6]{1,0,2:T(1,128)}, u32[]{:S(2)}) copy-start(f32[1,16,6]{1,0,2:T(1,128)} %param.9) | copy-start | bytes 1156
  67.3 182.5 %copy-start.1 = (f32[1,128,2048]{2,1,0:T(8,128)S(1)}, f32[1,128,2048]{2,1,0:T(8,128)}, u32[]{:S(2)}) copy-start(f32[1,128,2048]{2,1,0:T(8,128)} %param.10) | copy-start | bytes 3145732
Sparse Core Ops, SparseCore 0:
  38.2 194.3 all-gather.1
where the time goes:
time: 260 us; the launch traced here: 258 us
  waiting for transfers between devices  166 us (64%)
  local copies, waits for them, and re-layouts  33.3 us (13%)
  matrix products  17.1 us (7%)
  between operations  14.9 us (6%)
  other arithmetic  13.6 us (5%)
  starting transfers between devices  12.9 us (5%)
    all_gather x1, waiting for transfers between devices, local(): lax.all_gather(basis, 'visit', axis=2, tiled=True)  165 us
    another operation x6, local copies, waits for them, and re-layouts, surface_terms(): jnp.stack([jnp.ones_like(x_grid), x_grid, y_grid, x_grid * x_grid, x_grid...  25.9 us
    dot_general x1, matrix products, combine(): jnp.einsum('vkt,krc->vtrc', coef, images, precision=lax.Precision.HIGHEST)  17.1 us
    ppermute x2, starting transfers between devices, extended_2(): lax.ppermute(tail, axis, [(i, (i + 1) % count) for i in range(ends)])  6.57 us
    add x1, other arithmetic, separable(): images + col_taps[:, offset, None, None] * passed[:, :, offset:offset + s...  6.55 us
    ppermute x2, starting transfers between devices, extended_2(): lax.ppermute(head, axis, [((i + 1) % count, i) for i in range(ends)])  6.29 us
  transfers between devices with their start and end apart: 5, of which 2 were waited for; matrix products, arithmetic and copies ran while one was open for 13% of the time, Pallas kernels for 0%

commit v1 on v0

--- a/solution.py
+++ b/solution.py
@@ -58,15 +58,11 @@
     total_rows = tile_rows * lax.axis_size("tile")
     y_coord = coordinate(lax.axis_index("tile") * tile_rows, tile_rows, total_rows)
     visit_count = visits.shape[0]
+    all_coeffs = lax.all_gather(coeffs, "visit", axis=0, tiled=True)
     extended = extended_2(template, (("tile", 0), ("visit", 1)), half)
     basis = separable(extended, row_taps, col_taps, tile_rows, columns)
-    model = combine(
-        coeffs,
-        lax.all_gather(basis, "visit", axis=2, tiled=True),
-        y_coord,
-        jnp.int32(0),
-        full_width,
-    )
+    models = combine(all_coeffs, basis, y_coord, lax.axis_index("visit") * columns, full_width)
+    model = lax.all_to_all(models, "visit", 0, 2, tiled=True)
     local_boxes = lax.dynamic_slice_in_dim(
         boxes, lax.axis_index("visit") * visit_count, visit_count, 0
     )

time: 260 us -> 112 us (0.43)
  the two profiles are of different devices: /device:TPU:1 before, /device:TPU:32 now
where the time goes in v1:
time: 112 us; the launch traced here: 111 us
  blocking collectives  35.4 us (32%)
  waiting for transfers between devices  28.7 us (26%)
  starting transfers between devices  17.2 us (15%)
  local copies, waits for them, and re-layouts  12.6 us (11%)
  matrix products  11 us (10%)
  other arithmetic  5.05 us (5%)
  between operations  1.48 us (1%)
    all_gather x1, blocking collectives, local(): all_coeffs = lax.all_gather(coeffs, 'visit', axis=0, tiled=True)  35.4 us
    all_to_all x1, waiting for transfers between devices, local(): model = lax.all_to_all(models, 'visit', 0, 2, tiled=True)  28.7 us
    dot_general x1, matrix products, combine(): jnp.einsum('vkt,krc->vtrc', coef, images, precision=lax.Precision.HIGHEST)  11 us
    all_to_all x1, starting transfers between devices, local(): model = lax.all_to_all(models, 'visit', 0, 2, tiled=True)  6.67 us
    ppermute x2, starting transfers between devices, extended_2(): lax.ppermute(head, axis, [((i + 1) % count, i) for i in range(ends)])  5.76 us
    ppermute x2, starting transfers between devices, extended_2(): lax.ppermute(tail, axis, [(i, (i + 1) % count) for i in range(ends)])  4.77 us
    add x1, other arithmetic, separable(): passed + row_taps[:, offset, None, None] * padded[None, offset:offset + t...  2.88 us
    slice x2, local copies, waits for them, and re-layouts, separable(): row_taps[:, offset, None, None] * padded[None, offset:offset + tile_rows, :]  2.88 us
  transfers between devices with their start and end apart: 5, of which 1 were waited for; matrix products, arithmetic and copies ran while one was open for 8% of the time, Pallas kernels for 0%

profile of v1, /device:TPU:32, one launch (start us, length us, event | category | flops | bytes accessed | tf_op | source)
XLA Modules:
  0.0 111.4 jit_solution(16979642348646727575)
XLA Ops:
  0.0 0.0 copy-start
  0.0 0.0 copy-start.2
  0.0 0.8 fusion.72
  0.8 3.5 %collective-permute-start = (f32[10,128]{1,0:T(8,128)S(1)}, f32[10,128]{1,0:T(8,128)S(1)}, u32[]{:S(2)}, u32[]{:S(2)}) collective-permute-start(f32[10,128]{1,0:T(8,128)S(1)} %get-tuple-element.70), channel_id=1, source_target_pairs={{0,16},{16,32},{32,48},{48,64},{64,80},{80,96},{96,112},{112,128},... | collective-permute-start | bytes 15368 | tf_op jit(solution)/shard_map/ppermute | solution.py:15
  4.3 4.5 %collective-permute-start.1 = (f32[10,128]{1,0:T(8,128)S(1)}, f32[10,128]{1,0:T(8,128)S(1)}, u32[]{:S(2)}, u32[]{:S(2)}) collective-permute-start(f32[10,128]{1,0:T(8,128)S(1)} %get-tuple-element.71), channel_id=1, source_target_pairs={{16,0},{32,16},{48,32},{64,48},{80,64},{96,80},{112,96},{128,112},... | collective-permute-start | bytes 15368 | tf_op jit(solution)/shard_map/ppermute | solution.py:17
  8.7 1.9 %slice_reduce_fusion.40 = (f32[16]{0:T(128)S(1)}, f32[16]{0:T(128)S(1)}, f32[16]{0:T(128)S(1)}, f32[16]{0:T(128)S(1)}, f32[16]{0:T(128)S(1)}, /*index=5*/f32[16]...) fusion(f32[16,21]{1,0:T(8,128)} %param.7), kind=kLoop, calls=%fused_computation.113 | loop fusion | bytes 2432 | tf_op jit(solution)/shard_map/slice | solution.py:40
  10.7 1.9 %slice_reduce_fusion.41 = (f32[16]{0:T(128)S(1)}, f32[16]{0:T(128)S(1)}, f32[16]{0:T(128)S(1)}, f32[16]{0:T(128)S(1)}, f32[16]{0:T(128)S(1)}, /*index=5*/f32[16]...) fusion(f32[16,21]{1,0:T(8,128)} %param.8), kind=kLoop, calls=%fused_computation.114 | loop fusion | bytes 2432 | tf_op jit(solution)/shard_map/slice | solution.py:44
  12.6 0.2 broadcast_multiply_fusion
  12.8 1.0 slice_reduce_fusion.21
  13.8 0.0 collective-permute-done
  13.8 0.0 collective-permute-done.1
  13.8 0.9 pad_maximum_fusion.1
  14.7 0.1 fusion.71
  14.8 1.3 %collective-permute-start.2 = (f32[148,10]{1,0:T(8,128)S(1)}, f32[148,10]{1,0:T(8,128)S(1)}, u32[]{:S(2)}, u32[]{:S(2)}) collective-permute-start(f32[148,10]{1,0:T(8,128)S(1)} %get-tuple-element.68), channel_id=1, source_target_pairs={{0,1},{1,2},{2,3},{3,4},{4,5},{5,6},{6,7},{7,8},{8,9},{9,10},{10,1... | collective-permute-start | bytes 17768 | tf_op jit(solution)/shard_map/ppermute | solution.py:15
  16.1 1.3 %collective-permute-start.3 = (f32[148,10]{1,0:T(8,128)S(1)}, f32[148,10]{1,0:T(8,128)S(1)}, u32[]{:S(2)}, u32[]{:S(2)}) collective-permute-start(f32[148,10]{1,0:T(8,128)S(1)} %get-tuple-element.69), channel_id=1, source_target_pairs={{1,0},{2,1},{3,2},{4,3},{5,4},{6,5},{7,6},{8,7},{9,8},{10,9},{11,1... | collective-permute-start | bytes 17768 | tf_op jit(solution)/shard_map/ppermute | solution.py:17
  17.4 1.0 slice_reduce_fusion.1
  18.3 0.7 copy.14
  19.1 0.2 stack.17
  19.3 0.2 stack.19
  19.5 0.6 stack.20
  20.2 35.4 %all_gather.3 = f32[16,16,6]{1,2,0:T(8,128)S(1)} all-gather(f32[1,16,6]{1,2,0:T(8,128)S(1)} %copy.14), channel_id=1, replica_groups=mesh['tile'=16,'visit'=16] {'visit'}, dimensions={0}, use_global_device_ids=true | all-gather | bytes 6528 | tf_op jit(solution)/shard_map/all_gather | solution.py:61
  55.5 0.0 collective-permute-done.2
  55.5 0.0 collective-permute-done.3
  55.5 0.0 copy-done.2
  55.5 0.1 pad_maximum_fusion
  55.7 0.2 fusion.69
  55.9 2.9 %multiply_add_fusion = f32[16,128,148]{2,0,1:T(8,128)S(1)} fusion(f32[128,148]{1,0:T(8,128)S(1)} %get-tuple-element.48, f32[16]{0:T(128)S(1)} %get-tuple-element.46, f32[128,148]{1,0:T(8,128)S(1)} %get-tuple-element.49, f32[16]{0:T(128)S(1)} %get-tuple-element.45, f32[128,148]{1,0:T(8,128)S(1)} %get-tuple-element.50, f32[16]{0:T(128)S(1)} %get-tuple-element.27, ...), kind=kLoop, calls=%fused_computation.2 | loop fusion | flops 12427264 | bytes 2805056 | tf_op jit(solution)/shard_map/add | solution.py:40
  58.8 11.0 %fusion = f32[16,128,128]{2,0,1:T(8,128)S(1)} fusion(f32[6,128,128]{2,0,1:T(8,128)S(1)} %stack.20, f32[16,128,148]{2,0,1:T(8,128)S(1)} %multiply_add_fusion, f32[16]{0:T(128)S(1)} %get-tuple-element.25, f32[16]{0:T(128)S(1)} %get-tuple-element.24, f32[16]{0:T(128)S(1)} %get-tuple-element.6, f32[16]{0:T(128)S(1)} %get-tuple-element.7, ...), kind=kOutput, calls=%fused_computation.1 | convolution fusion | flops 315621376 | bytes 23669248 | tf_op jit(solution)/shard_map/vkt,krc->vtrc/dot_general | solution.py:50
  69.7 0.0 copy-start.1
  69.8 1.3 %copy.16 = f32[16,128,128]{2,1,0:T(8,128)} copy(f32[16,128,128]{2,0,1:T(8,128)S(1)} %fusion) | data formatting | bytes 2097152 | tf_op jit(solution)/shard_map/reduce_sum | solution.py:51
  71.0 6.7 %all-to-all-start = ((f32[16,128,128]{2,1,0:T(8,128)}), f32[16,128,128]{2,1,0:T(8,128)S(1)}, u32[]{:S(2)}, u32[]{:S(2)}) async-start(f32[16,128,128]{2,1,0:T(8,128)} %copy.16), calls=%async_computation | async-start | bytes 2097152 | tf_op jit(solution)/shard_map/all_to_all | solution.py:65
  77.7 0.0 copy-done.1
  77.7 0.3 copy.18
  78.1 0.0 copy-done
  78.1 0.1 constant_dynamic-slice_fusion
  78.2 0.6 fusion.73
  80.0 0.6 fusion.66
  80.6 28.7 %all-to-all-done = f32[16,128,128]{2,1,0:T(8,128)S(1)} async-done(((f32[16,128,128]{2,1,0:T(8,128)}), f32[16,128,128]{2,1,0:T(8,128)S(1)}, u32[]{:S(2)}, u32[]{:S(2)}) %all-to-all-start) | async-done | bytes 1048608 | tf_op jit(solution)/shard_map/all_to_all | solution.py:65
  109.3 0.3 copy.17
  109.6 0.4 fusion.42
  110.0 1.3 %copy.19 = f32[1,128,2048]{2,1,0:T(8,128)} copy(f32[1,128,2048]{1,2,0:T(8,128)S(1)} %fusion.42) | data formatting | bytes 2097152 | tf_op jit(solution)/shard_map/jit(_where)/select_n | solution.py:73
  (6 shorter events, 0.1 us)
Async XLA Ops:
  0.0 78.1 %copy-start = (s32[16,2]{0,1:T(2,128)S(1)}, s32[16,2]{0,1:T(2,128)}, u32[]{:S(2)}) copy-start(s32[16,2]{0,1:T(2,128)} %param.11) | copy-start | bytes 388
  0.0 55.5 %copy-start.2 = (f32[128,128]{1,0:T(8,128)S(1)}, f32[128,128]{1,0:T(8,128)}, u32[]{:S(2)}) copy-start(f32[128,128]{1,0:T(8,128)} %param.6) | copy-start | bytes 196612
  0.8 13.0 %collective-permute-start = (f32[10,128]{1,0:T(8,128)S(1)}, f32[10,128]{1,0:T(8,128)S(1)}, u32[]{:S(2)}, u32[]{:S(2)}) collective-permute-start(f32[10,128]{1,0:T(8,128)S(1)} %get-tuple-element.70), channel_id=1, source_target_pairs={{0,16},{16,32},{32,48},{48,64},{64,80},{80,96},{96,112},{112,128},... | collective-permute-start | bytes 15368 | tf_op jit(solution)/shard_map/ppermute | solution.py:15
  4.3 9.6 %collective-permute-start.1 = (f32[10,128]{1,0:T(8,128)S(1)}, f32[10,128]{1,0:T(8,128)S(1)}, u32[]{:S(2)}, u32[]{:S(2)}) collective-permute-start(f32[10,128]{1,0:T(8,128)S(1)} %get-tuple-element.71), channel_id=1, source_target_pairs={{16,0},{32,16},{48,32},{64,48},{80,64},{96,80},{112,96},{128,112},... | collective-permute-start | bytes 15368 | tf_op jit(solution)/shard_map/ppermute | solution.py:17
  14.8 40.8 %collective-permute-start.2 = (f32[148,10]{1,0:T(8,128)S(1)}, f32[148,10]{1,0:T(8,128)S(1)}, u32[]{:S(2)}, u32[]{:S(2)}) collective-permute-start(f32[148,10]{1,0:T(8,128)S(1)} %get-tuple-element.68), channel_id=1, source_target_pairs={{0,1},{1,2},{2,3},{3,4},{4,5},{5,6},{6,7},{7,8},{8,9},{9,10},{10,1... | collective-permute-start | bytes 17768 | tf_op jit(solution)/shard_map/ppermute | solution.py:15
  16.1 39.5 %collective-permute-start.3 = (f32[148,10]{1,0:T(8,128)S(1)}, f32[148,10]{1,0:T(8,128)S(1)}, u32[]{:S(2)}, u32[]{:S(2)}) collective-permute-start(f32[148,10]{1,0:T(8,128)S(1)} %get-tuple-element.69), channel_id=1, source_target_pairs={{1,0},{2,1},{3,2},{4,3},{5,4},{6,5},{7,6},{8,7},{9,8},{10,9},{11,1... | collective-permute-start | bytes 17768 | tf_op jit(solution)/shard_map/ppermute | solution.py:17
  69.7 8.0 %copy-start.1 = (f32[1,128,2048]{2,1,0:T(8,128)S(1)}, f32[1,128,2048]{2,1,0:T(8,128)}, u32[]{:S(2)}) copy-start(f32[1,128,2048]{2,1,0:T(8,128)} %param.10) | copy-start | bytes 3145732
  71.0 38.3 %all-to-all-start = ((f32[16,128,128]{2,1,0:T(8,128)}), f32[16,128,128]{2,1,0:T(8,128)S(1)}, u32[]{:S(2)}, u32[]{:S(2)}) async-start(f32[16,128,128]{2,1,0:T(8,128)} %copy.16), calls=%async_computation | async-start | bytes 2097152 | tf_op jit(solution)/shard_map/all_to_all | solution.py:65

commit v2 on v1

--- a/solution.py
+++ b/solution.py
@@ -58,7 +58,8 @@
     total_rows = tile_rows * lax.axis_size("tile")
     y_coord = coordinate(lax.axis_index("tile") * tile_rows, tile_rows, total_rows)
     visit_count = visits.shape[0]
-    all_coeffs = lax.all_gather(coeffs, "visit", axis=0, tiled=True)
+    copies = jnp.broadcast_to(coeffs, (lax.axis_size("visit"),) + coeffs.shape[1:])
+    all_coeffs = lax.all_to_all(copies, "visit", 0, 0, tiled=True)
     extended = extended_2(template, (("tile", 0), ("visit", 1)), half)
     basis = separable(extended, row_taps, col_taps, tile_rows, columns)
     models = combine(all_coeffs, basis, y_coord, lax.axis_index("visit") * columns, full_width)

time: 112 us -> 99.4 us (0.89)
  blocking collectives: 35.4 us -> 0 us
  starting transfers between devices: 17.2 us -> 38.3 us
    all_gather x1 -> x0, blocking collectives: 35.4 us -> none  [local(): all_coeffs = lax.all_gather(coeffs, 'visit', axis=0, tiled=True)]
    all_to_all x0 -> x1, starting transfers between devices: none -> 10.1 us  [local(): all_coeffs = lax.all_to_all(copies, 'visit', 0, 0, tiled=True)]
    all_to_all x1, starting transfers between devices: 6.67 us -> 16.6 us  [local(): model = lax.all_to_all(models, 'visit', 0, 2, tiled=True)]
  transfers between devices with their start and end apart: 5 -> 6, of which waited for: 1 -> 2; matrix products, arithmetic and copies ran while one was open for 8% -> 14% of each run, Pallas kernels for 0% -> 0%
where the time goes in v2:
time: 99.4 us; the launch traced here: 98.7 us
  starting transfers between devices  38.3 us (39%)
  waiting for transfers between devices  29.6 us (30%)
  local copies, waits for them, and re-layouts  13.2 us (13%)
  matrix products  11 us (11%)
  other arithmetic  5.05 us (5%)
  between operations  1.5 us (2%)
    all_to_all x1, waiting for transfers between devices, local(): model = lax.all_to_all(models, 'visit', 0, 2, tiled=True)  28.7 us
    all_to_all x1, starting transfers between devices, local(): model = lax.all_to_all(models, 'visit', 0, 2, tiled=True)  16.6 us
    dot_general x1, matrix products, combine(): jnp.einsum('vkt,krc->vtrc', coef, images, precision=lax.Precision.HIGHEST)  11 us
    all_to_all x1, starting transfers between devices, local(): all_coeffs = lax.all_to_all(copies, 'visit', 0, 0, tiled=True)  10.1 us
    ppermute x2, starting transfers between devices, extended_2(): lax.ppermute(tail, axis, [(i, (i + 1) % count) for i in range(ends)])  5.78 us
    ppermute x2, starting transfers between devices, extended_2(): lax.ppermute(head, axis, [((i + 1) % count, i) for i in range(ends)])  5.76 us
    add x1, other arithmetic, separable(): passed + row_taps[:, offset, None, None] * padded[None, offset:offset + t...  2.88 us
    slice x2, local copies, waits for them, and re-layouts, separable(): row_taps[:, offset, None, None] * padded[None, offset:offset + tile_rows, :]  2.88 us
  transfers between devices with their start and end apart: 6, of which 2 were waited for; matrix products, arithmetic and copies ran while one was open for 14% of the time, Pallas kernels for 0%

profile of v2, /device:TPU:32, one launch (start us, length us, event | category | flops | bytes accessed | tf_op | source)
XLA Modules:
  0.0 98.7 jit_solution(3940182608904754679)
XLA Ops:
  0.0 0.0 copy-start
  0.0 0.0 copy-start.2
  0.0 0.8 fusion.72
  0.8 3.5 %collective-permute-start = (f32[10,128]{1,0:T(8,128)S(1)}, f32[10,128]{1,0:T(8,128)S(1)}, u32[]{:S(2)}, u32[]{:S(2)}) collective-permute-start(f32[10,128]{1,0:T(8,128)S(1)} %get-tuple-element.70), channel_id=1, source_target_pairs={{0,16},{16,32},{32,48},{48,64},{64,80},{80,96},{96,112},{112,128},... | collective-permute-start | bytes 15368 | tf_op jit(solution)/shard_map/ppermute | solution.py:15
  4.3 4.5 %collective-permute-start.1 = (f32[10,128]{1,0:T(8,128)S(1)}, f32[10,128]{1,0:T(8,128)S(1)}, u32[]{:S(2)}, u32[]{:S(2)}) collective-permute-start(f32[10,128]{1,0:T(8,128)S(1)} %get-tuple-element.71), channel_id=1, source_target_pairs={{16,0},{32,16},{48,32},{64,48},{80,64},{96,80},{112,96},{128,112},... | collective-permute-start | bytes 15368 | tf_op jit(solution)/shard_map/ppermute | solution.py:17
  8.7 0.7 copy.24
  9.4 0.6 broadcast_in_dim.14
  10.1 10.1 %all-to-all-start = ((f32[16,16,6]{1,2,0:T(8,128)}), f32[16,16,6]{1,2,0:T(8,128)S(1)}, u32[]{:S(2)}, u32[]{:S(2)}) async-start(f32[16,16,6]{1,2,0:T(8,128)} %broadcast_in_dim.14), calls=%async_computation | async-start | bytes 131072 | tf_op jit(solution)/shard_map/all_to_all | solution.py:62
  20.2 1.9 %slice_reduce_fusion.40 = (f32[16]{0:T(128)S(1)}, f32[16]{0:T(128)S(1)}, f32[16]{0:T(128)S(1)}, f32[16]{0:T(128)S(1)}, f32[16]{0:T(128)S(1)}, /*index=5*/f32[16]...) fusion(f32[16,21]{1,0:T(8,128)} %param.7), kind=kLoop, calls=%fused_computation.113 | loop fusion | bytes 2432 | tf_op jit(solution)/shard_map/slice | solution.py:40
  22.2 1.9 %slice_reduce_fusion.41 = (f32[16]{0:T(128)S(1)}, f32[16]{0:T(128)S(1)}, f32[16]{0:T(128)S(1)}, f32[16]{0:T(128)S(1)}, f32[16]{0:T(128)S(1)}, /*index=5*/f32[16]...) fusion(f32[16,21]{1,0:T(8,128)} %param.8), kind=kLoop, calls=%fused_computation.114 | loop fusion | bytes 2432 | tf_op jit(solution)/shard_map/slice | solution.py:44
  24.1 0.2 broadcast_multiply_fusion
  24.3 1.0 slice_reduce_fusion.21
  25.3 0.0 collective-permute-done
  25.3 0.0 collective-permute-done.1
  25.3 0.9 pad_maximum_fusion.1
  26.1 0.1 fusion.71
  26.2 2.3 %collective-permute-start.2 = (f32[148,10]{1,0:T(8,128)S(1)}, f32[148,10]{1,0:T(8,128)S(1)}, u32[]{:S(2)}, u32[]{:S(2)}) collective-permute-start(f32[148,10]{1,0:T(8,128)S(1)} %get-tuple-element.68), channel_id=1, source_target_pairs={{0,1},{1,2},{2,3},{3,4},{4,5},{5,6},{6,7},{7,8},{8,9},{9,10},{10,1... | collective-permute-start | bytes 17768 | tf_op jit(solution)/shard_map/ppermute | solution.py:15
  28.5 1.3 %collective-permute-start.3 = (f32[148,10]{1,0:T(8,128)S(1)}, f32[148,10]{1,0:T(8,128)S(1)}, u32[]{:S(2)}, u32[]{:S(2)}) collective-permute-start(f32[148,10]{1,0:T(8,128)S(1)} %get-tuple-element.69), channel_id=1, source_target_pairs={{1,0},{2,1},{3,2},{4,3},{5,4},{6,5},{7,6},{8,7},{9,8},{10,9},{11,1... | collective-permute-start | bytes 17768 | tf_op jit(solution)/shard_map/ppermute | solution.py:17
  29.8 1.0 slice_reduce_fusion.1
  30.9 0.2 stack.17
  31.1 0.2 stack.19
  31.3 0.6 stack.20
  32.0 0.0 collective-permute-done.2
  32.0 0.9 collective-permute-done.3
  32.8 0.0 copy-done.2
  32.8 0.1 pad_maximum_fusion
  33.0 0.2 fusion.69
  33.2 2.9 %multiply_add_fusion = f32[16,128,148]{2,0,1:T(8,128)S(1)} fusion(f32[128,148]{1,0:T(8,128)S(1)} %get-tuple-element.48, f32[16]{0:T(128)S(1)} %get-tuple-element.46, f32[128,148]{1,0:T(8,128)S(1)} %get-tuple-element.49, f32[16]{0:T(128)S(1)} %get-tuple-element.45, f32[128,148]{1,0:T(8,128)S(1)} %get-tuple-element.50, f32[16]{0:T(128)S(1)} %get-tuple-element.27, ...), kind=kLoop, calls=%fused_computation.2 | loop fusion | flops 12427264 | bytes 2805056 | tf_op jit(solution)/shard_map/add | solution.py:40
  36.1 0.0 all-to-all-done
  36.1 11.0 %fusion = f32[16,128,128]{2,0,1:T(8,128)S(1)} fusion(f32[6,128,128]{2,0,1:T(8,128)S(1)} %stack.20, f32[16,128,148]{2,0,1:T(8,128)S(1)} %multiply_add_fusion, f32[16]{0:T(128)S(1)} %get-tuple-element.25, f32[16]{0:T(128)S(1)} %get-tuple-element.24, f32[16]{0:T(128)S(1)} %get-tuple-element.6, f32[16]{0:T(128)S(1)} %get-tuple-element.7, ...), kind=kOutput, calls=%fused_computation.1 | convolution fusion | flops 315621376 | bytes 23669248 | tf_op jit(solution)/shard_map/vkt,krc->vtrc/dot_general | solution.py:50
  47.1 0.0 copy-start.1
  47.1 1.3 %copy.13 = f32[16,128,128]{2,1,0:T(8,128)} copy(f32[16,128,128]{2,0,1:T(8,128)S(1)} %fusion) | data formatting | bytes 2097152 | tf_op jit(solution)/shard_map/reduce_sum | solution.py:51
  48.4 16.6 %all-to-all-start.1 = ((f32[16,128,128]{2,1,0:T(8,128)}), f32[16,128,128]{2,1,0:T(8,128)S(1)}, u32[]{:S(2)}, u32[]{:S(2)}) async-start(f32[16,128,128]{2,1,0:T(8,128)} %copy.13), calls=%async_computation.1 | async-start | bytes 2097152 | tf_op jit(solution)/shard_map/all_to_all | solution.py:66
  65.0 0.0 copy-done.1
  65.0 0.3 copy.15
  65.4 0.0 copy-done
  65.4 0.1 constant_dynamic-slice_fusion
  65.5 0.6 fusion.73
  67.3 0.6 fusion.66
  67.9 28.7 %all-to-all-done.1 = f32[16,128,128]{2,1,0:T(8,128)S(1)} async-done(((f32[16,128,128]{2,1,0:T(8,128)}), f32[16,128,128]{2,1,0:T(8,128)S(1)}, u32[]{:S(2)}, u32[]{:S(2)}) %all-to-all-start.1) | async-done | bytes 1048608 | tf_op jit(solution)/shard_map/all_to_all | solution.py:66
  96.6 0.3 copy.14
  97.0 0.4 fusion.42
  97.4 1.3 %copy.16 = f32[1,128,2048]{2,1,0:T(8,128)} copy(f32[1,128,2048]{1,2,0:T(8,128)S(1)} %fusion.42) | data formatting | bytes 2097152 | tf_op jit(solution)/shard_map/jit(_where)/select_n | solution.py:74
  (6 shorter events, 0.1 us)
Async XLA Ops:
  0.0 65.4 %copy-start = (s32[16,2]{0,1:T(2,128)S(1)}, s32[16,2]{0,1:T(2,128)}, u32[]{:S(2)}) copy-start(s32[16,2]{0,1:T(2,128)} %param.11) | copy-start | bytes 388
  0.0 32.8 %copy-start.2 = (f32[128,128]{1,0:T(8,128)S(1)}, f32[128,128]{1,0:T(8,128)}, u32[]{:S(2)}) copy-start(f32[128,128]{1,0:T(8,128)} %param.6) | copy-start | bytes 196612
  0.8 24.5 %collective-permute-start = (f32[10,128]{1,0:T(8,128)S(1)}, f32[10,128]{1,0:T(8,128)S(1)}, u32[]{:S(2)}, u32[]{:S(2)}) collective-permute-start(f32[10,128]{1,0:T(8,128)S(1)} %get-tuple-element.70), channel_id=1, source_target_pairs={{0,16},{16,32},{32,48},{48,64},{64,80},{80,96},{96,112},{112,128},... | collective-permute-start | bytes 15368 | tf_op jit(solution)/shard_map/ppermute | solution.py:15
  4.3 21.0 %collective-permute-start.1 = (f32[10,128]{1,0:T(8,128)S(1)}, f32[10,128]{1,0:T(8,128)S(1)}, u32[]{:S(2)}, u32[]{:S(2)}) collective-permute-start(f32[10,128]{1,0:T(8,128)S(1)} %get-tuple-element.71), channel_id=1, source_target_pairs={{16,0},{32,16},{48,32},{64,48},{80,64},{96,80},{112,96},{128,112},... | collective-permute-start | bytes 15368 | tf_op jit(solution)/shard_map/ppermute | solution.py:17
  10.1 26.0 %all-to-all-start = ((f32[16,16,6]{1,2,0:T(8,128)}), f32[16,16,6]{1,2,0:T(8,128)S(1)}, u32[]{:S(2)}, u32[]{:S(2)}) async-start(f32[16,16,6]{1,2,0:T(8,128)} %broadcast_in_dim.14), calls=%async_computation | async-start | bytes 131072 | tf_op jit(solution)/shard_map/all_to_all | solution.py:62
  26.2 5.8 %collective-permute-start.2 = (f32[148,10]{1,0:T(8,128)S(1)}, f32[148,10]{1,0:T(8,128)S(1)}, u32[]{:S(2)}, u32[]{:S(2)}) collective-permute-start(f32[148,10]{1,0:T(8,128)S(1)} %get-tuple-element.68), channel_id=1, source_target_pairs={{0,1},{1,2},{2,3},{3,4},{4,5},{5,6},{6,7},{7,8},{8,9},{9,10},{10,1... | collective-permute-start | bytes 17768 | tf_op jit(solution)/shard_map/ppermute | solution.py:15
  28.5 4.3 %collective-permute-start.3 = (f32[148,10]{1,0:T(8,128)S(1)}, f32[148,10]{1,0:T(8,128)S(1)}, u32[]{:S(2)}, u32[]{:S(2)}) collective-permute-start(f32[148,10]{1,0:T(8,128)S(1)} %get-tuple-element.69), channel_id=1, source_target_pairs={{1,0},{2,1},{3,2},{4,3},{5,4},{6,5},{7,6},{8,7},{9,8},{10,9},{11,1... | collective-permute-start | bytes 17768 | tf_op jit(solution)/shard_map/ppermute | solution.py:17
  47.1 17.9 %copy-start.1 = (f32[1,128,2048]{2,1,0:T(8,128)S(1)}, f32[1,128,2048]{2,1,0:T(8,128)}, u32[]{:S(2)}) copy-start(f32[1,128,2048]{2,1,0:T(8,128)} %param.10) | copy-start | bytes 3145732
  48.4 48.2 %all-to-all-start.1 = ((f32[16,128,128]{2,1,0:T(8,128)}), f32[16,128,128]{2,1,0:T(8,128)S(1)}, u32[]{:S(2)}, u32[]{:S(2)}) async-start(f32[16,128,128]{2,1,0:T(8,128)} %copy.13), calls=%async_computation.1 | async-start | bytes 2097152 | tf_op jit(solution)/shard_map/all_to_all | solution.py:66

commit v3 on v1

v3 whole, which is shorter than its diff:
```python
import jax
import jax.numpy as jnp
from jax import lax
from jax.sharding import Mesh
from jax.sharding import PartitionSpec as P


def coordinate(first, count, total):
    return 2.0 * ((first + jnp.arange(count)).astype(jnp.float32) + 0.5) / total - 1.0


def surface_terms(y_coord, x_coord):
    y_grid = y_coord[:, None] * jnp.ones_like(x_coord)[None, :]
    x_grid = jnp.ones_like(y_coord)[:, None] * x_coord[None, :]
    return jnp.stack(
        [jnp.ones_like(x_grid), x_grid, y_grid, x_grid * x_grid, x_grid * y_grid, y_grid * y_grid]
    )


def separable(padded, row_taps, col_taps, tile_rows, span):
    passed = jnp.zeros((row_taps.shape[0], tile_rows, padded.shape[1]), jnp.float32)
    for offset in range(row_taps.shape[1]):
        passed = (
            passed + row_taps[:, offset, None, None] * padded[None, offset : offset + tile_rows, :]
        )
    images = jnp.zeros((row_taps.shape[0], tile_rows, span), jnp.float32)
    for offset in range(col_taps.shape[1]):
        images = images + col_taps[:, offset, None, None] * passed[:, :, offset : offset + span]
    return images


def local(template, row_taps, col_taps, coeffs, visits, boxes):
    half = row_taps.shape[1] // 2
    tile_rows, columns = template.shape
    tiles = lax.axis_size("tile")
    halves = lax.axis_size("zhi")
    group = lax.axis_size("xc")
    tile = lax.axis_index("tile")
    side = lax.axis_index("zhi")
    place = lax.axis_index("xc")
    full_width = columns * halves * group
    total_rows = tile_rows * tiles

    copies = jnp.broadcast_to(coeffs, (group,) + coeffs.shape[1:])
    half_coeffs = lax.all_to_all(copies, "xc", 0, 0, tiled=True)

    top = template[:half]
    bottom = template[tile_rows - half :]
    swap = [(h, halves - 1 - h) for h in range(halves)]
    partner = lax.ppermute(template, "zhi", swap)
    down = [(i, i + 1) for i in range(tiles - 1)]
    up = [(i + 1, i) for i in range(tiles - 1)]
    above = lax.ppermute(bottom, "tile", down)
    below = lax.ppermute(top, "tile", up)

    def crossed(pairs):
        return [(i * halves + h, j * halves + halves - 1 - h) for i, j in pairs for h in range(halves)]

    partner_above = lax.ppermute(bottom, ("tile", "zhi"), crossed(down))
    partner_below = lax.ppermute(top, ("tile", "zhi"), crossed(up))
    own = jnp.concatenate([above, template, below], axis=0)
    other = jnp.concatenate([partner_above, partner, partner_below], axis=0)
    first = side == 0
    blocks = jnp.stack([jnp.where(first, own, other), jnp.where(first, other, own)])
    blocks = jnp.pad(blocks, ((0, 0), (0, 0), (2 * half, 2 * half)))
    span = columns + 2 * half
    y_coord = coordinate(tile * tile_rows, tile_rows, total_rows)
    models = []
    for b in range(halves):
        basis = separable(blocks[b], row_taps, col_taps, tile_rows, span)
        start = (b * group + place) * columns - half
        terms = surface_terms(y_coord, coordinate(start, span, full_width))
        weighted = jnp.einsum("vkt,krc->vtrc", half_coeffs, basis, precision=lax.Precision.HIGHEST)
        models.append(jnp.sum(weighted * terms[None], axis=1))
    models = jnp.stack(models, axis=1)
    parts = lax.all_to_all(models, "xc", 0, 0, tiled=True)
    parts = jnp.swapaxes(parts, 0, 1).reshape((halves * group,) + parts.shape[2:])
    core = parts[:, :, half : half + columns]
    left = parts[:, :, :half]
    right = parts[:, :, half + columns :]
    edge = jnp.zeros_like(left[:1])
    core = core.at[:, :, :half].add(jnp.concatenate([edge, right[:-1]], axis=0))
    core = core.at[:, :, columns - half :].add(jnp.concatenate([left[1:], edge], axis=0))
    model = jnp.swapaxes(core, 0, 1).reshape(1, tile_rows, full_width)

    visit = side * group + place
    local_boxes = lax.dynamic_slice_in_dim(boxes, visit, 1, 0)
    column_index = jnp.arange(full_width)
    inside = (column_index[None, :] >= local_boxes[:, 0:1]) & (
        column_index[None, :] < local_boxes[:, 0:1] + local_boxes[:, 1:2]
    )
    return jnp.where(inside[:, None, :], visits - model, jnp.float32(0.0))


def solution(mesh):
    tiles, visits = mesh.devices.shape
    split = Mesh(mesh.devices.reshape(tiles, 2, visits // 2), ("tile", "zhi", "xc"))
    cols = ("zhi", "xc")
    placed = (P("tile", cols), P(), P(), P(cols, None, None), P(cols, "tile", None), P())
    return jax.shard_map(
        local, mesh=split, in_specs=placed, out_specs=P(cols, "tile", None), check_vma=False
    )
```

time: 112 us -> 142 us (1.27)
  local copies, waits for them, and re-layouts: 12.6 us -> 69.4 us
  blocking collectives: 35.4 us -> 0 us
  starting transfers between devices: 17.2 us -> 33.3 us
  waiting for transfers between devices: 28.7 us -> 14.9 us
  matrix products: 11 us -> 13.4 us
  other arithmetic: 5.05 us -> 7.42 us
    mul x0 -> x45, local copies, waits for them, and re-layouts: none -> 48.8 us  [separable(): row_taps[:, offset, None, None] * padded[None, offset:offset + tile_rows, :]]
    all_gather x1 -> x0, blocking collectives: 35.4 us -> none  [local(): all_coeffs = lax.all_gather(coeffs, 'visit', axis=0, tiled=True)]
    all_to_all x1 -> x2, waiting for transfers between devices: 28.7 us -> 14.8 us  [the longest x1 14.8 us: local(): parts = lax.all_to_all(models, 'xc', 0, 0, tiled=True)]
    ppermute x4 -> x5, starting transfers between devices: 10.5 us -> 24.1 us  [the longest x1 9.21 us: local(): partner_above = lax.ppermute(bottom, ('tile', 'zhi'), crossed(down))]
    another operation x6 -> x8, local copies, waits for them, and re-layouts: 1.13 us -> 5.4 us  [surface_terms(): jnp.stack([jnp.ones_like(x_grid), x_grid, y_grid, x_grid * x_grid, x_grid...]
    add x1 -> x2, other arithmetic: 2.88 us -> 5.71 us  [separable(): passed + row_taps[:, offset, None, None] * padded[None, offset:offset + t...]
    all_to_all x1 -> x2, starting transfers between devices: 6.67 us -> 9.23 us  [the longest x1 4.93 us: local(): parts = lax.all_to_all(models, 'xc', 0, 0, tiled=True)]
    dot_general x1 -> x2, matrix products: 11 us -> 13.4 us  [local(): jnp.einsum('vkt,krc->vtrc', half_coeffs, basis, precision=lax.Precision.H...]
  transfers between devices with their start and end apart: 5 -> 7, of which waited for: 1 -> 1; matrix products, arithmetic and copies ran while one was open for 8% -> 51% of each run, Pallas kernels for 0% -> 0%
where the time goes in v3:
time: 142 us; the launch traced here: 141 us
  local copies, waits for them, and re-layouts  69.4 us (49%)
  starting transfers between devices  33.3 us (23%)
  waiting for transfers between devices  14.9 us (10%)
  matrix products  13.4 us (9%)
  other arithmetic  7.42 us (5%)
  between operations  2.47 us (2%)
    mul x45, local copies, waits for them, and re-layouts, separable(): row_taps[:, offset, None, None] * padded[None, offset:offset + tile_rows, :]  48.8 us
    all_to_all x1, waiting for transfers between devices, local(): parts = lax.all_to_all(models, 'xc', 0, 0, tiled=True)  14.8 us
    dot_general x2, matrix products, local(): jnp.einsum('vkt,krc->vtrc', half_coeffs, basis, precision=lax.Precision.H...  13.4 us
    ppermute x1, starting transfers between devices, local(): partner_above = lax.ppermute(bottom, ('tile', 'zhi'), crossed(down))  9.21 us
    ppermute x1, starting transfers between devices, local(): partner = lax.ppermute(template, 'zhi', swap)  5.89 us
    add x2, other arithmetic, separable(): passed + row_taps[:, offset, None, None] * padded[None, offset:offset + t...  5.71 us
    another operation x8, local copies, waits for them, and re-layouts, surface_terms(): jnp.stack([jnp.ones_like(x_grid), x_grid, y_grid, x_grid * x_grid, x_grid...  5.4 us
    all_to_all x1, starting transfers between devices, local(): parts = lax.all_to_all(models, 'xc', 0, 0, tiled=True)  4.93 us
  transfers between devices with their start and end apart: 7, of which 1 were waited for; matrix products, arithmetic and copies ran while one was open for 51% of the time, Pallas kernels for 0%

profile of v3, /device:TPU:32, one launch (start us, length us, event | category | flops | bytes accessed | tf_op | source)
XLA Modules:
  0.0 140.8 jit_solution(49157283445642022)
XLA Ops:
  0.0 0.7 fusion.141
  0.7 3.5 %collective-permute-start = (f32[10,128]{1,0:T(8,128)S(1)}, f32[10,128]{1,0:T(8,128)S(1)}, u32[]{:S(2)}, u32[]{:S(2)}) collective-permute-start(f32[10,128]{1,0:T(8,128)S(1)} %get-tuple-element.117), channel_id=1, source_target_pairs={{0,16},{16,32},{32,48},{48,64},{64,80},{80,96},{96,112},{112,128},... | collective-permute-start | bytes 15368 | tf_op jit(solution)/shard_map/ppermute | solution.py:53
  4.2 9.2 %collective-permute-start.2 = (f32[10,128]{1,0:T(8,128)S(1)}, f32[10,128]{1,0:T(8,128)S(1)}, u32[]{:S(2)}, u32[]{:S(2)}) collective-permute-start(f32[10,128]{1,0:T(8,128)S(1)} %get-tuple-element.117), channel_id=1, source_target_pairs={{0,24},{8,16},{16,40},{24,32},{32,56},{40,48},{48,72},{56,64},{64,... | collective-permute-start | bytes 15368 | tf_op jit(solution)/shard_map/ppermute | solution.py:59
  13.4 3.6 %collective-permute-start.1 = (f32[10,128]{1,0:T(8,128)S(1)}, f32[10,128]{1,0:T(8,128)S(1)}, u32[]{:S(2)}, u32[]{:S(2)}) collective-permute-start(f32[10,128]{1,0:T(8,128)S(1)} %get-tuple-element.118), channel_id=1, source_target_pairs={{16,0},{32,16},{48,32},{64,48},{80,64},{96,80},{112,96},{128,112},... | collective-permute-start | bytes 15368 | tf_op jit(solution)/shard_map/ppermute | solution.py:54
  17.0 1.9 %collective-permute-start.4 = (f32[10,128]{1,0:T(8,128)S(1)}, f32[10,128]{1,0:T(8,128)S(1)}, u32[]{:S(2)}, u32[]{:S(2)}) collective-permute-start(f32[10,128]{1,0:T(8,128)S(1)} %get-tuple-element.118), channel_id=1, source_target_pairs={{16,8},{24,0},{32,24},{40,16},{48,40},{56,32},{64,56},{72,48},{80,... | collective-permute-start | bytes 15368 | tf_op jit(solution)/shard_map/ppermute | solution.py:60
  18.9 5.9 %collective-permute-start.3 = (f32[128,128]{1,0:T(8,128)}, f32[128,128]{1,0:T(8,128)S(1)}, u32[]{:S(2)}, u32[]{:S(2)}) collective-permute-start(f32[128,128]{1,0:T(8,128)} %param.10), channel_id=1, source_target_pairs={{0,8},{8,0},{1,9},{9,1},{2,10},{10,2},{3,11},{11,3},{4,12},{12,4},... | collective-permute-start | bytes 196616 | tf_op jit(solution)/shard_map/ppermute | solution.py:50
  26.1 4.3 %all-to-all-start = ((f32[8,16,6]{1,2,0:T(8,128)}), f32[8,16,6]{1,2,0:T(8,128)}, u32[]{:S(2)}, u32[]{:S(2)}) async-start(f32[8,16,6]{1,2,0:T(8,128)} %broadcast_in_dim.14), calls=%async_computation | async-start | bytes 65536 | tf_op jit(solution)/shard_map/all_to_all | solution.py:45
  30.4 2.5 %slice_reduce_fusion.40 = (f32[16]{0:T(128)S(1)}, f32[16]{0:T(128)S(1)}, f32[16]{0:T(128)S(1)}, f32[16]{0:T(128)S(1)}, f32[16]{0:T(128)S(1)}, /*index=5*/f32[16]...) fusion(f32[16,21]{1,0:T(8,128)} %param.11), kind=kLoop, calls=%fused_computation.236 | loop fusion | bytes 2432 | tf_op jit(solution)/shard_map/slice | solution.py:24
  32.9 1.6 %slice_reduce_fusion.21 = (f32[16]{0:T(128)}, f32[16]{0:T(128)}) fusion(f32[16,21]{1,0:T(8,128)} %param.11), kind=kLoop, calls=%fused_computation.217 | loop fusion | bytes 256 | tf_op jit(solution)/shard_map/slice | solution.py:24
  34.5 2.5 %slice_reduce_fusion.41 = (f32[16]{0:T(128)}, f32[16]{0:T(128)}, f32[16]{0:T(128)}, f32[16]{0:T(128)}, f32[16]{0:T(128)}, /*index=5*/f32[16]{0:T(128)}, f32[16]{...) fusion(f32[16,21]{1,0:T(8,128)} %param.12), kind=kLoop, calls=%fused_computation.237 | loop fusion | bytes 2432 | tf_op jit(solution)/shard_map/slice | solution.py:28
  37.4 1.5 %slice_reduce_fusion.1 = (f32[16]{0:T(128)}, f32[16]{0:T(128)}) fusion(f32[16,21]{1,0:T(8,128)} %param.12), kind=kLoop, calls=%fused_computation.197 | loop fusion | bytes 256 | tf_op jit(solution)/shard_map/slice | solution.py:28
  39.5 2.5 %stack.47 = f32[6,128,148]{1,0,2:T(8,128)} concatenate(f32[1,128,148]{1,0,2:T(1,128)S(1)} %broadcast.231, f32[1,128,148]{1,0,2:T(1,128)S(1)} %stack.43, f32[1,128,148]{1,0,2:T(1,128)S(1)} %stack.44, f32[1,128,148]{1,0,2:T(1,128)S(1)} %stack.45, f32[1,128,148]{1,0,2:T(1,128)S(1)} %get-tuple-element.121, f32[1,128,148]{1,0,2:T(1,128)S(1)} %stack.46), dimensions={0} | concatenate | bytes 909312 | tf_op jit(solution)/shard_map/stack | solution.py:15
  42.4 2.0 %stack.51 = f32[6,128,148]{1,0,2:T(8,128)S(1)} concatenate(f32[1,128,148]{1,0,2:T(1,128)S(1)} %broadcast.231, f32[1,128,148]{1,0,2:T(1,128)S(1)} %stack.49, f32[1,128,148]{1,0,2:T(1,128)S(1)} %stack.44, f32[1,128,148]{1,0,2:T(1,128)S(1)} %stack.50, f32[1,128,148]{1,0,2:T(1,128)S(1)} %get-tuple-element.122, f32[1,128,148]{1,0,2:T(1,128)S(1)} %stack.46), dimensions={0} | concatenate | bytes 909312 | tf_op jit(solution)/shard_map/stack | solution.py:15
  44.8 1.4 slice_bitcast_fusion.40
  46.2 0.8 slice_bitcast_fusion.39
  47.0 0.7 copy.182
  47.8 1.6 %copy.183 = f32[128,168]{0,1:T(8,128)} copy(f32[128,168]{1,0:T(8,128)} %get-tuple-element.92) | data formatting | bytes 172032 | tf_op jit(solution)/shard_map/mul | solution.py:24
  49.4 1.6 %copy.187 = f32[128,168]{0,1:T(8,128)} copy(f32[128,168]{1,0:T(8,128)} %get-tuple-element.110) | data formatting | bytes 172032 | tf_op jit(solution)/shard_map/mul | solution.py:24
  51.0 1.7 %copy.188 = f32[128,168]{0,1:T(8,128)} copy(f32[128,168]{1,0:T(8,128)} %get-tuple-element.109) | data formatting | bytes 172032 | tf_op jit(solution)/shard_map/mul | solution.py:24
  52.7 1.6 %copy.189 = f32[128,168]{0,1:T(8,128)} copy(f32[128,168]{1,0:T(8,128)} %get-tuple-element.108) | data formatting | bytes 172032 | tf_op jit(solution)/shard_map/mul | solution.py:24
  54.3 1.6 %copy.190 = f32[128,168]{0,1:T(8,128)} copy(f32[128,168]{1,0:T(8,128)} %get-tuple-element.107) | data formatting | bytes 172032 | tf_op jit(solution)/shard_map/mul | solution.py:24
  56.0 1.6 %copy.191 = f32[128,168]{0,1:T(8,128)} copy(f32[128,168]{1,0:T(8,128)} %get-tuple-element.106) | data formatting | bytes 172032 | tf_op jit(solution)/shard_map/mul | solution.py:24
  57.6 1.6 %copy.192 = f32[128,168]{0,1:T(8,128)} copy(f32[128,168]{1,0:T(8,128)} %get-tuple-element.105) | data formatting | bytes 172032 | tf_op jit(solution)/shard_map/mul | solution.py:24
  59.2 1.6 %copy.193 = f32[128,168]{0,1:T(8,128)} copy(f32[128,168]{1,0:T(8,128)} %get-tuple-element.104) | data formatting | bytes 172032 | tf_op jit(solution)/shard_map/mul | solution.py:24
  60.9 1.6 %copy.194 = f32[128,168]{0,1:T(8,128)} copy(f32[128,168]{1,0:T(8,128)} %get-tuple-element.103) | data formatting | bytes 172032 | tf_op jit(solution)/shard_map/mul | solution.py:24
  62.5 1.6 %copy.195 = f32[128,168]{0,1:T(8,128)} copy(f32[128,168]{1,0:T(8,128)} %get-tuple-element.102) | data formatting | bytes 172032 | tf_op jit(solution)/shard_map/mul | solution.py:24
  64.2 1.6 %copy.196 = f32[128,168]{0,1:T(8,128)} copy(f32[128,168]{1,0:T(8,128)} %get-tuple-element.101) | data formatting | bytes 172032 | tf_op jit(solution)/shard_map/mul | solution.py:24
  65.8 1.6 %copy.197 = f32[128,168]{0,1:T(8,128)} copy(f32[128,168]{1,0:T(8,128)} %get-tuple-element.100) | data formatting | bytes 172032 | tf_op jit(solution)/shard_map/mul | solution.py:24
  67.4 1.7 %copy.198 = f32[128,168]{0,1:T(8,128)} copy(f32[128,168]{1,0:T(8,128)} %get-tuple-element.99) | data formatting | bytes 172032 | tf_op jit(solution)/shard_map/mul | solution.py:24
  69.1 1.6 %copy.199 = f32[128,168]{0,1:T(8,128)} copy(f32[128,168]{1,0:T(8,128)} %get-tuple-element.98) | data formatting | bytes 172032 | tf_op jit(solution)/shard_map/mul | solution.py:24
  70.7 1.6 %copy.200 = f32[128,168]{0,1:T(8,128)} copy(f32[128,168]{1,0:T(8,128)} %get-tuple-element.97) | data formatting | bytes 172032 | tf_op jit(solution)/shard_map/mul | solution.py:24
  72.4 0.7 copy.201
  73.1 0.7 copy.202
  73.8 1.6 %copy.184 = f32[128,168]{0,1:T(8,128)} copy(f32[128,168]{1,0:T(8,128)} %get-tuple-element.111) | data formatting | bytes 172032 | tf_op jit(solution)/shard_map/mul | solution.py:24
  75.4 1.6 %copy.185 = f32[128,168]{0,1:T(8,128)} copy(f32[128,168]{1,0:T(8,128)} %get-tuple-element.113) | data formatting | bytes 172032 | tf_op jit(solution)/shard_map/mul | solution.py:24
  77.1 1.6 %copy.186 = f32[128,168]{0,1:T(8,128)} copy(f32[128,168]{1,0:T(8,128)} %get-tuple-element.112) | data formatting | bytes 172032 | tf_op jit(solution)/shard_map/mul | solution.py:24
  78.8 0.7 copy.205
  79.6 0.7 copy.206
  80.3 0.7 copy.207
  81.0 0.7 copy.208
  81.8 0.7 copy.209
  82.5 0.7 copy.210
  83.2 0.7 copy.211
  84.0 0.7 copy.212
  84.7 0.7 copy.213
  85.4 0.7 copy.214
  86.1 0.7 copy.215
  86.9 0.7 copy.216
  87.6 0.8 copy.217
  88.4 0.7 copy.218
  89.1 0.7 copy.219
  89.8 0.7 copy.220
  90.6 0.7 copy.221
  91.3 0.7 copy.222
  92.0 0.7 copy.223
  92.8 0.7 copy.224
  93.8 3.8 %multiply_add_fusion.1 = f32[16,128,168]{1,0,2:T(8,128)S(1)} fusion(f32[128,168]{0,1:T(8,128)} %copy.202, f32[16]{0:T(128)} %get-tuple-element.70, f32[128,168]{0,1:T(8,128)} %copy.201, f32[16]{0:T(128)} %get-tuple-element.69, f32[128,168]{0,1:T(8,128)} %copy.200, f32[16]{0:T(128)S(1)} %get-tuple-element.51, f32[128,168]{0,1:T(8,128)} %copy.199, ...), kind=kLoop, calls=%fused_computation.5 | loop fusion | flops 14106624 | bytes 3183936 | tf_op jit(solution)/shard_map/add | solution.py:24
  98.0 1.9 %multiply_add_fusion = f32[16,128,168]{1,0,2:T(8,128)S(1)} fusion(f32[128,168]{0,1:T(8,128)S(1)} %copy-done.24, f32[128,168]{0,1:T(8,128)S(1)} %copy-done.23, f32[128,168]{0,1:T(8,128)S(1)} %copy-done.22, f32[128,168]{0,1:T(8,128)S(1)} %copy-done.21, f32[128,168]{0,1:T(8,128)S(1)} %copy-done.20, f32[128,168]{0,1:T(8,128)S(1)} %copy-done.19, ...), kind=kLoop, calls=%fused_computation.4 | loop fusion | flops 14106624 | bytes 3183936 | tf_op jit(solution)/shard_map/add | solution.py:24
  100.2 6.9 %fusion.1 = f32[8,128,148]{1,0,2:T(8,128)S(1)} fusion(f32[6,128,148]{1,0,2:T(8,128)} %stack.47, f32[16,128,168]{1,0,2:T(8,128)S(1)} %multiply_add_fusion.1, f32[16]{0:T(128)} %get-tuple-element.49, f32[16]{0:T(128)} %get-tuple-element.48, f32[16]{0:T(128)S(1)} %copy-done.43, f32[16]{0:T(128)} %get-tuple-element.31, f32[16]{0:T(128)} %get-tuple-element.32, ...), kind=kOutput, calls=%fused_computation.3 | convolution fusion | flops 188682240 | bytes 26526912 | tf_op jit(solution)/shard_map/vkt,krc->vtrc/dot_general | solution.py:73
  107.2 6.5 %fusion = f32[8,128,148]{1,0,2:T(8,128)S(1)} fusion(f32[6,128,148]{1,0,2:T(8,128)S(1)} %stack.51, f32[16,128,168]{1,0,2:T(8,128)S(1)} %multiply_add_fusion, f32[16]{0:T(128)S(1)} %copy-done.62, f32[16]{0:T(128)S(1)} %copy-done.61, f32[16]{0:T(128)S(1)} %copy-done.43, f32[16]{0:T(128)S(1)} %copy-done.44, f32[16]{0:T(128)S(1)} %copy-done.45, ...), kind=kOutput, calls=%fused_computation.1 | convolution fusion | flops 188682240 | bytes 26686976 | tf_op jit(solution)/shard_map/vkt,krc->vtrc/dot_general | solution.py:73
  113.9 2.0 %copy.226 = f32[8,2,128,148]{2,1,3,0:T(2,128)} copy(f32[8,2,128,148]{2,0,3,1:T(8,128)S(1)} %pad_maximum_fusion) | data formatting | bytes 2424832 | tf_op jit(solution)/shard_map/stack | solution.py:75
  115.8 4.9 %all-to-all-start.1 = ((f32[8,2,128,148]{2,1,3,0:T(2,128)}), f32[8,2,128,148]{2,1,3,0:T(2,128)S(1)}, u32[]{:S(2)}, u32[]{:S(2)}) async-start(f32[8,2,128,148]{2,1,3,0:T(2,128)} %copy.226), calls=%async_computation.1 | async-start | bytes 2424832 | tf_op jit(solution)/shard_map/all_to_all | solution.py:76
  123.6 14.8 %all-to-all-done.1 = f32[8,2,128,148]{2,1,3,0:T(2,128)S(1)} async-done(((f32[8,2,128,148]{2,1,3,0:T(2,128)}), f32[8,2,128,148]{2,1,3,0:T(2,128)S(1)}, u32[]{:S(2)}, u32[]{:S(2)}) %all-to-all-start.1) | async-done | bytes 1212448 | tf_op jit(solution)/shard_map/all_to_all | solution.py:76
  139.5 1.3 copy.230
  (161 shorter events, 6.2 us)
Async XLA Ops:
  0.0 121.1 %copy-start = (s32[16,2]{0,1:T(2,128)S(1)}, s32[16,2]{0,1:T(2,128)}, u32[]{:S(2)}) copy-start(s32[16,2]{0,1:T(2,128)} %param.15) | copy-start | bytes 388
  0.7 43.7 %collective-permute-start = (f32[10,128]{1,0:T(8,128)S(1)}, f32[10,128]{1,0:T(8,128)S(1)}, u32[]{:S(2)}, u32[]{:S(2)}) collective-permute-start(f32[10,128]{1,0:T(8,128)S(1)} %get-tuple-element.117), channel_id=1, source_target_pairs={{0,16},{16,32},{32,48},{48,64},{64,80},{80,96},{96,112},{112,128},... | collective-permute-start | bytes 15368 | tf_op jit(solution)/shard_map/ppermute | solution.py:53
  4.2 40.2 %collective-permute-start.2 = (f32[10,128]{1,0:T(8,128)S(1)}, f32[10,128]{1,0:T(8,128)S(1)}, u32[]{:S(2)}, u32[]{:S(2)}) collective-permute-start(f32[10,128]{1,0:T(8,128)S(1)} %get-tuple-element.117), channel_id=1, source_target_pairs={{0,24},{8,16},{16,40},{24,32},{32,56},{40,48},{48,72},{56,64},{64,... | collective-permute-start | bytes 15368 | tf_op jit(solution)/shard_map/ppermute | solution.py:59
  13.4 31.0 %collective-permute-start.1 = (f32[10,128]{1,0:T(8,128)S(1)}, f32[10,128]{1,0:T(8,128)S(1)}, u32[]{:S(2)}, u32[]{:S(2)}) collective-permute-start(f32[10,128]{1,0:T(8,128)S(1)} %get-tuple-element.118), channel_id=1, source_target_pairs={{16,0},{32,16},{48,32},{64,48},{80,64},{96,80},{112,96},{128,112},... | collective-permute-start | bytes 15368 | tf_op jit(solution)/shard_map/ppermute | solution.py:54
  17.0 27.4 %collective-permute-start.4 = (f32[10,128]{1,0:T(8,128)S(1)}, f32[10,128]{1,0:T(8,128)S(1)}, u32[]{:S(2)}, u32[]{:S(2)}) collective-permute-start(f32[10,128]{1,0:T(8,128)S(1)} %get-tuple-element.118), channel_id=1, source_target_pairs={{16,8},{24,0},{32,24},{40,16},{48,40},{56,32},{64,56},{72,48},{80,... | collective-permute-start | bytes 15368 | tf_op jit(solution)/shard_map/ppermute | solution.py:60
  18.9 25.5 %collective-permute-start.3 = (f32[128,128]{1,0:T(8,128)}, f32[128,128]{1,0:T(8,128)S(1)}, u32[]{:S(2)}, u32[]{:S(2)}) collective-permute-start(f32[128,128]{1,0:T(8,128)} %param.10), channel_id=1, source_target_pairs={{0,8},{8,0},{1,9},{9,1},{2,10},{10,2},{3,11},{11,3},{4,12},{12,4},... | collective-permute-start | bytes 196616 | tf_op jit(solution)/shard_map/ppermute | solution.py:50
  26.1 73.8 %all-to-all-start = ((f32[8,16,6]{1,2,0:T(8,128)}), f32[8,16,6]{1,2,0:T(8,128)}, u32[]{:S(2)}, u32[]{:S(2)}) async-start(f32[8,16,6]{1,2,0:T(8,128)} %broadcast_in_dim.14), calls=%async_computation | async-start | bytes 65536 | tf_op jit(solution)/shard_map/all_to_all | solution.py:45
  37.4 7.1 %copy-start.25 = (f32[128,128]{1,0:T(8,128)S(1)}, f32[128,128]{1,0:T(8,128)}, u32[]{:S(2)}) copy-start(f32[128,128]{1,0:T(8,128)} %param.10) | copy-start | bytes 196612
  51.0 21.3 %copy-start.2 = (f32[128,168]{1,0:T(8,128)S(1)}, f32[128,168]{1,0:T(8,128)}, u32[]{:S(2)}) copy-start(f32[128,168]{1,0:T(8,128)} %get-tuple-element.96) | copy-start | bytes 258052
  83.2 9.5 %copy-start.3 = (f32[128,168]{1,0:T(8,128)S(1)}, f32[128,168]{1,0:T(8,128)}, u32[]{:S(2)}) copy-start(f32[128,168]{1,0:T(8,128)} %get-tuple-element.114) | copy-start | bytes 258052
  84.7 8.8 %copy-start.4 = (f32[128,168]{0,1:T(8,128)S(1)}, f32[128,168]{0,1:T(8,128)}, u32[]{:S(2)}) copy-start(f32[128,168]{0,1:T(8,128)} %copy.182) | copy-start | bytes 258052
  93.5 4.2 %copy-start.8 = (f32[128,168]{0,1:T(8,128)S(1)}, f32[128,168]{0,1:T(8,128)}, u32[]{:S(2)}) copy-start(f32[128,168]{0,1:T(8,128)} %copy.208) | copy-start | bytes 258052
  93.5 4.2 %copy-start.9 = (f32[128,168]{0,1:T(8,128)S(1)}, f32[128,168]{0,1:T(8,128)}, u32[]{:S(2)}) copy-start(f32[128,168]{0,1:T(8,128)} %copy.209) | copy-start | bytes 258052
  93.5 4.2 %copy-start.10 = (f32[128,168]{0,1:T(8,128)S(1)}, f32[128,168]{0,1:T(8,128)}, u32[]{:S(2)}) copy-start(f32[128,168]{0,1:T(8,128)} %copy.210) | copy-start | bytes 258052
  93.5 4.2 %copy-start.11 = (f32[128,168]{0,1:T(8,128)S(1)}, f32[128,168]{0,1:T(8,128)}, u32[]{:S(2)}) copy-start(f32[128,168]{0,1:T(8,128)} %copy.211) | copy-start | bytes 258052
  93.5 4.2 %copy-start.12 = (f32[128,168]{0,1:T(8,128)S(1)}, f32[128,168]{0,1:T(8,128)}, u32[]{:S(2)}) copy-start(f32[128,168]{0,1:T(8,128)} %copy.212) | copy-start | bytes 258052
  93.5 4.2 %copy-start.13 = (f32[128,168]{0,1:T(8,128)S(1)}, f32[128,168]{0,1:T(8,128)}, u32[]{:S(2)}) copy-start(f32[128,168]{0,1:T(8,128)} %copy.213) | copy-start | bytes 258052
  93.6 4.2 %copy-start.14 = (f32[128,168]{0,1:T(8,128)S(1)}, f32[128,168]{0,1:T(8,128)}, u32[]{:S(2)}) copy-start(f32[128,168]{0,1:T(8,128)} %copy.214) | copy-start | bytes 258052
  93.6 4.2 %copy-start.15 = (f32[128,168]{0,1:T(8,128)S(1)}, f32[128,168]{0,1:T(8,128)}, u32[]{:S(2)}) copy-start(f32[128,168]{0,1:T(8,128)} %copy.215) | copy-start | bytes 258052
  93.6 4.2 %copy-start.16 = (f32[128,168]{0,1:T(8,128)S(1)}, f32[128,168]{0,1:T(8,128)}, u32[]{:S(2)}) copy-start(f32[128,168]{0,1:T(8,128)} %copy.216) | copy-start | bytes 258052
  93.6 4.2 %copy-start.17 = (f32[128,168]{0,1:T(8,128)S(1)}, f32[128,168]{0,1:T(8,128)}, u32[]{:S(2)}) copy-start(f32[128,168]{0,1:T(8,128)} %copy.217) | copy-start | bytes 258052
  93.6 4.2 %copy-start.18 = (f32[128,168]{0,1:T(8,128)S(1)}, f32[128,168]{0,1:T(8,128)}, u32[]{:S(2)}) copy-start(f32[128,168]{0,1:T(8,128)} %copy.218) | copy-start | bytes 258052
  93.6 4.2 %copy-start.19 = (f32[128,168]{0,1:T(8,128)S(1)}, f32[128,168]{0,1:T(8,128)}, u32[]{:S(2)}) copy-start(f32[128,168]{0,1:T(8,128)} %copy.219) | copy-start | bytes 258052
  93.6 4.2 %copy-start.20 = (f32[128,168]{0,1:T(8,128)S(1)}, f32[128,168]{0,1:T(8,128)}, u32[]{:S(2)}) copy-start(f32[128,168]{0,1:T(8,128)} %copy.220) | copy-start | bytes 258052
  93.6 4.2 %copy-start.21 = (f32[128,168]{0,1:T(8,128)S(1)}, f32[128,168]{0,1:T(8,128)}, u32[]{:S(2)}) copy-start(f32[128,168]{0,1:T(8,128)} %copy.221) | copy-start | bytes 258052
  93.6 4.2 %copy-start.22 = (f32[128,168]{0,1:T(8,128)S(1)}, f32[128,168]{0,1:T(8,128)}, u32[]{:S(2)}) copy-start(f32[128,168]{0,1:T(8,128)} %copy.222) | copy-start | bytes 258052
  93.7 4.2 %copy-start.23 = (f32[128,168]{0,1:T(8,128)S(1)}, f32[128,168]{0,1:T(8,128)}, u32[]{:S(2)}) copy-start(f32[128,168]{0,1:T(8,128)} %copy.223) | copy-start | bytes 258052
  93.7 4.2 %copy-start.24 = (f32[128,168]{0,1:T(8,128)S(1)}, f32[128,168]{0,1:T(8,128)}, u32[]{:S(2)}) copy-start(f32[128,168]{0,1:T(8,128)} %copy.224) | copy-start | bytes 258052
  93.7 4.2 %copy-start.26 = (f32[16]{0:T(128)S(1)}, f32[16]{0:T(128)}, u32[]{:S(2)}) copy-start(f32[16]{0:T(128)} %get-tuple-element.55) | copy-start | bytes 196
  93.7 4.2 %copy-start.27 = (f32[16]{0:T(128)S(1)}, f32[16]{0:T(128)}, u32[]{:S(2)}) copy-start(f32[16]{0:T(128)} %get-tuple-element.56) | copy-start | bytes 196
  93.7 4.2 %copy-start.28 = (f32[16]{0:T(128)S(1)}, f32[16]{0:T(128)}, u32[]{:S(2)}) copy-start(f32[16]{0:T(128)} %get-tuple-element.57) | copy-start | bytes 196
  93.7 4.2 %copy-start.29 = (f32[16]{0:T(128)S(1)}, f32[16]{0:T(128)}, u32[]{:S(2)}) copy-start(f32[16]{0:T(128)} %get-tuple-element.58) | copy-start | bytes 196
  93.7 4.2 %copy-start.30 = (f32[16]{0:T(128)S(1)}, f32[16]{0:T(128)}, u32[]{:S(2)}) copy-start(f32[16]{0:T(128)} %get-tuple-element.59) | copy-start | bytes 196
  93.7 4.2 %copy-start.31 = (f32[16]{0:T(128)S(1)}, f32[16]{0:T(128)}, u32[]{:S(2)}) copy-start(f32[16]{0:T(128)} %get-tuple-element.60) | copy-start | bytes 196
  93.7 4.2 %copy-start.32 = (f32[16]{0:T(128)S(1)}, f32[16]{0:T(128)}, u32[]{:S(2)}) copy-start(f32[16]{0:T(128)} %get-tuple-element.61) | copy-start | bytes 196
  93.7 4.2 %copy-start.33 = (f32[16]{0:T(128)S(1)}, f32[16]{0:T(128)}, u32[]{:S(2)}) copy-start(f32[16]{0:T(128)} %get-tuple-element.62) | copy-start | bytes 196
  93.8 4.2 %copy-start.34 = (f32[16]{0:T(128)S(1)}, f32[16]{0:T(128)}, u32[]{:S(2)}) copy-start(f32[16]{0:T(128)} %get-tuple-element.63) | copy-start | bytes 196
  93.8 4.2 %copy-start.35 = (f32[16]{0:T(128)S(1)}, f32[16]{0:T(128)}, u32[]{:S(2)}) copy-start(f32[16]{0:T(128)} %get-tuple-element.64) | copy-start | bytes 196
  93.8 4.2 %copy-start.36 = (f32[16]{0:T(128)S(1)}, f32[16]{0:T(128)}, u32[]{:S(2)}) copy-start(f32[16]{0:T(128)} %get-tuple-element.65) | copy-start | bytes 196
  93.8 4.2 %copy-start.37 = (f32[16]{0:T(128)S(1)}, f32[16]{0:T(128)}, u32[]{:S(2)}) copy-start(f32[16]{0:T(128)} %get-tuple-element.66) | copy-start | bytes 196
  93.8 4.2 %copy-start.38 = (f32[16]{0:T(128)S(1)}, f32[16]{0:T(128)}, u32[]{:S(2)}) copy-start(f32[16]{0:T(128)} %get-tuple-element.67) | copy-start | bytes 196
  93.8 4.2 %copy-start.39 = (f32[16]{0:T(128)S(1)}, f32[16]{0:T(128)}, u32[]{:S(2)}) copy-start(f32[16]{0:T(128)} %get-tuple-element.68) | copy-start | bytes 196
  93.8 4.2 %copy-start.40 = (f32[16]{0:T(128)S(1)}, f32[16]{0:T(128)}, u32[]{:S(2)}) copy-start(f32[16]{0:T(128)} %get-tuple-element.69) | copy-start | bytes 196
  100.0 7.1 %copy-start.44 = (f32[16]{0:T(128)S(1)}, f32[16]{0:T(128)}, u32[]{:S(2)}) copy-start(f32[16]{0:T(128)} %get-tuple-element.31) | copy-start | bytes 196
  100.0 7.1 %copy-start.45 = (f32[16]{0:T(128)S(1)}, f32[16]{0:T(128)}, u32[]{:S(2)}) copy-start(f32[16]{0:T(128)} %get-tuple-element.32) | copy-start | bytes 196
  100.0 7.1 %copy-start.46 = (f32[16]{0:T(128)S(1)}, f32[16]{0:T(128)}, u32[]{:S(2)}) copy-start(f32[16]{0:T(128)} %get-tuple-element.33) | copy-start | bytes 196
  100.0 7.1 %copy-start.47 = (f32[16]{0:T(128)S(1)}, f32[16]{0:T(128)}, u32[]{:S(2)}) copy-start(f32[16]{0:T(128)} %get-tuple-element.34) | copy-start | bytes 196
  100.0 7.1 %copy-start.48 = (f32[16]{0:T(128)S(1)}, f32[16]{0:T(128)}, u32[]{:S(2)}) copy-start(f32[16]{0:T(128)} %get-tuple-element.35) | copy-start | bytes 196
  100.0 7.1 %copy-start.49 = (f32[16]{0:T(128)S(1)}, f32[16]{0:T(128)}, u32[]{:S(2)}) copy-start(f32[16]{0:T(128)} %get-tuple-element.36) | copy-start | bytes 196
  100.0 7.1 %copy-start.50 = (f32[16]{0:T(128)S(1)}, f32[16]{0:T(128)}, u32[]{:S(2)}) copy-start(f32[16]{0:T(128)} %get-tuple-element.37) | copy-start | bytes 196
  100.0 7.1 %copy-start.51 = (f32[16]{0:T(128)S(1)}, f32[16]{0:T(128)}, u32[]{:S(2)}) copy-start(f32[16]{0:T(128)} %get-tuple-element.38) | copy-start | bytes 196
  100.0 7.1 %copy-start.52 = (f32[16]{0:T(128)S(1)}, f32[16]{0:T(128)}, u32[]{:S(2)}) copy-start(f32[16]{0:T(128)} %get-tuple-element.39) | copy-start | bytes 196
  100.1 7.1 %copy-start.53 = (f32[16]{0:T(128)S(1)}, f32[16]{0:T(128)}, u32[]{:S(2)}) copy-start(f32[16]{0:T(128)} %get-tuple-element.40) | copy-start | bytes 196
  100.1 7.1 %copy-start.54 = (f32[16]{0:T(128)S(1)}, f32[16]{0:T(128)}, u32[]{:S(2)}) copy-start(f32[16]{0:T(128)} %get-tuple-element.41) | copy-start | bytes 196
  100.1 7.1 %copy-start.55 = (f32[16]{0:T(128)S(1)}, f32[16]{0:T(128)}, u32[]{:S(2)}) copy-start(f32[16]{0:T(128)} %get-tuple-element.42) | copy-start | bytes 196
  100.1 7.1 %copy-start.56 = (f32[16]{0:T(128)S(1)}, f32[16]{0:T(128)}, u32[]{:S(2)}) copy-start(f32[16]{0:T(128)} %get-tuple-element.43) | copy-start | bytes 196
  100.1 7.1 %copy-start.57 = (f32[16]{0:T(128)S(1)}, f32[16]{0:T(128)}, u32[]{:S(2)}) copy-start(f32[16]{0:T(128)} %get-tuple-element.44) | copy-start | bytes 196
  100.1 7.1 %copy-start.58 = (f32[16]{0:T(128)S(1)}, f32[16]{0:T(128)}, u32[]{:S(2)}) copy-start(f32[16]{0:T(128)} %get-tuple-element.45) | copy-start | bytes 196
  100.1 7.1 %copy-start.59 = (f32[16]{0:T(128)S(1)}, f32[16]{0:T(128)}, u32[]{:S(2)}) copy-start(f32[16]{0:T(128)} %get-tuple-element.46) | copy-start | bytes 196
  100.1 7.1 %copy-start.60 = (f32[16]{0:T(128)S(1)}, f32[16]{0:T(128)}, u32[]{:S(2)}) copy-start(f32[16]{0:T(128)} %get-tuple-element.47) | copy-start | bytes 196
  100.1 7.1 %copy-start.61 = (f32[16]{0:T(128)S(1)}, f32[16]{0:T(128)}, u32[]{:S(2)}) copy-start(f32[16]{0:T(128)} %get-tuple-element.48) | copy-start | bytes 196
  100.1 7.1 %copy-start.62 = (f32[16]{0:T(128)S(1)}, f32[16]{0:T(128)}, u32[]{:S(2)}) copy-start(f32[16]{0:T(128)} %get-tuple-element.49) | copy-start | bytes 196
  115.8 4.9 %copy-start.1 = (f32[1,128,2048]{2,1,0:T(8,128)S(1)}, f32[1,128,2048]{2,1,0:T(8,128)}, u32[]{:S(2)}) copy-start(f32[1,128,2048]{2,1,0:T(8,128)} %param.14) | copy-start | bytes 3145732
  115.8 22.6 %all-to-all-start.1 = ((f32[8,2,128,148]{2,1,3,0:T(2,128)}), f32[8,2,128,148]{2,1,3,0:T(2,128)S(1)}, u32[]{:S(2)}, u32[]{:S(2)}) async-start(f32[8,2,128,148]{2,1,3,0:T(2,128)} %copy.226), calls=%async_computation.1 | async-start | bytes 2424832 | tf_op jit(solution)/shard_map/all_to_all | solution.py:76
  (6 other events, 20.5 us)

commit v4 on v3

--- a/solution.py
+++ b/solution.py
@@ -17,16 +17,20 @@
     )
 
 
-def separable(padded, row_taps, col_taps, tile_rows, span):
-    passed = jnp.zeros((row_taps.shape[0], tile_rows, padded.shape[1]), jnp.float32)
-    for offset in range(row_taps.shape[1]):
-        passed = (
-            passed + row_taps[:, offset, None, None] * padded[None, offset : offset + tile_rows, :]
-        )
-    images = jnp.zeros((row_taps.shape[0], tile_rows, span), jnp.float32)
-    for offset in range(col_taps.shape[1]):
-        images = images + col_taps[:, offset, None, None] * passed[:, :, offset : offset + span]
-    return images
+def banded(taps, rows, cols):
+    offset = lax.broadcasted_iota(jnp.int32, (rows, cols), 1) - lax.broadcasted_iota(jnp.int32, (rows, cols), 0)
+    band = jnp.zeros((taps.shape[0], rows, cols), jnp.float32)
+    for tap in range(taps.shape[1]):
+        band = band + jnp.where(offset == tap, taps[:, tap, None, None], jnp.float32(0.0))
+    return band
+
+
+def separable(blocks, row_taps, col_taps, tile_rows, span):
+    reach = row_taps.shape[1]
+    down = banded(row_taps, tile_rows, tile_rows + reach - 1)
+    across = jnp.swapaxes(banded(col_taps, span, span + reach - 1), 1, 2)
+    passed = jnp.einsum("kra,bac->bkrc", down, blocks, precision=lax.Precision.HIGHEST)
+    return jnp.einsum("bkrc,kcd->bkrd", passed, across, precision=lax.Precision.HIGHEST)
 
 
 def local(template, row_taps, col_taps, coeffs, visits, boxes):
@@ -65,12 +69,12 @@
     blocks = jnp.pad(blocks, ((0, 0), (0, 0), (2 * half, 2 * half)))
     span = columns + 2 * half
     y_coord = coordinate(tile * tile_rows, tile_rows, total_rows)
+    basis = separable(blocks, row_taps, col_taps, tile_rows, span)
     models = []
     for b in range(halves):
-        basis = separable(blocks[b], row_taps, col_taps, tile_rows, span)
         start = (b * group + place) * columns - half
         terms = surface_terms(y_coord, coordinate(start, span, full_width))
-        weighted = jnp.einsum("vkt,krc->vtrc", half_coeffs, basis, precision=lax.Precision.HIGHEST)
+        weighted = jnp.einsum("vkt,krc->vtrc", half_coeffs, basis[b], precision=lax.Precision.HIGHEST)
         models.append(jnp.sum(weighted * terms[None], axis=1))
     models = jnp.stack(models, axis=1)
     parts = lax.all_to_all(models, "xc", 0, 0, tiled=True)

time: 142 us -> 87.8 us (0.62)
  local copies, waits for them, and re-layouts: 69.4 us -> 16.1 us
  matrix products: 13.4 us -> 19.1 us
  other arithmetic: 7.42 us -> 2.14 us
    mul x45 -> x0, local copies, waits for them, and re-layouts: 48.8 us -> none  [separable(): row_taps[:, offset, None, None] * padded[None, offset:offset + tile_rows, :]]
    dot_general x2 -> x4, matrix products: 13.4 us -> 19.1 us  [the longest x1 7.82 us: separable(): jnp.einsum('bkrc,kcd->bkrd', passed, across, precision=lax.Precision.HIGH...]
    add x2 -> x0, other arithmetic: 5.71 us -> none  [separable(): passed + row_taps[:, offset, None, None] * padded[None, offset:offset + t...]
    slice x4, local copies, waits for them, and re-layouts: 8.03 us -> 3.57 us  [banded(): taps[:, tap, None, None]]
  transfers between devices with their start and end apart: 7 -> 7, of which waited for: 1 -> 1; matrix products, arithmetic and copies ran while one was open for 51% -> 30% of each run, Pallas kernels for 0% -> 0%
where the time goes in v4:
time: 87.8 us; the launch traced here: 87.3 us
  starting transfers between devices  33.3 us (38%)
  matrix products  19.1 us (22%)
  local copies, waits for them, and re-layouts  16.1 us (18%)
  waiting for transfers between devices  14.9 us (17%)
  other arithmetic  2.14 us (2%)
  between operations  1.76 us (2%)
    all_to_all x1, waiting for transfers between devices, local(): parts = lax.all_to_all(models, 'xc', 0, 0, tiled=True)  14.8 us
    ppermute x1, starting transfers between devices, local(): partner_above = lax.ppermute(bottom, ('tile', 'zhi'), crossed(down))  9.21 us
    dot_general x1, matrix products, separable(): jnp.einsum('bkrc,kcd->bkrd', passed, across, precision=lax.Precision.HIGH...  7.82 us
    dot_general x2, matrix products, local(): jnp.einsum('vkt,krc->vtrc', half_coeffs, basis[b], precision=lax.Precisio...  6.38 us
    ppermute x1, starting transfers between devices, local(): partner = lax.ppermute(template, 'zhi', swap)  5.89 us
    another operation x8, local copies, waits for them, and re-layouts, surface_terms(): jnp.stack([jnp.ones_like(x_grid), x_grid, y_grid, x_grid * x_grid, x_grid...  5.4 us
    all_to_all x1, starting transfers between devices, local(): parts = lax.all_to_all(models, 'xc', 0, 0, tiled=True)  4.93 us
    dot_general x1, matrix products, separable(): jnp.einsum('kra,bac->bkrc', down, blocks, precision=lax.Precision.HIGHEST)  4.93 us
  transfers between devices with their start and end apart: 7, of which 1 were waited for; matrix products, arithmetic and copies ran while one was open for 30% of the time, Pallas kernels for 0%

profile of v4, /device:TPU:32, one launch (start us, length us, event | category | flops | bytes accessed | tf_op | source)
XLA Modules:
  0.0 87.3 jit_solution(13687433466223542870)
XLA Ops:
  0.0 0.0 copy-start
  0.0 0.0 copy-start.1
  0.0 0.7 fusion.253
  0.7 3.5 %collective-permute-start = (f32[10,128]{1,0:T(8,128)S(1)}, f32[10,128]{1,0:T(8,128)S(1)}, u32[]{:S(2)}, u32[]{:S(2)}) collective-permute-start(f32[10,128]{1,0:T(8,128)S(1)} %get-tuple-element.77), channel_id=1, source_target_pairs={{0,16},{16,32},{32,48},{48,64},{64,80},{80,96},{96,112},{112,128},... | collective-permute-start | bytes 15368 | tf_op jit(solution)/shard_map/ppermute | solution.py:57
  4.2 9.2 %collective-permute-start.2 = (f32[10,128]{1,0:T(8,128)S(1)}, f32[10,128]{1,0:T(8,128)S(1)}, u32[]{:S(2)}, u32[]{:S(2)}) collective-permute-start(f32[10,128]{1,0:T(8,128)S(1)} %get-tuple-element.77), channel_id=1, source_target_pairs={{0,24},{8,16},{16,40},{24,32},{32,56},{40,48},{48,72},{56,64},{64,... | collective-permute-start | bytes 15368 | tf_op jit(solution)/shard_map/ppermute | solution.py:63
  13.4 3.6 %collective-permute-start.1 = (f32[10,128]{1,0:T(8,128)S(1)}, f32[10,128]{1,0:T(8,128)S(1)}, u32[]{:S(2)}, u32[]{:S(2)}) collective-permute-start(f32[10,128]{1,0:T(8,128)S(1)} %get-tuple-element.78), channel_id=1, source_target_pairs={{16,0},{32,16},{48,32},{64,48},{80,64},{96,80},{112,96},{128,112},... | collective-permute-start | bytes 15368 | tf_op jit(solution)/shard_map/ppermute | solution.py:58
  17.0 1.9 %collective-permute-start.4 = (f32[10,128]{1,0:T(8,128)S(1)}, f32[10,128]{1,0:T(8,128)S(1)}, u32[]{:S(2)}, u32[]{:S(2)}) collective-permute-start(f32[10,128]{1,0:T(8,128)S(1)} %get-tuple-element.78), channel_id=1, source_target_pairs={{16,8},{24,0},{32,24},{40,16},{48,40},{56,32},{64,56},{72,48},{80,... | collective-permute-start | bytes 15368 | tf_op jit(solution)/shard_map/ppermute | solution.py:64
  19.0 5.9 %collective-permute-start.3 = (f32[128,128]{1,0:T(8,128)}, f32[128,128]{1,0:T(8,128)S(1)}, u32[]{:S(2)}, u32[]{:S(2)}) collective-permute-start(f32[128,128]{1,0:T(8,128)} %param.10), channel_id=1, source_target_pairs={{0,8},{8,0},{1,9},{9,1},{2,10},{10,2},{3,11},{11,3},{4,12},{12,4},... | collective-permute-start | bytes 196616 | tf_op jit(solution)/shard_map/ppermute | solution.py:54
  24.8 0.7 copy.55
  25.5 0.6 broadcast_in_dim.635
  26.1 4.3 %all-to-all-start = ((f32[8,16,6]{1,2,0:T(8,128)}), f32[8,16,6]{1,2,0:T(8,128)S(1)}, u32[]{:S(2)}, u32[]{:S(2)}) async-start(f32[8,16,6]{1,2,0:T(8,128)} %broadcast_in_dim.635), calls=%async_computation | async-start | bytes 65536 | tf_op jit(solution)/shard_map/all_to_all | solution.py:49
  30.8 1.9 %slice_reduce_fusion.20 = (f32[16]{0:T(128)S(1)}, f32[16]{0:T(128)S(1)}, f32[16]{0:T(128)S(1)}, f32[16]{0:T(128)S(1)}, f32[16]{0:T(128)S(1)}, /*index=5*/f32[16]...) fusion(f32[16,21]{1,0:T(8,128)} %param.11), kind=kLoop, calls=%fused_computation.275 | loop fusion | bytes 2432 | tf_op jit(solution)/shard_map/slice | solution.py:24
  32.7 1.0 %slice_reduce_fusion.1 = (f32[16]{0:T(128)S(1)}, f32[16]{0:T(128)S(1)}) fusion(f32[16,21]{1,0:T(8,128)} %param.11), kind=kLoop, calls=%fused_computation.256 | loop fusion | bytes 256 | tf_op jit(solution)/shard_map/slice | solution.py:24
  34.1 0.0 copy-done.1
  34.2 0.5 slice_reduce_fusion.41
  34.7 0.4 broadcast_multiply_fusion.1
  35.1 0.2 slice_reduce_fusion.22
  35.3 0.2 stack.43
  35.5 0.2 stack.45
  35.7 0.0 copy-start.4
  35.9 2.0 %stack.47 = f32[6,128,148]{1,0,2:T(8,128)S(1)} concatenate(f32[1,128,148]{1,0,2:T(1,128)S(1)} %broadcast.231, f32[1,128,148]{1,0,2:T(1,128)S(1)} %stack.43, f32[1,128,148]{1,0,2:T(1,128)S(1)} %stack.44, f32[1,128,148]{1,0,2:T(1,128)S(1)} %stack.45, f32[1,128,148]{1,0,2:T(1,128)S(1)} %get-tuple-element.81, f32[1,128,148]{1,0,2:T(1,128)S(1)} %stack.46), dimensions={0} | concatenate | bytes 909312 | tf_op jit(solution)/shard_map/stack | solution.py:15
  37.9 0.2 stack.49
  38.1 0.2 stack.50
  38.3 2.5 %stack.51 = f32[6,128,148]{1,0,2:T(8,128)} concatenate(f32[1,128,148]{1,0,2:T(1,128)S(1)} %broadcast.231, f32[1,128,148]{1,0,2:T(1,128)S(1)} %stack.49, f32[1,128,148]{1,0,2:T(1,128)S(1)} %stack.44, f32[1,128,148]{1,0,2:T(1,128)S(1)} %stack.50, f32[1,128,148]{1,0,2:T(1,128)S(1)} %get-tuple-element.82, f32[1,128,148]{1,0,2:T(1,128)S(1)} %stack.46), dimensions={0} | concatenate | bytes 909312 | tf_op jit(solution)/shard_map/stack | solution.py:15
  40.8 0.0 collective-permute-done
  40.8 0.0 collective-permute-done.1
  40.8 0.0 collective-permute-done.2
  40.8 0.0 collective-permute-done.4
  40.8 0.0 collective-permute-done.3
  40.8 0.0 copy-done.4
  40.9 4.9 %fusion.51 = f32[2,168,16,128]{3,1,0,2:T(8,128)S(1)} fusion(f32[16]{0:T(128)S(1)} %get-tuple-element.70, f32[16]{0:T(128)S(1)} %get-tuple-element.69, f32[16]{0:T(128)S(1)} %get-tuple-element.51, f32[16]{0:T(128)S(1)} %get-tuple-element.52, f32[16]{0:T(128)S(1)} %get-tuple-element.53, f32[16]{0:T(128)S(1)} %get-tuple-element.54, ...), kind=kOutput, calls=%fused_computation.51 | convolution fusion | flops 1234840960 | bytes 3303232 | tf_op jit(solution)/shard_map/kra,bac->bkrc/dot_general | solution.py:32
  45.8 7.8 %fusion.46 = f32[2,16,128,148]{2,3,0,1:T(8,128)S(1)} fusion(f32[2,168,16,128]{3,1,0,2:T(8,128)S(1)} %fusion.51, f32[16]{0:T(128)S(1)} %get-tuple-element.49, f32[16]{0:T(128)S(1)} %get-tuple-element.48, f32[16]{0:T(128)S(1)} %get-tuple-element.30, f32[16]{0:T(128)S(1)} %get-tuple-element.31, f32[16]{0:T(128)S(1)} %get-tuple-element.32, ...), kind=kOutput, calls=%fused_computation.48 | convolution fusion | flops 1238426112 | bytes 5700832 | tf_op jit(solution)/shard_map/bkrc,kcd->bkrd/dot_general | solution.py:33
  53.6 0.2 slice_bitcast_fusion.1
  53.8 0.0 all-to-all-done
  53.8 0.0 copy-start.2
  53.8 3.2 %fusion.1 = f32[8,128,148]{1,0,2:T(8,128)S(1)} fusion(f32[6,128,148]{1,0,2:T(8,128)S(1)} %stack.47, f32[16,128,148,1]{1,2,0,3:T(8,128)S(1)} %get-tuple-element.71, f32[8,16,6]{1,2,0:T(8,128)S(1)} %all-to-all-done), kind=kOutput, calls=%fused_computation.3 | convolution fusion | flops 176254976 | bytes 2276352 | tf_op jit(solution)/shard_map/vkt,krc->vtrc/dot_general | solution.py:77
  57.0 0.0 copy-done.2
  57.0 3.2 %fusion = f32[8,128,148]{1,0,2:T(8,128)S(1)} fusion(f32[6,128,148]{1,0,2:T(8,128)S(1)} %copy-done.2, f32[16,128,148,1]{1,2,0,3:T(8,128)S(1)} %get-tuple-element.72, f32[8,16,6]{1,2,0:T(8,128)S(1)} %all-to-all-done), kind=kOutput, calls=%fused_computation.1 | convolution fusion | flops 176254976 | bytes 2276352 | tf_op jit(solution)/shard_map/vkt,krc->vtrc/dot_general | solution.py:77
  60.2 0.1 pad_maximum_fusion
  60.3 2.0 %copy.26 = f32[8,2,128,148]{2,1,3,0:T(2,128)} copy(f32[8,2,128,148]{2,0,3,1:T(8,128)S(1)} %pad_maximum_fusion) | data formatting | bytes 2424832 | tf_op jit(solution)/shard_map/stack | solution.py:79
  62.3 0.0 copy-start.3
  62.3 4.9 %all-to-all-start.1 = ((f32[8,2,128,148]{2,1,3,0:T(2,128)}), f32[8,2,128,148]{2,1,3,0:T(2,128)S(1)}, u32[]{:S(2)}, u32[]{:S(2)}) async-start(f32[8,2,128,148]{2,1,3,0:T(2,128)} %copy.26), calls=%async_computation.1 | async-start | bytes 2424832 | tf_op jit(solution)/shard_map/all_to_all | solution.py:80
  67.2 0.0 copy-done.3
  67.2 0.3 copy.29
  67.5 0.0 copy-done
  67.6 0.1 constant_dynamic-slice_fusion
  67.6 0.5 fusion.254
  69.4 0.6 fusion.243
  70.1 14.8 %all-to-all-done.1 = f32[8,2,128,148]{2,1,3,0:T(2,128)S(1)} async-done(((f32[8,2,128,148]{2,1,3,0:T(2,128)}), f32[8,2,128,148]{2,1,3,0:T(2,128)S(1)}, u32[]{:S(2)}, u32[]{:S(2)}) %all-to-all-start.1) | async-done | bytes 1212448 | tf_op jit(solution)/shard_map/all_to_all | solution.py:80
  84.9 0.2 copy.54
  85.1 0.1 slice.262
  85.3 0.3 copy.28
  85.6 0.3 fusion.139
  86.0 1.3 %copy.30 = f32[1,128,2048]{2,1,0:T(8,128)} copy(f32[1,128,2048]{1,2,0:T(8,128)S(1)} %fusion.139) | data formatting | bytes 2097152 | tf_op jit(solution)/shard_map/jit(_where)/select_n | solution.py:96
  (32 shorter events, 0.9 us)
Async XLA Ops:
  0.0 67.5 %copy-start = (s32[16,2]{0,1:T(2,128)S(1)}, s32[16,2]{0,1:T(2,128)}, u32[]{:S(2)}) copy-start(s32[16,2]{0,1:T(2,128)} %param.15) | copy-start | bytes 388
  0.0 34.1 %copy-start.1 = (f32[16,21]{1,0:T(8,128)S(1)}, f32[16,21]{1,0:T(8,128)}, u32[]{:S(2)}) copy-start(f32[16,21]{1,0:T(8,128)} %param.12) | copy-start | bytes 4036
  0.7 40.0 %collective-permute-start = (f32[10,128]{1,0:T(8,128)S(1)}, f32[10,128]{1,0:T(8,128)S(1)}, u32[]{:S(2)}, u32[]{:S(2)}) collective-permute-start(f32[10,128]{1,0:T(8,128)S(1)} %get-tuple-element.77), channel_id=1, source_target_pairs={{0,16},{16,32},{32,48},{48,64},{64,80},{80,96},{96,112},{112,128},... | collective-permute-start | bytes 15368 | tf_op jit(solution)/shard_map/ppermute | solution.py:57
  4.2 36.6 %collective-permute-start.2 = (f32[10,128]{1,0:T(8,128)S(1)}, f32[10,128]{1,0:T(8,128)S(1)}, u32[]{:S(2)}, u32[]{:S(2)}) collective-permute-start(f32[10,128]{1,0:T(8,128)S(1)} %get-tuple-element.77), channel_id=1, source_target_pairs={{0,24},{8,16},{16,40},{24,32},{32,56},{40,48},{48,72},{56,64},{64,... | collective-permute-start | bytes 15368 | tf_op jit(solution)/shard_map/ppermute | solution.py:63
  13.4 27.4 %collective-permute-start.1 = (f32[10,128]{1,0:T(8,128)S(1)}, f32[10,128]{1,0:T(8,128)S(1)}, u32[]{:S(2)}, u32[]{:S(2)}) collective-permute-start(f32[10,128]{1,0:T(8,128)S(1)} %get-tuple-element.78), channel_id=1, source_target_pairs={{16,0},{32,16},{48,32},{64,48},{80,64},{96,80},{112,96},{128,112},... | collective-permute-start | bytes 15368 | tf_op jit(solution)/shard_map/ppermute | solution.py:58
  17.0 23.8 %collective-permute-start.4 = (f32[10,128]{1,0:T(8,128)S(1)}, f32[10,128]{1,0:T(8,128)S(1)}, u32[]{:S(2)}, u32[]{:S(2)}) collective-permute-start(f32[10,128]{1,0:T(8,128)S(1)} %get-tuple-element.78), channel_id=1, source_target_pairs={{16,8},{24,0},{32,24},{40,16},{48,40},{56,32},{64,56},{72,48},{80,... | collective-permute-start | bytes 15368 | tf_op jit(solution)/shard_map/ppermute | solution.py:64
  19.0 21.9 %collective-permute-start.3 = (f32[128,128]{1,0:T(8,128)}, f32[128,128]{1,0:T(8,128)S(1)}, u32[]{:S(2)}, u32[]{:S(2)}) collective-permute-start(f32[128,128]{1,0:T(8,128)} %param.10), channel_id=1, source_target_pairs={{0,8},{8,0},{1,9},{9,1},{2,10},{10,2},{3,11},{11,3},{4,12},{12,4},... | collective-permute-start | bytes 196616 | tf_op jit(solution)/shard_map/ppermute | solution.py:54
  26.1 27.7 %all-to-all-start = ((f32[8,16,6]{1,2,0:T(8,128)}), f32[8,16,6]{1,2,0:T(8,128)S(1)}, u32[]{:S(2)}, u32[]{:S(2)}) async-start(f32[8,16,6]{1,2,0:T(8,128)} %broadcast_in_dim.635), calls=%async_computation | async-start | bytes 65536 | tf_op jit(solution)/shard_map/all_to_all | solution.py:49
  35.7 5.1 %copy-start.4 = (f32[128,128]{1,0:T(8,128)S(1)}, f32[128,128]{1,0:T(8,128)}, u32[]{:S(2)}) copy-start(f32[128,128]{1,0:T(8,128)} %param.10) | copy-start | bytes 196612
  53.8 3.2 %copy-start.2 = (f32[6,128,148]{1,0,2:T(8,128)S(1)}, f32[6,128,148]{1,0,2:T(8,128)}, u32[]{:S(2)}) copy-start(f32[6,128,148]{1,0,2:T(8,128)} %stack.51) | copy-start | bytes 1363972
  62.3 4.9 %copy-start.3 = (f32[1,128,2048]{2,1,0:T(8,128)S(1)}, f32[1,128,2048]{2,1,0:T(8,128)}, u32[]{:S(2)}) copy-start(f32[1,128,2048]{2,1,0:T(8,128)} %param.14) | copy-start | bytes 3145732
  62.3 22.6 %all-to-all-start.1 = ((f32[8,2,128,148]{2,1,3,0:T(2,128)}), f32[8,2,128,148]{2,1,3,0:T(2,128)S(1)}, u32[]{:S(2)}, u32[]{:S(2)}) async-start(f32[8,2,128,148]{2,1,3,0:T(2,128)} %copy.26), calls=%async_computation.1 | async-start | bytes 2424832 | tf_op jit(solution)/shard_map/all_to_all | solution.py:80

commit v5 on v4

--- a/solution.py
+++ b/solution.py
@@ -19,18 +19,16 @@
 
 def banded(taps, rows, cols):
     offset = lax.broadcasted_iota(jnp.int32, (rows, cols), 1) - lax.broadcasted_iota(jnp.int32, (rows, cols), 0)
-    band = jnp.zeros((taps.shape[0], rows, cols), jnp.float32)
-    for tap in range(taps.shape[1]):
-        band = band + jnp.where(offset == tap, taps[:, tap, None, None], jnp.float32(0.0))
-    return band
+    picks = (offset[None] == jnp.arange(taps.shape[1])[:, None, None]).astype(jnp.float32)
+    return jnp.einsum("ka,arc->krc", taps, picks, precision=lax.Precision.HIGHEST)
 
 
 def separable(blocks, row_taps, col_taps, tile_rows, span):
     reach = row_taps.shape[1]
     down = banded(row_taps, tile_rows, tile_rows + reach - 1)
     across = jnp.swapaxes(banded(col_taps, span, span + reach - 1), 1, 2)
-    passed = jnp.einsum("kra,bac->bkrc", down, blocks, precision=lax.Precision.HIGHEST)
-    return jnp.einsum("bkrc,kcd->bkrd", passed, across, precision=lax.Precision.HIGHEST)
+    passed = jnp.einsum("kra,bac->bkrc", down, blocks, precision=lax.Precision.HIGH)
+    return jnp.einsum("bkrc,kcd->bkrd", passed, across, precision=lax.Precision.HIGH)
 
 
 def local(template, row_taps, col_taps, coeffs, visits, boxes):
@@ -71,11 +69,12 @@
     y_coord = coordinate(tile * tile_rows, tile_rows, total_rows)
     basis = separable(blocks, row_taps, col_taps, tile_rows, span)
     models = []
+    y = y_coord[:, None]
     for b in range(halves):
         start = (b * group + place) * columns - half
-        terms = surface_terms(y_coord, coordinate(start, span, full_width))
-        weighted = jnp.einsum("vkt,krc->vtrc", half_coeffs, basis[b], precision=lax.Precision.HIGHEST)
-        models.append(jnp.sum(weighted * terms[None], axis=1))
+        x = coordinate(start, span, full_width)[None, :]
+        w = jnp.einsum("vkt,krc->tvrc", half_coeffs, basis[b], precision=lax.Precision.HIGH)
+        models.append(w[0] + x * w[1] + y * w[2] + (x * x) * w[3] + (x * y) * w[4] + (y * y) * w[5])
     models = jnp.stack(models, axis=1)
     parts = lax.all_to_all(models, "xc", 0, 0, tiled=True)
     parts = jnp.swapaxes(parts, 0, 1).reshape((halves * group,) + parts.shape[2:])

time: 87.8 us -> 77 us (0.88)
  the two profiles are of different devices: /device:TPU:32 before, /device:TPU:16 now
where the time goes in v5:
time: 77 us; the launch traced here: 76.6 us
  starting transfers between devices  35.1 us (46%)
  matrix products  15.9 us (21%)
  waiting for transfers between devices  14.8 us (19%)
  local copies, waits for them, and re-layouts  7.16 us (9%)
  other arithmetic  2.13 us (3%)
  between operations  1.6 us (2%)
    all_to_all x1, waiting for transfers between devices, local(): parts = lax.all_to_all(models, 'xc', 0, 0, tiled=True)  14.7 us
    ppermute x1, starting transfers between devices, local(): partner_below = lax.ppermute(top, ('tile', 'zhi'), crossed(up))  8.97 us
    ppermute x1, starting transfers between devices, local(): partner = lax.ppermute(template, 'zhi', swap)  6.19 us
    dot_general x1, matrix products, separable(): jnp.einsum('kra,bac->bkrc', down, blocks, precision=lax.Precision.HIGH)  5.15 us
    all_to_all x1, starting transfers between devices, local(): parts = lax.all_to_all(models, 'xc', 0, 0, tiled=True)  4.93 us
    ppermute x1, starting transfers between devices, local(): partner_above = lax.ppermute(bottom, ('tile', 'zhi'), crossed(down))  4.86 us
    dot_general x2, matrix products, banded(): jnp.einsum('ka,arc->krc', taps, picks, precision=lax.Precision.HIGHEST)  4.35 us
    all_to_all x1, starting transfers between devices, local(): half_coeffs = lax.all_to_all(copies, 'xc', 0, 0, tiled=True)  4.3 us
  transfers between devices with their start and end apart: 7, of which 1 were waited for; matrix products, arithmetic and copies ran while one was open for 21% of the time, Pallas kernels for 0%

profile of v5, /device:TPU:16, one launch (start us, length us, event | category | flops | bytes accessed | tf_op | source)
XLA Modules:
  0.0 76.6 jit_solution(10979633432603565805)
XLA Ops:
  0.0 0.0 copy-start
  0.0 0.0 copy-start.3
  0.0 0.7 fusion.68
  0.7 9.0 %collective-permute-start.4 = (f32[10,128]{1,0:T(8,128)S(1)}, f32[10,128]{1,0:T(8,128)S(1)}, u32[]{:S(2)}, u32[]{:S(2)}) collective-permute-start(f32[10,128]{1,0:T(8,128)S(1)} %get-tuple-element.36), channel_id=1, source_target_pairs={{16,8},{24,0},{32,24},{40,16},{48,40},{56,32},{64,56},{72,48},{80,... | collective-permute-start | bytes 15368 | tf_op jit(solution)/shard_map/ppermute | solution.py:62
  9.7 2.4 %collective-permute-start.1 = (f32[10,128]{1,0:T(8,128)S(1)}, f32[10,128]{1,0:T(8,128)S(1)}, u32[]{:S(2)}, u32[]{:S(2)}) collective-permute-start(f32[10,128]{1,0:T(8,128)S(1)} %get-tuple-element.36), channel_id=1, source_target_pairs={{16,0},{32,16},{48,32},{64,48},{80,64},{96,80},{112,96},{128,112},... | collective-permute-start | bytes 15368 | tf_op jit(solution)/shard_map/ppermute | solution.py:56
  12.1 3.5 %collective-permute-start = (f32[10,128]{1,0:T(8,128)S(1)}, f32[10,128]{1,0:T(8,128)S(1)}, u32[]{:S(2)}, u32[]{:S(2)}) collective-permute-start(f32[10,128]{1,0:T(8,128)S(1)} %get-tuple-element.35), channel_id=1, source_target_pairs={{0,16},{16,32},{32,48},{48,64},{64,80},{80,96},{96,112},{112,128},... | collective-permute-start | bytes 15368 | tf_op jit(solution)/shard_map/ppermute | solution.py:55
  15.6 4.9 %collective-permute-start.2 = (f32[10,128]{1,0:T(8,128)S(1)}, f32[10,128]{1,0:T(8,128)S(1)}, u32[]{:S(2)}, u32[]{:S(2)}) collective-permute-start(f32[10,128]{1,0:T(8,128)S(1)} %get-tuple-element.35), channel_id=1, source_target_pairs={{0,24},{8,16},{16,40},{24,32},{32,56},{40,48},{48,72},{56,64},{64,... | collective-permute-start | bytes 15368 | tf_op jit(solution)/shard_map/ppermute | solution.py:61
  20.5 6.2 %collective-permute-start.3 = (f32[128,128]{1,0:T(8,128)}, f32[128,128]{1,0:T(8,128)S(1)}, u32[]{:S(2)}, u32[]{:S(2)}) collective-permute-start(f32[128,128]{1,0:T(8,128)} %param.10), channel_id=1, source_target_pairs={{0,8},{8,0},{1,9},{9,1},{2,10},{10,2},{3,11},{11,3},{4,12},{12,4},... | collective-permute-start | bytes 196616 | tf_op jit(solution)/shard_map/ppermute | solution.py:52
  26.6 0.7 copy.112
  27.3 0.6 broadcast_in_dim.14
  28.0 4.3 %all-to-all-start = ((f32[8,16,6]{1,2,0:T(8,128)}), f32[8,16,6]{1,2,0:T(8,128)S(1)}, u32[]{:S(2)}, u32[]{:S(2)}) async-start(f32[8,16,6]{1,2,0:T(8,128)} %broadcast_in_dim.14), calls=%async_computation | async-start | bytes 65536 | tf_op jit(solution)/shard_map/all_to_all | solution.py:47
  32.3 0.0 copy-done
  32.4 0.0 copy-start.2
  32.4 1.7 %fusion.13 = f32[16,148,168,1]{2,0,1,3:T(8,128)S(1)} fusion(s32[148,168]{1,0:T(8,128)S(1)} %iota_subtract_fusion, f32[16,21]{1,0:T(8,128)S(1)} %copy-done), kind=kOutput, calls=%fused_computation.13 | convolution fusion | flops 100773792 | bytes 1692096 | tf_op jit(solution)/shard_map/ka,arc->krc/dot_general | solution.py:23
  34.1 0.1 broadcast_multiply_fusion.1
  34.2 0.0 copy-done.3
  34.2 2.7 %fusion.14 = f32[16,128,148,1]{2,0,1,3:T(8,128)} fusion(s32[128,148]{1,0:T(8,128)S(1)} %iota_subtract_fusion.1, f32[16,21]{1,0:T(8,128)S(1)} %copy-done.3), kind=kOutput, calls=%fused_computation.14 | convolution fusion | flops 76780032 | bytes 1289536 | tf_op jit(solution)/shard_map/ka,arc->krc/dot_general | solution.py:23
  36.8 0.0 collective-permute-done.4
  36.9 0.0 collective-permute-done
  36.9 0.0 collective-permute-done.1
  36.9 0.0 collective-permute-done.2
  36.9 0.0 collective-permute-done.3
  36.9 0.0 copy-done.2
  36.9 5.2 %fusion.5 = f32[2,168,16,128]{3,1,0,2:T(8,128)S(1)} fusion(f32[16,128,148,1]{2,0,1,3:T(8,128)} %fusion.14, f32[1,148,128]{2,1,0:T(8,128)S(1)} %get-tuple-element.34, f32[1,148,128]{2,1,0:T(8,128)S(1)} %get-tuple-element.33), kind=kOutput, calls=%fused_computation.7 | convolution fusion | flops 611356032 | bytes 4116480 | tf_op jit(solution)/shard_map/kra,bac->bkrc/dot_general | solution.py:30
  42.1 3.0 %fusion.8 = f32[2,16,128,148]{2,3,0,1:T(8,128)S(1)} fusion(f32[2,168,16,128]{3,1,0,2:T(8,128)S(1)} %fusion.5, f32[16,148,168,1]{2,0,1,3:T(8,128)S(1)} %fusion.13), kind=kOutput, calls=%fused_computation.12 | convolution fusion | flops 611057664 | bytes 6768640 | tf_op jit(solution)/shard_map/bkrc,kcd->bkrd/dot_general | solution.py:31
  45.1 0.2 slice_bitcast_fusion.1
  45.3 0.0 all-to-all-done
  45.3 1.6 %convolution_bitcast_fusion = f32[6,8,128,148]{2,1,3,0:T(8,128)S(1)} fusion(f32[16,128,148]{1,2,0:T(8,128)S(1)} %get-tuple-element.30, f32[8,16,6,1]{1,2,0,3:T(8,128)S(1)} %bitcast.160), kind=kOutput, calls=%fused_computation.9 | convolution fusion | flops 87293952 | bytes 4852736 | tf_op jit(solution)/shard_map/vkt,krc->tvrc/dot_general | solution.py:76
  46.9 0.4 fusion.21
  47.3 1.8 %convolution_bitcast_fusion.1 = f32[6,8,128,148]{2,1,0,3:T(8,128)S(1)} fusion(f32[16,128,148,1]{1,2,0,3:T(8,128)S(1)} %get-tuple-element.29, f32[8,16,6]{1,2,0:T(8,128)S(1)} %all-to-all-done), kind=kOutput, calls=%fused_computation.10 | convolution fusion | flops 87293952 | bytes 4852736 | tf_op jit(solution)/shard_map/vkt,krc->tvrc/dot_general | solution.py:76
  49.0 0.4 fusion.31
  49.5 0.1 pad_maximum_fusion
  49.5 0.0 copy-start.1
  49.6 2.0 %copy.67 = f32[8,2,128,148]{2,1,3,0:T(2,128)} copy(f32[8,2,128,148]{2,0,3,1:T(8,128)S(1)} %pad_maximum_fusion) | data formatting | bytes 2424832 | tf_op jit(solution)/shard_map/stack | solution.py:78
  51.5 0.0 copy-start.4
  51.5 4.9 %all-to-all-start.1 = ((f32[8,2,128,148]{2,1,3,0:T(2,128)}), f32[8,2,128,148]{2,1,3,0:T(2,128)S(1)}, u32[]{:S(2)}, u32[]{:S(2)}) async-start(f32[8,2,128,148]{2,1,3,0:T(2,128)} %copy.67), calls=%async_computation.1 | async-start | bytes 2424832 | tf_op jit(solution)/shard_map/all_to_all | solution.py:79
  56.5 0.0 copy-done.1
  56.5 0.3 copy.70
  56.8 0.0 copy-done.4
  56.8 0.1 constant_dynamic-slice_fusion
  56.9 0.6 fusion.69
  58.8 0.6 fusion.59
  59.4 14.7 %all-to-all-done.1 = f32[8,2,128,148]{2,1,3,0:T(2,128)S(1)} async-done(((f32[8,2,128,148]{2,1,3,0:T(2,128)}), f32[8,2,128,148]{2,1,3,0:T(2,128)S(1)}, u32[]{:S(2)}, u32[]{:S(2)}) %all-to-all-start.1) | async-done | bytes 1212448 | tf_op jit(solution)/shard_map/all_to_all | solution.py:79
  74.2 0.2 copy.111
  74.4 0.1 slice.154
  74.5 0.3 copy.69
  74.9 0.4 fusion.19
  75.3 1.3 %copy.71 = f32[1,128,2048]{2,1,0:T(8,128)} copy(f32[1,128,2048]{1,2,0:T(8,128)S(1)} %fusion.19) | data formatting | bytes 2097152 | tf_op jit(solution)/shard_map/jit(_where)/select_n | solution.py:95
  (9 shorter events, 0.1 us)
Async XLA Ops:
  0.0 32.3 %copy-start = (f32[16,21]{1,0:T(8,128)S(1)}, f32[16,21]{1,0:T(8,128)}, u32[]{:S(2)}) copy-start(f32[16,21]{1,0:T(8,128)} %param.12) | copy-start | bytes 4036
  0.0 34.2 %copy-start.3 = (f32[16,21]{1,0:T(8,128)S(1)}, f32[16,21]{1,0:T(8,128)}, u32[]{:S(2)}) copy-start(f32[16,21]{1,0:T(8,128)} %param.11) | copy-start | bytes 4036
  0.7 36.1 %collective-permute-start.4 = (f32[10,128]{1,0:T(8,128)S(1)}, f32[10,128]{1,0:T(8,128)S(1)}, u32[]{:S(2)}, u32[]{:S(2)}) collective-permute-start(f32[10,128]{1,0:T(8,128)S(1)} %get-tuple-element.36), channel_id=1, source_target_pairs={{16,8},{24,0},{32,24},{40,16},{48,40},{56,32},{64,56},{72,48},{80,... | collective-permute-start | bytes 15368 | tf_op jit(solution)/shard_map/ppermute | solution.py:62
  9.7 27.1 %collective-permute-start.1 = (f32[10,128]{1,0:T(8,128)S(1)}, f32[10,128]{1,0:T(8,128)S(1)}, u32[]{:S(2)}, u32[]{:S(2)}) collective-permute-start(f32[10,128]{1,0:T(8,128)S(1)} %get-tuple-element.36), channel_id=1, source_target_pairs={{16,0},{32,16},{48,32},{64,48},{80,64},{96,80},{112,96},{128,112},... | collective-permute-start | bytes 15368 | tf_op jit(solution)/shard_map/ppermute | solution.py:56
  12.1 24.8 %collective-permute-start = (f32[10,128]{1,0:T(8,128)S(1)}, f32[10,128]{1,0:T(8,128)S(1)}, u32[]{:S(2)}, u32[]{:S(2)}) collective-permute-start(f32[10,128]{1,0:T(8,128)S(1)} %get-tuple-element.35), channel_id=1, source_target_pairs={{0,16},{16,32},{32,48},{48,64},{64,80},{80,96},{96,112},{112,128},... | collective-permute-start | bytes 15368 | tf_op jit(solution)/shard_map/ppermute | solution.py:55
  15.6 21.3 %collective-permute-start.2 = (f32[10,128]{1,0:T(8,128)S(1)}, f32[10,128]{1,0:T(8,128)S(1)}, u32[]{:S(2)}, u32[]{:S(2)}) collective-permute-start(f32[10,128]{1,0:T(8,128)S(1)} %get-tuple-element.35), channel_id=1, source_target_pairs={{0,24},{8,16},{16,40},{24,32},{32,56},{40,48},{48,72},{56,64},{64,... | collective-permute-start | bytes 15368 | tf_op jit(solution)/shard_map/ppermute | solution.py:61
  20.5 16.4 %collective-permute-start.3 = (f32[128,128]{1,0:T(8,128)}, f32[128,128]{1,0:T(8,128)S(1)}, u32[]{:S(2)}, u32[]{:S(2)}) collective-permute-start(f32[128,128]{1,0:T(8,128)} %param.10), channel_id=1, source_target_pairs={{0,8},{8,0},{1,9},{9,1},{2,10},{10,2},{3,11},{11,3},{4,12},{12,4},... | collective-permute-start | bytes 196616 | tf_op jit(solution)/shard_map/ppermute | solution.py:52
  28.0 17.3 %all-to-all-start = ((f32[8,16,6]{1,2,0:T(8,128)}), f32[8,16,6]{1,2,0:T(8,128)S(1)}, u32[]{:S(2)}, u32[]{:S(2)}) async-start(f32[8,16,6]{1,2,0:T(8,128)} %broadcast_in_dim.14), calls=%async_computation | async-start | bytes 65536 | tf_op jit(solution)/shard_map/all_to_all | solution.py:47
  32.4 4.5 %copy-start.2 = (f32[128,128]{1,0:T(8,128)S(1)}, f32[128,128]{1,0:T(8,128)}, u32[]{:S(2)}) copy-start(f32[128,128]{1,0:T(8,128)} %param.10) | copy-start | bytes 196612
  49.5 6.9 %copy-start.1 = (f32[1,128,2048]{2,1,0:T(8,128)S(1)}, f32[1,128,2048]{2,1,0:T(8,128)}, u32[]{:S(2)}) copy-start(f32[1,128,2048]{2,1,0:T(8,128)} %param.14) | copy-start | bytes 3145732
  51.5 5.3 %copy-start.4 = (s32[16,2]{0,1:T(2,128)S(1)}, s32[16,2]{0,1:T(2,128)}, u32[]{:S(2)}) copy-start(s32[16,2]{0,1:T(2,128)} %param.15) | copy-start | bytes 388
  51.5 22.6 %all-to-all-start.1 = ((f32[8,2,128,148]{2,1,3,0:T(2,128)}), f32[8,2,128,148]{2,1,3,0:T(2,128)S(1)}, u32[]{:S(2)}, u32[]{:S(2)}) async-start(f32[8,2,128,148]{2,1,3,0:T(2,128)} %copy.67), calls=%async_computation.1 | async-start | bytes 2424832 | tf_op jit(solution)/shard_map/all_to_all | solution.py:79

commit v6 on v5

--- a/solution.py
+++ b/solution.py
@@ -17,16 +17,18 @@
     )
 
 
-def banded(taps, rows, cols):
+def banded(row_taps, col_taps, rows, cols):
     offset = lax.broadcasted_iota(jnp.int32, (rows, cols), 1) - lax.broadcasted_iota(jnp.int32, (rows, cols), 0)
-    picks = (offset[None] == jnp.arange(taps.shape[1])[:, None, None]).astype(jnp.float32)
+    picks = (offset[None] == jnp.arange(row_taps.shape[1])[:, None, None]).astype(jnp.float32)
+    taps = jnp.concatenate([row_taps, col_taps], axis=0)
     return jnp.einsum("ka,arc->krc", taps, picks, precision=lax.Precision.HIGHEST)
 
 
 def separable(blocks, row_taps, col_taps, tile_rows, span):
-    reach = row_taps.shape[1]
-    down = banded(row_taps, tile_rows, tile_rows + reach - 1)
-    across = jnp.swapaxes(banded(col_taps, span, span + reach - 1), 1, 2)
+    kernels, reach = row_taps.shape
+    bands = banded(row_taps, col_taps, span, span + reach - 1)
+    down = bands[:kernels, :tile_rows, : tile_rows + reach - 1]
+    across = jnp.swapaxes(bands[kernels:], 1, 2)
     passed = jnp.einsum("kra,bac->bkrc", down, blocks, precision=lax.Precision.HIGH)
     return jnp.einsum("bkrc,kcd->bkrd", passed, across, precision=lax.Precision.HIGH)
 
@@ -48,20 +50,13 @@
 
     top = template[:half]
     bottom = template[tile_rows - half :]
-    swap = [(h, halves - 1 - h) for h in range(halves)]
-    partner = lax.ppermute(template, "zhi", swap)
     down = [(i, i + 1) for i in range(tiles - 1)]
     up = [(i + 1, i) for i in range(tiles - 1)]
     above = lax.ppermute(bottom, "tile", down)
     below = lax.ppermute(top, "tile", up)
-
-    def crossed(pairs):
-        return [(i * halves + h, j * halves + halves - 1 - h) for i, j in pairs for h in range(halves)]
-
-    partner_above = lax.ppermute(bottom, ("tile", "zhi"), crossed(down))
-    partner_below = lax.ppermute(top, ("tile", "zhi"), crossed(up))
     own = jnp.concatenate([above, template, below], axis=0)
-    other = jnp.concatenate([partner_above, partner, partner_below], axis=0)
+    swap = [(h, halves - 1 - h) for h in range(halves)]
+    other = lax.ppermute(own, "zhi", swap)
     first = side == 0
     blocks = jnp.stack([jnp.where(first, own, other), jnp.where(first, other, own)])
     blocks = jnp.pad(blocks, ((0, 0), (0, 0), (2 * half, 2 * half)))

time: 77 us -> 70.7 us (0.918)
  the two profiles are of different devices: /device:TPU:16 before, /device:TPU:32 now
where the time goes in v6:
time: 70.7 us; the launch traced here: 70.1 us
  starting transfers between devices  24.1 us (34%)
  waiting for transfers between devices  17.7 us (25%)
  matrix products  13.5 us (19%)
  local copies, waits for them, and re-layouts  11 us (16%)
  other arithmetic  2.15 us (3%)
  between operations  1.56 us (2%)
    all_to_all x1, waiting for transfers between devices, local(): parts = lax.all_to_all(models, 'xc', 0, 0, tiled=True)  14.8 us
    ppermute x1, starting transfers between devices, local(): other = lax.ppermute(own, 'zhi', swap)  6.56 us
    all_to_all x1, starting transfers between devices, local(): parts = lax.all_to_all(models, 'xc', 0, 0, tiled=True)  5.35 us
    dot_general x1, matrix products, separable(): jnp.einsum('kra,bac->bkrc', down, blocks, precision=lax.Precision.HIGH)  5.15 us
    ppermute x1, starting transfers between devices, local(): below = lax.ppermute(top, 'tile', up)  4.47 us
    all_to_all x1, starting transfers between devices, local(): half_coeffs = lax.all_to_all(copies, 'xc', 0, 0, tiled=True)  4.3 us
    ppermute x1, starting transfers between devices, local(): above = lax.ppermute(bottom, 'tile', down)  3.47 us
    dot_general x2, matrix products, local(): jnp.einsum('vkt,krc->tvrc', half_coeffs, basis[b], precision=lax.Precisio...  3.16 us
  transfers between devices with their start and end apart: 5, of which 2 were waited for; matrix products, arithmetic and copies ran while one was open for 24% of the time, Pallas kernels for 0%

profile of v6, /device:TPU:32, one launch (start us, length us, event | category | flops | bytes accessed | tf_op | source)
XLA Modules:
  0.0 70.1 jit_solution(8525453599282026869)
XLA Ops:
  0.0 0.0 copy-start
  0.0 0.7 %fusion.63 = (f32[10,128]{1,0:T(8,128)S(1)}, f32[10,128]{1,0:T(8,128)S(1)}) fusion(f32[128,128]{1,0:T(8,128)} %param.10), kind=kLoop, calls=%fused_computation.98 | loop fusion | bytes 20480 | tf_op jit(solution)/shard_map/slice | solution.py:52
  0.7 3.5 %collective-permute-start = (f32[10,128]{1,0:T(8,128)S(1)}, f32[10,128]{1,0:T(8,128)S(1)}, u32[]{:S(2)}, u32[]{:S(2)}) collective-permute-start(f32[10,128]{1,0:T(8,128)S(1)} %get-tuple-element.35), channel_id=1, source_target_pairs={{0,16},{16,32},{32,48},{48,64},{64,80},{80,96},{96,112},{112,128},... | collective-permute-start | bytes 15368 | tf_op jit(solution)/shard_map/ppermute | solution.py:55
  4.2 4.5 %collective-permute-start.1 = (f32[10,128]{1,0:T(8,128)S(1)}, f32[10,128]{1,0:T(8,128)S(1)}, u32[]{:S(2)}, u32[]{:S(2)}) collective-permute-start(f32[10,128]{1,0:T(8,128)S(1)} %get-tuple-element.36), channel_id=1, source_target_pairs={{16,0},{32,16},{48,32},{64,48},{80,64},{96,80},{112,96},{128,112},... | collective-permute-start | bytes 15368 | tf_op jit(solution)/shard_map/ppermute | solution.py:56
  8.7 0.7 copy.124
  9.4 0.6 broadcast_in_dim.14
  10.0 4.3 %all-to-all-start = ((f32[8,16,6]{1,2,0:T(8,128)}), f32[8,16,6]{1,2,0:T(8,128)S(1)}, u32[]{:S(2)}, u32[]{:S(2)}) async-start(f32[8,16,6]{1,2,0:T(8,128)} %broadcast_in_dim.14), calls=%async_computation | async-start | bytes 65536 | tf_op jit(solution)/shard_map/all_to_all | solution.py:49
  14.3 0.8 %copy.65 = f32[16,21]{0,1:T(8,128)S(1)} copy(f32[16,21]{1,0:T(8,128)} %param.11) | data formatting | bytes 2688 | tf_op args[1]
  15.1 0.8 %copy.66 = f32[16,21]{0,1:T(8,128)S(1)} copy(f32[16,21]{1,0:T(8,128)} %param.12) | data formatting | bytes 2688 | tf_op args[2]
  15.9 2.2 %fusion = f32[32,148,168]{2,0,1:T(8,128)S(1)} fusion(s32[148,168]{1,0:T(8,128)S(1)} %iota_subtract_fusion, f32[16,21]{0,1:T(8,128)S(1)} %copy.66, f32[16,21]{0,1:T(8,128)S(1)} %copy.65), kind=kOutput, calls=%fused_computation.1 | convolution fusion | flops 201026112 | bytes 3284736 | tf_op jit(solution)/shard_map/ka,arc->krc/dot_general | solution.py:24
  18.1 1.5 %slice_bitcast_fusion.1 = f32[16,128,148,1]{2,0,1,3:T(8,128)} fusion(f32[32,148,168]{2,0,1:T(8,128)S(1)} %fusion), kind=kLoop, calls=%fused_computation.6 | loop fusion | bytes 2424832 | tf_op jit(solution)/shard_map/slice | solution.py:30
  19.6 0.0 copy-start.2
  19.7 0.2 slice_bitcast_fusion
  20.0 0.0 collective-permute-done
  20.0 0.0 collective-permute-done.1
  20.0 0.5 copy-done.2
  20.5 6.6 %collective-permute-start.2 = (f32[148,128]{1,0:T(8,128)S(1)}, f32[148,128]{1,0:T(8,128)S(1)}, u32[]{:S(2)}, u32[]{:S(2)}) collective-permute-start(f32[148,128]{1,0:T(8,128)S(1)} %pad_maximum_fusion.1), channel_id=1, source_target_pairs={{0,8},{8,0},{1,9},{9,1},{2,10},{10,2},{3,11},{11,3},{4,12},{12,4},... | collective-permute-start | bytes 227336 | tf_op jit(solution)/shard_map/ppermute | solution.py:59
  27.1 0.1 broadcast_multiply_fusion.1
  27.2 3.0 %collective-permute-done.2 = f32[148,128]{1,0:T(8,128)S(1)} collective-permute-done((f32[148,128]{1,0:T(8,128)S(1)}, f32[148,128]{1,0:T(8,128)S(1)}, u32[]{:S(2)}, u32[]{:S(2)}) %collective-permute-start.2) | collective-permute-done | bytes 75808 | tf_op jit(solution)/shard_map/ppermute | solution.py:59
  30.2 5.2 %fusion.4 = f32[2,168,16,128]{3,1,0,2:T(8,128)S(1)} fusion(f32[16,128,148,1]{2,0,1,3:T(8,128)} %slice_bitcast_fusion.1, f32[1,148,128]{2,1,0:T(8,128)S(1)} %get-tuple-element.34, f32[1,148,128]{2,1,0:T(8,128)S(1)} %get-tuple-element.33), kind=kOutput, calls=%fused_computation.7 | convolution fusion | flops 611356032 | bytes 4116480 | tf_op jit(solution)/shard_map/kra,bac->bkrc/dot_general | solution.py:32
  35.3 3.0 %fusion.7 = f32[2,16,128,148]{2,3,0,1:T(8,128)S(1)} fusion(f32[2,168,16,128]{3,1,0,2:T(8,128)S(1)} %fusion.4, f32[16,148,168,1]{2,0,1,3:T(8,128)S(1)} %slice_bitcast_fusion), kind=kOutput, calls=%fused_computation.12 | convolution fusion | flops 611057664 | bytes 6768640 | tf_op jit(solution)/shard_map/bkrc,kcd->bkrd/dot_general | solution.py:33
  38.3 0.2 slice_bitcast_fusion.3
  38.5 0.0 all-to-all-done
  38.5 1.6 %convolution_bitcast_fusion = f32[6,8,128,148]{2,1,3,0:T(8,128)S(1)} fusion(f32[16,128,148]{1,2,0:T(8,128)S(1)} %get-tuple-element.30, f32[8,16,6,1]{1,2,0,3:T(8,128)S(1)} %bitcast.151), kind=kOutput, calls=%fused_computation.9 | convolution fusion | flops 87293952 | bytes 4852736 | tf_op jit(solution)/shard_map/vkt,krc->tvrc/dot_general | solution.py:71
  40.1 1.6 %convolution_bitcast_fusion.1 = f32[6,8,128,148]{2,1,0,3:T(8,128)S(1)} fusion(f32[16,128,148,1]{1,2,0,3:T(8,128)S(1)} %get-tuple-element.29, f32[8,16,6]{1,2,0:T(8,128)S(1)} %all-to-all-done), kind=kOutput, calls=%fused_computation.10 | convolution fusion | flops 87293952 | bytes 4852736 | tf_op jit(solution)/shard_map/vkt,krc->tvrc/dot_general | solution.py:71
  41.7 0.4 fusion.27
  42.1 0.4 fusion.17
  42.5 0.1 pad_maximum_fusion
  42.6 0.0 copy-start.1
  42.6 2.0 %copy.79 = f32[8,2,128,148]{2,1,3,0:T(2,128)} copy(f32[8,2,128,148]{2,0,3,1:T(8,128)S(1)} %pad_maximum_fusion) | data formatting | bytes 2424832 | tf_op jit(solution)/shard_map/stack | solution.py:73
  44.6 5.3 %all-to-all-start.1 = ((f32[8,2,128,148]{2,1,3,0:T(2,128)}), f32[8,2,128,148]{2,1,3,0:T(2,128)S(1)}, u32[]{:S(2)}, u32[]{:S(2)}) async-start(f32[8,2,128,148]{2,1,3,0:T(2,128)} %copy.79), calls=%async_computation.1 | async-start | bytes 2424832 | tf_op jit(solution)/shard_map/all_to_all | solution.py:74
  50.0 0.0 copy-done.1
  50.0 0.3 copy.82
  50.3 0.0 copy-done
  50.3 0.1 constant_dynamic-slice_fusion
  50.4 0.5 fusion.64
  52.2 0.6 fusion.53
  52.9 14.8 %all-to-all-done.1 = f32[8,2,128,148]{2,1,3,0:T(2,128)S(1)} async-done(((f32[8,2,128,148]{2,1,3,0:T(2,128)}), f32[8,2,128,148]{2,1,3,0:T(2,128)S(1)}, u32[]{:S(2)}, u32[]{:S(2)}) %all-to-all-start.1) | async-done | bytes 1212448 | tf_op jit(solution)/shard_map/all_to_all | solution.py:74
  67.7 0.2 copy.123
  67.9 0.1 slice.164
  68.1 0.3 copy.81
  68.4 0.4 fusion.15
  68.8 1.3 %copy.83 = f32[1,128,2048]{2,1,0:T(8,128)} copy(f32[1,128,2048]{1,2,0:T(8,128)S(1)} %fusion.15) | data formatting | bytes 2097152 | tf_op jit(solution)/shard_map/jit(_where)/select_n | solution.py:90
  (9 shorter events, 0.1 us)
Async XLA Ops:
  0.0 50.3 %copy-start = (s32[16,2]{0,1:T(2,128)S(1)}, s32[16,2]{0,1:T(2,128)}, u32[]{:S(2)}) copy-start(s32[16,2]{0,1:T(2,128)} %param.15) | copy-start | bytes 388
  0.7 19.2 %collective-permute-start = (f32[10,128]{1,0:T(8,128)S(1)}, f32[10,128]{1,0:T(8,128)S(1)}, u32[]{:S(2)}, u32[]{:S(2)}) collective-permute-start(f32[10,128]{1,0:T(8,128)S(1)} %get-tuple-element.35), channel_id=1, source_target_pairs={{0,16},{16,32},{32,48},{48,64},{64,80},{80,96},{96,112},{112,128},... | collective-permute-start | bytes 15368 | tf_op jit(solution)/shard_map/ppermute | solution.py:55
  4.2 15.8 %collective-permute-start.1 = (f32[10,128]{1,0:T(8,128)S(1)}, f32[10,128]{1,0:T(8,128)S(1)}, u32[]{:S(2)}, u32[]{:S(2)}) collective-permute-start(f32[10,128]{1,0:T(8,128)S(1)} %get-tuple-element.36), channel_id=1, source_target_pairs={{16,0},{32,16},{48,32},{64,48},{80,64},{96,80},{112,96},{128,112},... | collective-permute-start | bytes 15368 | tf_op jit(solution)/shard_map/ppermute | solution.py:56
  10.0 28.5 %all-to-all-start = ((f32[8,16,6]{1,2,0:T(8,128)}), f32[8,16,6]{1,2,0:T(8,128)S(1)}, u32[]{:S(2)}, u32[]{:S(2)}) async-start(f32[8,16,6]{1,2,0:T(8,128)} %broadcast_in_dim.14), calls=%async_computation | async-start | bytes 65536 | tf_op jit(solution)/shard_map/all_to_all | solution.py:49
  19.6 0.8 %copy-start.2 = (f32[128,128]{1,0:T(8,128)S(1)}, f32[128,128]{1,0:T(8,128)}, u32[]{:S(2)}) copy-start(f32[128,128]{1,0:T(8,128)} %param.10) | copy-start | bytes 196612
  20.5 9.6 %collective-permute-start.2 = (f32[148,128]{1,0:T(8,128)S(1)}, f32[148,128]{1,0:T(8,128)S(1)}, u32[]{:S(2)}, u32[]{:S(2)}) collective-permute-start(f32[148,128]{1,0:T(8,128)S(1)} %pad_maximum_fusion.1), channel_id=1, source_target_pairs={{0,8},{8,0},{1,9},{9,1},{2,10},{10,2},{3,11},{11,3},{4,12},{12,4},... | collective-permute-start | bytes 227336 | tf_op jit(solution)/shard_map/ppermute | solution.py:59
  42.6 7.4 %copy-start.1 = (f32[1,128,2048]{2,1,0:T(8,128)S(1)}, f32[1,128,2048]{2,1,0:T(8,128)}, u32[]{:S(2)}) copy-start(f32[1,128,2048]{2,1,0:T(8,128)} %param.14) | copy-start | bytes 3145732
  44.6 23.0 %all-to-all-start.1 = ((f32[8,2,128,148]{2,1,3,0:T(2,128)}), f32[8,2,128,148]{2,1,3,0:T(2,128)S(1)}, u32[]{:S(2)}, u32[]{:S(2)}) async-start(f32[8,2,128,148]{2,1,3,0:T(2,128)} %copy.79), calls=%async_computation.1 | async-start | bytes 2424832 | tf_op jit(solution)/shard_map/all_to_all | solution.py:74

commit v7 on v6

--- a/solution.py
+++ b/solution.py
@@ -24,13 +24,9 @@
     return jnp.einsum("ka,arc->krc", taps, picks, precision=lax.Precision.HIGHEST)
 
 
-def separable(blocks, row_taps, col_taps, tile_rows, span):
-    kernels, reach = row_taps.shape
-    bands = banded(row_taps, col_taps, span, span + reach - 1)
-    down = bands[:kernels, :tile_rows, : tile_rows + reach - 1]
-    across = jnp.swapaxes(bands[kernels:], 1, 2)
-    passed = jnp.einsum("kra,bac->bkrc", down, blocks, precision=lax.Precision.HIGH)
-    return jnp.einsum("bkrc,kcd->bkrd", passed, across, precision=lax.Precision.HIGH)
+def separable(block, down, across):
+    passed = jnp.einsum("kra,ac->krc", down, block, precision=lax.Precision.HIGH)
+    return jnp.einsum("krc,kcd->krd", passed, across, precision=lax.Precision.HIGH)
 
 
 def local(template, row_taps, col_taps, coeffs, visits, boxes):
@@ -58,20 +54,25 @@
     swap = [(h, halves - 1 - h) for h in range(halves)]
     other = lax.ppermute(own, "zhi", swap)
     first = side == 0
-    blocks = jnp.stack([jnp.where(first, own, other), jnp.where(first, other, own)])
-    blocks = jnp.pad(blocks, ((0, 0), (0, 0), (2 * half, 2 * half)))
     span = columns + 2 * half
     y_coord = coordinate(tile * tile_rows, tile_rows, total_rows)
-    basis = separable(blocks, row_taps, col_taps, tile_rows, span)
+    kernels, reach = row_taps.shape
+    bands = banded(row_taps, col_taps, span, span + reach - 1)
+    down = bands[:kernels, :tile_rows, : tile_rows + reach - 1]
+    across = jnp.swapaxes(bands[kernels:], 1, 2)
     models = []
     y = y_coord[:, None]
-    for b in range(halves):
-        start = (b * group + place) * columns - half
+    for b, block in enumerate((own, other)):
+        block = jnp.pad(block, ((0, 0), (2 * half, 2 * half)))
+        basis = separable(block, down, across)
+        source = side if b == 0 else halves - 1 - side
+        start = (source * group + place) * columns - half
         x = coordinate(start, span, full_width)[None, :]
-        w = jnp.einsum("vkt,krc->tvrc", half_coeffs, basis[b], precision=lax.Precision.HIGH)
+        w = jnp.einsum("vkt,krc->tvrc", half_coeffs, basis, precision=lax.Precision.HIGH)
         models.append(w[0] + x * w[1] + y * w[2] + (x * x) * w[3] + (x * y) * w[4] + (y * y) * w[5])
     models = jnp.stack(models, axis=1)
     parts = lax.all_to_all(models, "xc", 0, 0, tiled=True)
+    parts = jnp.where(first, parts, parts[:, ::-1])
     parts = jnp.swapaxes(parts, 0, 1).reshape((halves * group,) + parts.shape[2:])
     core = parts[:, :, half : half + columns]
     left = parts[:, :, :half]

time: 70.7 us -> 72.8 us (1.030)
  local copies, waits for them, and re-layouts: 11 us -> 14 us
  waiting for transfers between devices: 17.7 us -> 14.8 us
  matrix products: 13.5 us -> 15.9 us
    ppermute x1, waiting for transfers between devices: 2.96 us -> 0.01 us  [local(): other = lax.ppermute(own, 'zhi', swap)]
    slice x2 -> x3, local copies, waits for them, and re-layouts: 1.79 us -> 4.6 us  [the longest x2 4.36 us: local(): down = bands[:kernels, :tile_rows, :tile_rows + reach - 1]]
    dot_general x4 -> x6, matrix products: 11.3 us -> 13.7 us  [the longest x2 6.19 us: separable(): jnp.einsum('krc,kcd->krd', passed, across, precision=lax.Precision.HIGH)]
    unnamed x10 -> x12, local copies, waits for them, and re-layouts: 3.09 us -> 3.44 us
  transfers between devices with their start and end apart: 5 -> 5, of which waited for: 2 -> 1; matrix products, arithmetic and copies ran while one was open for 24% -> 28% of each run, Pallas kernels for 0% -> 0%
where the time goes in v7:
time: 72.8 us; the launch traced here: 72.2 us
  starting transfers between devices  23.7 us (33%)
  matrix products  15.9 us (22%)
  waiting for transfers between devices  14.8 us (20%)
  local copies, waits for them, and re-layouts  14 us (19%)
  other arithmetic  2.24 us (3%)
  between operations  1.55 us (2%)
    all_to_all x1, waiting for transfers between devices, local(): parts = lax.all_to_all(models, 'xc', 0, 0, tiled=True)  14.8 us
    ppermute x1, starting transfers between devices, local(): other = lax.ppermute(own, 'zhi', swap)  6.56 us
    dot_general x2, matrix products, separable(): jnp.einsum('krc,kcd->krd', passed, across, precision=lax.Precision.HIGH)  6.19 us
    all_to_all x1, starting transfers between devices, local(): parts = lax.all_to_all(models, 'xc', 0, 0, tiled=True)  4.93 us
    ppermute x1, starting transfers between devices, local(): below = lax.ppermute(top, 'tile', up)  4.47 us
    dot_general x2, matrix products, local(): jnp.einsum('vkt,krc->tvrc', half_coeffs, basis, precision=lax.Precision.H...  4.44 us
    slice x2, local copies, waits for them, and re-layouts, local(): down = bands[:kernels, :tile_rows, :tile_rows + reach - 1]  4.36 us
    all_to_all x1, starting transfers between devices, local(): half_coeffs = lax.all_to_all(copies, 'xc', 0, 0, tiled=True)  4.3 us
  transfers between devices with their start and end apart: 5, of which 1 were waited for; matrix products, arithmetic and copies ran while one was open for 28% of the time, Pallas kernels for 0%

profile of v7, /device:TPU:32, one launch (start us, length us, event | category | flops | bytes accessed | tf_op | source)
XLA Modules:
  0.0 72.2 jit_solution(10523967747320422782)
XLA Ops:
  0.0 0.0 copy-start
  0.0 0.7 %fusion.55 = (f32[10,128]{1,0:T(8,128)S(1)}, f32[10,128]{1,0:T(8,128)S(1)}) fusion(f32[128,128]{1,0:T(8,128)} %param.10), kind=kLoop, calls=%fused_computation.85 | loop fusion | bytes 20480 | tf_op jit(solution)/shard_map/slice | solution.py:48
  0.7 3.5 %collective-permute-start = (f32[10,128]{1,0:T(8,128)S(1)}, f32[10,128]{1,0:T(8,128)S(1)}, u32[]{:S(2)}, u32[]{:S(2)}) collective-permute-start(f32[10,128]{1,0:T(8,128)S(1)} %get-tuple-element.31), channel_id=1, source_target_pairs={{0,16},{16,32},{32,48},{48,64},{64,80},{80,96},{96,112},{112,128},... | collective-permute-start | bytes 15368 | tf_op jit(solution)/shard_map/ppermute | solution.py:51
  4.2 4.5 %collective-permute-start.1 = (f32[10,128]{1,0:T(8,128)S(1)}, f32[10,128]{1,0:T(8,128)S(1)}, u32[]{:S(2)}, u32[]{:S(2)}) collective-permute-start(f32[10,128]{1,0:T(8,128)S(1)} %get-tuple-element.32), channel_id=1, source_target_pairs={{16,0},{32,16},{48,32},{64,48},{80,64},{96,80},{112,96},{128,112},... | collective-permute-start | bytes 15368 | tf_op jit(solution)/shard_map/ppermute | solution.py:52
  8.7 0.7 copy.118
  9.4 0.6 broadcast_in_dim.14
  10.0 4.3 %all-to-all-start = ((f32[8,16,6]{1,2,0:T(8,128)}), f32[8,16,6]{1,2,0:T(8,128)S(1)}, u32[]{:S(2)}, u32[]{:S(2)}) async-start(f32[8,16,6]{1,2,0:T(8,128)} %broadcast_in_dim.14), calls=%async_computation | async-start | bytes 65536 | tf_op jit(solution)/shard_map/all_to_all | solution.py:45
  14.4 0.8 %copy.64 = f32[16,21]{0,1:T(8,128)S(1)} copy(f32[16,21]{1,0:T(8,128)} %param.11) | data formatting | bytes 2688 | tf_op args[1]
  15.2 0.8 %copy.65 = f32[16,21]{0,1:T(8,128)S(1)} copy(f32[16,21]{1,0:T(8,128)} %param.12) | data formatting | bytes 2688 | tf_op args[2]
  15.9 2.2 %fusion = f32[32,148,168]{2,0,1:T(8,128)S(1)} fusion(s32[148,168]{1,0:T(8,128)S(1)} %iota_subtract_fusion, f32[16,21]{0,1:T(8,128)S(1)} %copy.65, f32[16,21]{0,1:T(8,128)S(1)} %copy.64), kind=kOutput, calls=%fused_computation.1 | convolution fusion | flops 201026112 | bytes 3284736 | tf_op jit(solution)/shard_map/ka,arc->krc/dot_general | solution.py:24
  18.2 0.1 broadcast_multiply_fusion.1
  18.3 1.5 %slice.140 = f32[16,128,148]{2,0,1:T(8,128)} slice(f32[32,148,168]{2,0,1:T(8,128)S(1)} %fusion), slice={[0:16], [0:128], [0:148]} | slice | bytes 2424832 | tf_op jit(solution)/shard_map/slice | solution.py:61
  19.8 0.2 slice.141
  20.1 0.0 copy-start.3
  20.1 2.8 %copy.66 = f32[16,128,148]{1,2,0:T(8,128)} copy(f32[16,128,148]{2,0,1:T(8,128)} %slice.140) | data formatting | bytes 2424832 | tf_op jit(solution)/shard_map/slice | solution.py:61
  22.9 0.0 collective-permute-done
  22.9 0.0 collective-permute-done.1
  22.9 0.0 copy-done.3
  22.9 6.6 %collective-permute-start.2 = (f32[148,128]{1,0:T(8,128)S(1)}, f32[148,128]{1,0:T(8,128)S(1)}, u32[]{:S(2)}, u32[]{:S(2)}) collective-permute-start(f32[148,128]{1,0:T(8,128)S(1)} %pad_maximum_fusion.1), channel_id=1, source_target_pairs={{0,8},{8,0},{1,9},{9,1},{2,10},{10,2},{3,11},{11,3},{4,12},{12,4},... | collective-permute-start | bytes 227336 | tf_op jit(solution)/shard_map/ppermute | solution.py:55
  29.5 2.2 %fusion.36 = f32[16,128,168]{1,2,0:T(8,128)S(1)} fusion(f32[16,128,148]{1,2,0:T(8,128)} %copy.66, f32[148,128]{1,0:T(8,128)S(1)} %pad_maximum_fusion.1), kind=kOutput, calls=%fused_computation.52 | convolution fusion | flops 305528832 | bytes 2664448 | tf_op jit(solution)/shard_map/kra,ac->krc/dot_general | solution.py:28
  31.7 3.6 %fusion.6 = f32[16,128,148,1]{1,2,0,3:T(8,128)} fusion(f32[16,128,168]{1,2,0:T(8,128)S(1)} %fusion.36, f32[16,148,168]{2,0,1:T(8,128)S(1)} %slice.141), kind=kOutput, calls=%fused_computation.10 | convolution fusion | flops 305528832 | bytes 4179968 | tf_op jit(solution)/shard_map/krc,kcd->krd/dot_general | solution.py:29
  35.3 0.0 all-to-all-done
  35.3 2.9 %convolution_bitcast_fusion.1 = f32[6,8,128,148]{2,1,0,3:T(8,128)S(1)} fusion(f32[16,128,148,1]{1,2,0,3:T(8,128)} %fusion.6, f32[8,16,6]{1,2,0:T(8,128)S(1)} %all-to-all-done), kind=kOutput, calls=%fused_computation.7 | convolution fusion | flops 87293952 | bytes 4852736 | tf_op jit(solution)/shard_map/vkt,krc->tvrc/dot_general | solution.py:71
  38.1 0.0 copy-start.1
  38.2 0.4 fusion.25
  38.6 0.0 collective-permute-done.2
  38.6 0.8 %copy-done.1 = f32[16,128,148]{1,2,0:T(8,128)S(1)} copy-done((f32[16,128,148]{1,2,0:T(8,128)S(1)}, f32[16,128,148]{1,2,0:T(8,128)}, u32[]{:S(2)}) %copy-start.1) | copy-done | bytes 1212440
  39.4 0.9 %fusion.34 = f32[16,128,168]{1,2,0:T(8,128)S(1)} fusion(f32[16,128,148]{1,2,0:T(8,128)S(1)} %copy-done.1, f32[148,128]{1,0:T(8,128)S(1)} %collective-permute-done.2), kind=kOutput, calls=%fused_computation.50 | convolution fusion | flops 305528832 | bytes 2664448 | tf_op jit(solution)/shard_map/kra,ac->krc/dot_general | solution.py:28
  40.3 2.6 %fusion.1 = f32[16,128,148]{1,2,0:T(8,128)S(1)} fusion(f32[16,128,168]{1,2,0:T(8,128)S(1)} %fusion.34, f32[16,148,168]{2,0,1:T(8,128)S(1)} %slice.141), kind=kOutput, calls=%fused_computation.2 | convolution fusion | flops 305528832 | bytes 4179968 | tf_op jit(solution)/shard_map/krc,kcd->krd/dot_general | solution.py:29
  42.9 1.6 %convolution_bitcast_fusion = f32[6,8,128,148]{2,1,3,0:T(8,128)S(1)} fusion(f32[16,128,148]{1,2,0:T(8,128)S(1)} %fusion.1, f32[8,16,6,1]{1,2,0,3:T(8,128)S(1)} %bitcast.135), kind=kOutput, calls=%fused_computation.6 | convolution fusion | flops 87293952 | bytes 4852736 | tf_op jit(solution)/shard_map/vkt,krc->tvrc/dot_general | solution.py:71
  44.5 0.4 fusion.15
  44.9 0.1 pad_maximum_fusion
  45.0 2.0 %copy.80 = f32[8,2,128,148]{2,1,3,0:T(2,128)} copy(f32[8,2,128,148]{2,0,3,1:T(8,128)S(1)} %pad_maximum_fusion) | data formatting | bytes 2424832 | tf_op jit(solution)/shard_map/stack | solution.py:73
  47.0 0.0 copy-start.2
  47.0 4.9 %all-to-all-start.1 = ((f32[8,2,128,148]{2,1,3,0:T(2,128)}), f32[8,2,128,148]{2,1,3,0:T(2,128)S(1)}, u32[]{:S(2)}, u32[]{:S(2)}) async-start(f32[8,2,128,148]{2,1,3,0:T(2,128)} %copy.80), calls=%async_computation.1 | async-start | bytes 2424832 | tf_op jit(solution)/shard_map/all_to_all | solution.py:74
  52.0 0.0 copy-done.2
  52.0 0.3 copy.84
  52.3 0.0 copy-done
  52.3 0.1 constant_dynamic-slice_fusion
  52.4 0.6 fusion.56
  54.2 0.6 fusion.47
  54.9 14.8 %all-to-all-done.1 = f32[8,2,128,148]{2,1,3,0:T(2,128)S(1)} async-done(((f32[8,2,128,148]{2,1,3,0:T(2,128)}), f32[8,2,128,148]{2,1,3,0:T(2,128)S(1)}, u32[]{:S(2)}, u32[]{:S(2)}) %all-to-all-start.1) | async-done | bytes 1212448 | tf_op jit(solution)/shard_map/all_to_all | solution.py:74
  69.7 0.2 copy.82
  69.9 0.1 fusion.9
  70.0 0.1 slice.154
  70.2 0.3 copy.83
  70.5 0.4 fusion.13
  70.9 1.3 %copy.85 = f32[1,128,2048]{2,1,0:T(8,128)} copy(f32[1,128,2048]{1,2,0:T(8,128)S(1)} %fusion.13) | data formatting | bytes 2097152 | tf_op jit(solution)/shard_map/jit(_where)/select_n | solution.py:91
  (8 shorter events, 0.1 us)
Async XLA Ops:
  0.0 52.3 %copy-start = (s32[16,2]{0,1:T(2,128)S(1)}, s32[16,2]{0,1:T(2,128)}, u32[]{:S(2)}) copy-start(s32[16,2]{0,1:T(2,128)} %param.15) | copy-start | bytes 388
  0.7 22.2 %collective-permute-start = (f32[10,128]{1,0:T(8,128)S(1)}, f32[10,128]{1,0:T(8,128)S(1)}, u32[]{:S(2)}, u32[]{:S(2)}) collective-permute-start(f32[10,128]{1,0:T(8,128)S(1)} %get-tuple-element.31), channel_id=1, source_target_pairs={{0,16},{16,32},{32,48},{48,64},{64,80},{80,96},{96,112},{112,128},... | collective-permute-start | bytes 15368 | tf_op jit(solution)/shard_map/ppermute | solution.py:51
  4.2 18.7 %collective-permute-start.1 = (f32[10,128]{1,0:T(8,128)S(1)}, f32[10,128]{1,0:T(8,128)S(1)}, u32[]{:S(2)}, u32[]{:S(2)}) collective-permute-start(f32[10,128]{1,0:T(8,128)S(1)} %get-tuple-element.32), channel_id=1, source_target_pairs={{16,0},{32,16},{48,32},{64,48},{80,64},{96,80},{112,96},{128,112},... | collective-permute-start | bytes 15368 | tf_op jit(solution)/shard_map/ppermute | solution.py:52
  10.0 25.3 %all-to-all-start = ((f32[8,16,6]{1,2,0:T(8,128)}), f32[8,16,6]{1,2,0:T(8,128)S(1)}, u32[]{:S(2)}, u32[]{:S(2)}) async-start(f32[8,16,6]{1,2,0:T(8,128)} %broadcast_in_dim.14), calls=%async_computation | async-start | bytes 65536 | tf_op jit(solution)/shard_map/all_to_all | solution.py:45
  20.1 2.8 %copy-start.3 = (f32[128,128]{1,0:T(8,128)S(1)}, f32[128,128]{1,0:T(8,128)}, u32[]{:S(2)}) copy-start(f32[128,128]{1,0:T(8,128)} %param.10) | copy-start | bytes 196612
  22.9 15.7 %collective-permute-start.2 = (f32[148,128]{1,0:T(8,128)S(1)}, f32[148,128]{1,0:T(8,128)S(1)}, u32[]{:S(2)}, u32[]{:S(2)}) collective-permute-start(f32[148,128]{1,0:T(8,128)S(1)} %pad_maximum_fusion.1), channel_id=1, source_target_pairs={{0,8},{8,0},{1,9},{9,1},{2,10},{10,2},{3,11},{11,3},{4,12},{12,4},... | collective-permute-start | bytes 227336 | tf_op jit(solution)/shard_map/ppermute | solution.py:55
  38.1 1.3 %copy-start.1 = (f32[16,128,148]{1,2,0:T(8,128)S(1)}, f32[16,128,148]{1,2,0:T(8,128)}, u32[]{:S(2)}) copy-start(f32[16,128,148]{1,2,0:T(8,128)} %copy.66) | copy-start | bytes 3637252
  47.0 4.9 %copy-start.2 = (f32[1,128,2048]{2,1,0:T(8,128)S(1)}, f32[1,128,2048]{2,1,0:T(8,128)}, u32[]{:S(2)}) copy-start(f32[1,128,2048]{2,1,0:T(8,128)} %param.14) | copy-start | bytes 3145732
  47.0 22.6 %all-to-all-start.1 = ((f32[8,2,128,148]{2,1,3,0:T(2,128)}), f32[8,2,128,148]{2,1,3,0:T(2,128)S(1)}, u32[]{:S(2)}, u32[]{:S(2)}) async-start(f32[8,2,128,148]{2,1,3,0:T(2,128)} %copy.80), calls=%async_computation.1 | async-start | bytes 2424832 | tf_op jit(solution)/shard_map/all_to_all | solution.py:74

commit v8 on v6

--- a/solution.py
+++ b/solution.py
@@ -48,15 +48,15 @@
     copies = jnp.broadcast_to(coeffs, (group,) + coeffs.shape[1:])
     half_coeffs = lax.all_to_all(copies, "xc", 0, 0, tiled=True)
 
-    top = template[:half]
-    bottom = template[tile_rows - half :]
+    swap = [(h, halves - 1 - h) for h in range(halves)]
+    pair = jnp.stack([template, lax.ppermute(template, "zhi", swap)])
     down = [(i, i + 1) for i in range(tiles - 1)]
     up = [(i + 1, i) for i in range(tiles - 1)]
-    above = lax.ppermute(bottom, "tile", down)
-    below = lax.ppermute(top, "tile", up)
-    own = jnp.concatenate([above, template, below], axis=0)
-    swap = [(h, halves - 1 - h) for h in range(halves)]
-    other = lax.ppermute(own, "zhi", swap)
+    above = lax.ppermute(pair[:, tile_rows - half :], "tile", down)
+    below = lax.ppermute(pair[:, :half], "tile", up)
+    extended = jnp.concatenate([above, pair, below], axis=1)
+    own = extended[0]
+    other = extended[1]
     first = side == 0
     blocks = jnp.stack([jnp.where(first, own, other), jnp.where(first, other, own)])
     blocks = jnp.pad(blocks, ((0, 0), (0, 0), (2 * half, 2 * half)))

time: 70.7 us -> 69.2 us (0.979)
  the two profiles are of different devices: /device:TPU:32 before, /device:TPU:24 now
where the time goes in v8:
time: 69.2 us; the launch traced here: 68.8 us
  starting transfers between devices  22.3 us (32%)
  waiting for transfers between devices  19 us (27%)
  matrix products  13.5 us (20%)
  local copies, waits for them, and re-layouts  10.3 us (15%)
  other arithmetic  2.17 us (3%)
  between operations  1.56 us (2%)
    all_to_all x1, waiting for transfers between devices, local(): parts = lax.all_to_all(models, 'xc', 0, 0, tiled=True)  14.8 us
    ppermute x1, starting transfers between devices, local(): pair = jnp.stack([template, lax.ppermute(template, 'zhi', swap)])  7.19 us
    dot_general x1, matrix products, separable(): jnp.einsum('kra,bac->bkrc', down, blocks, precision=lax.Precision.HIGH)  5.15 us
    all_to_all x1, starting transfers between devices, local(): parts = lax.all_to_all(models, 'xc', 0, 0, tiled=True)  4.8 us
    all_to_all x1, starting transfers between devices, local(): half_coeffs = lax.all_to_all(copies, 'xc', 0, 0, tiled=True)  4.3 us
    ppermute x1, waiting for transfers between devices, local(): below = lax.ppermute(pair[:, :half], 'tile', up)  4.17 us
    ppermute x1, starting transfers between devices, local(): below = lax.ppermute(pair[:, :half], 'tile', up)  3.44 us
    dot_general x2, matrix products, local(): jnp.einsum('vkt,krc->tvrc', half_coeffs, basis[b], precision=lax.Precisio...  3.16 us
  transfers between devices with their start and end apart: 5, of which 2 were waited for; matrix products, arithmetic and copies ran while one was open for 25% of the time, Pallas kernels for 0%

profile of v8, /device:TPU:24, one launch (start us, length us, event | category | flops | bytes accessed | tf_op | source)
XLA Modules:
  0.0 68.8 jit_solution(2811940115406928276)
XLA Ops:
  0.0 0.0 copy-start
  0.0 7.2 %collective-permute-start = (f32[128,128]{1,0:T(8,128)}, f32[128,128]{1,0:T(8,128)S(1)}, u32[]{:S(2)}, u32[]{:S(2)}) collective-permute-start(f32[128,128]{1,0:T(8,128)} %param.10), channel_id=1, source_target_pairs={{0,8},{8,0},{1,9},{9,1},{2,10},{10,2},{3,11},{11,3},{4,12},{12,4},... | collective-permute-start | bytes 196616 | tf_op jit(solution)/shard_map/ppermute | solution.py:52
  7.2 0.7 copy.124
  7.9 0.6 broadcast_in_dim.14
  8.5 4.3 %all-to-all-start = ((f32[8,16,6]{1,2,0:T(8,128)}), f32[8,16,6]{1,2,0:T(8,128)S(1)}, u32[]{:S(2)}, u32[]{:S(2)}) async-start(f32[8,16,6]{1,2,0:T(8,128)} %broadcast_in_dim.14), calls=%async_computation | async-start | bytes 65536 | tf_op jit(solution)/shard_map/all_to_all | solution.py:49
  12.8 0.8 %copy.65 = f32[16,21]{0,1:T(8,128)S(1)} copy(f32[16,21]{1,0:T(8,128)} %param.11) | data formatting | bytes 2688 | tf_op args[1]
  13.6 0.8 %copy.66 = f32[16,21]{0,1:T(8,128)S(1)} copy(f32[16,21]{1,0:T(8,128)} %param.12) | data formatting | bytes 2688 | tf_op args[2]
  14.4 2.2 %fusion = f32[32,148,168]{2,0,1:T(8,128)S(1)} fusion(s32[148,168]{1,0:T(8,128)S(1)} %iota_subtract_fusion, f32[16,21]{0,1:T(8,128)S(1)} %copy.66, f32[16,21]{0,1:T(8,128)S(1)} %copy.65), kind=kOutput, calls=%fused_computation.1 | convolution fusion | flops 201026112 | bytes 3284736 | tf_op jit(solution)/shard_map/ka,arc->krc/dot_general | solution.py:24
  16.6 1.5 %slice_bitcast_fusion.1 = f32[16,128,148,1]{2,0,1,3:T(8,128)} fusion(f32[32,148,168]{2,0,1:T(8,128)S(1)} %fusion), kind=kLoop, calls=%fused_computation.6 | loop fusion | bytes 2424832 | tf_op jit(solution)/shard_map/slice | solution.py:30
  18.1 0.0 copy-start.2
  18.2 0.2 slice_bitcast_fusion
  18.5 0.0 collective-permute-done
  18.5 0.5 copy-done.2
  19.0 2.6 %collective-permute-start.1 = (f32[2,10,128]{2,1,0:T(8,128)S(1)}, f32[2,10,128]{2,1,0:T(8,128)S(1)}, u32[]{:S(2)}, u32[]{:S(2)}) collective-permute-start(f32[2,10,128]{2,1,0:T(8,128)S(1)} %get-tuple-element.35), channel_id=1, source_target_pairs={{0,16},{16,32},{32,48},{48,64},{64,80},{80,96},{96,112},{112,128},... | collective-permute-start | bytes 30728 | tf_op jit(solution)/shard_map/ppermute | solution.py:55
  21.6 3.4 %collective-permute-start.2 = (f32[2,10,128]{2,1,0:T(8,128)S(1)}, f32[2,10,128]{2,1,0:T(8,128)S(1)}, u32[]{:S(2)}, u32[]{:S(2)}) collective-permute-start(f32[2,10,128]{2,1,0:T(8,128)S(1)} %get-tuple-element.36), channel_id=1, source_target_pairs={{16,0},{32,16},{48,32},{64,48},{80,64},{96,80},{112,96},{128,112},... | collective-permute-start | bytes 30728 | tf_op jit(solution)/shard_map/ppermute | solution.py:56
  25.0 0.1 broadcast_multiply_fusion.1
  25.1 0.0 collective-permute-done.1
  25.1 4.2 %collective-permute-done.2 = f32[2,10,128]{2,1,0:T(8,128)S(1)} collective-permute-done((f32[2,10,128]{2,1,0:T(8,128)S(1)}, f32[2,10,128]{2,1,0:T(8,128)S(1)}, u32[]{:S(2)}, u32[]{:S(2)}) %collective-permute-start.2) | collective-permute-done | bytes 10272 | tf_op jit(solution)/shard_map/ppermute | solution.py:56
  29.4 5.2 %fusion.4 = f32[2,168,16,128]{3,1,0,2:T(8,128)S(1)} fusion(f32[16,128,148,1]{2,0,1,3:T(8,128)} %slice_bitcast_fusion.1, f32[1,148,128]{2,1,0:T(8,128)S(1)} %get-tuple-element.34, f32[1,148,128]{2,1,0:T(8,128)S(1)} %get-tuple-element.33), kind=kOutput, calls=%fused_computation.7 | convolution fusion | flops 611356032 | bytes 4116480 | tf_op jit(solution)/shard_map/kra,bac->bkrc/dot_general | solution.py:32
  34.5 3.0 %fusion.7 = f32[2,16,128,148]{2,3,0,1:T(8,128)S(1)} fusion(f32[2,168,16,128]{3,1,0,2:T(8,128)S(1)} %fusion.4, f32[16,148,168,1]{2,0,1,3:T(8,128)S(1)} %slice_bitcast_fusion), kind=kOutput, calls=%fused_computation.12 | convolution fusion | flops 611057664 | bytes 6768640 | tf_op jit(solution)/shard_map/bkrc,kcd->bkrd/dot_general | solution.py:33
  37.5 0.2 slice_bitcast_fusion.3
  37.7 0.0 all-to-all-done
  37.7 1.6 %convolution_bitcast_fusion = f32[6,8,128,148]{2,1,3,0:T(8,128)S(1)} fusion(f32[16,128,148]{1,2,0:T(8,128)S(1)} %get-tuple-element.30, f32[8,16,6,1]{1,2,0,3:T(8,128)S(1)} %bitcast.153), kind=kOutput, calls=%fused_computation.9 | convolution fusion | flops 87293952 | bytes 4852736 | tf_op jit(solution)/shard_map/vkt,krc->tvrc/dot_general | solution.py:71
  39.3 1.6 %convolution_bitcast_fusion.1 = f32[6,8,128,148]{2,1,0,3:T(8,128)S(1)} fusion(f32[16,128,148,1]{1,2,0,3:T(8,128)S(1)} %get-tuple-element.29, f32[8,16,6]{1,2,0:T(8,128)S(1)} %all-to-all-done), kind=kOutput, calls=%fused_computation.10 | convolution fusion | flops 87293952 | bytes 4852736 | tf_op jit(solution)/shard_map/vkt,krc->tvrc/dot_general | solution.py:71
  40.9 0.4 fusion.27
  41.3 0.4 fusion.17
  41.7 0.1 pad_maximum_fusion
  41.8 0.0 copy-start.1
  41.8 2.0 %copy.79 = f32[8,2,128,148]{2,1,3,0:T(2,128)} copy(f32[8,2,128,148]{2,0,3,1:T(8,128)S(1)} %pad_maximum_fusion) | data formatting | bytes 2424832 | tf_op jit(solution)/shard_map/stack | solution.py:73
  43.8 4.8 %all-to-all-start.1 = ((f32[8,2,128,148]{2,1,3,0:T(2,128)}), f32[8,2,128,148]{2,1,3,0:T(2,128)S(1)}, u32[]{:S(2)}, u32[]{:S(2)}) async-start(f32[8,2,128,148]{2,1,3,0:T(2,128)} %copy.79), calls=%async_computation.1 | async-start | bytes 2424832 | tf_op jit(solution)/shard_map/all_to_all | solution.py:74
  48.6 0.0 copy-done.1
  48.6 0.3 copy.82
  49.0 0.0 copy-done
  49.0 0.1 constant_dynamic-slice_fusion
  49.1 0.5 fusion.63
  50.9 0.6 fusion.53
  51.5 14.8 %all-to-all-done.1 = f32[8,2,128,148]{2,1,3,0:T(2,128)S(1)} async-done(((f32[8,2,128,148]{2,1,3,0:T(2,128)}), f32[8,2,128,148]{2,1,3,0:T(2,128)S(1)}, u32[]{:S(2)}, u32[]{:S(2)}) %all-to-all-start.1) | async-done | bytes 1212448 | tf_op jit(solution)/shard_map/all_to_all | solution.py:74
  66.3 0.2 copy.123
  66.6 0.1 slice.174
  66.7 0.3 copy.81
  67.1 0.4 fusion.15
  67.5 1.3 %copy.83 = f32[1,128,2048]{2,1,0:T(8,128)} copy(f32[1,128,2048]{1,2,0:T(8,128)S(1)} %fusion.15) | data formatting | bytes 2097152 | tf_op jit(solution)/shard_map/jit(_where)/select_n | solution.py:90
  (10 shorter events, 0.1 us)
Async XLA Ops:
  0.0 49.0 %copy-start = (s32[16,2]{0,1:T(2,128)S(1)}, s32[16,2]{0,1:T(2,128)}, u32[]{:S(2)}) copy-start(s32[16,2]{0,1:T(2,128)} %param.15) | copy-start | bytes 388
  0.0 18.5 %collective-permute-start = (f32[128,128]{1,0:T(8,128)}, f32[128,128]{1,0:T(8,128)S(1)}, u32[]{:S(2)}, u32[]{:S(2)}) collective-permute-start(f32[128,128]{1,0:T(8,128)} %param.10), channel_id=1, source_target_pairs={{0,8},{8,0},{1,9},{9,1},{2,10},{10,2},{3,11},{11,3},{4,12},{12,4},... | collective-permute-start | bytes 196616 | tf_op jit(solution)/shard_map/ppermute | solution.py:52
  8.5 29.2 %all-to-all-start = ((f32[8,16,6]{1,2,0:T(8,128)}), f32[8,16,6]{1,2,0:T(8,128)S(1)}, u32[]{:S(2)}, u32[]{:S(2)}) async-start(f32[8,16,6]{1,2,0:T(8,128)} %broadcast_in_dim.14), calls=%async_computation | async-start | bytes 65536 | tf_op jit(solution)/shard_map/all_to_all | solution.py:49
  18.1 0.8 %copy-start.2 = (f32[128,128]{1,0:T(8,128)S(1)}, f32[128,128]{1,0:T(8,128)}, u32[]{:S(2)}) copy-start(f32[128,128]{1,0:T(8,128)} %param.10) | copy-start | bytes 196612
  19.0 6.1 %collective-permute-start.1 = (f32[2,10,128]{2,1,0:T(8,128)S(1)}, f32[2,10,128]{2,1,0:T(8,128)S(1)}, u32[]{:S(2)}, u32[]{:S(2)}) collective-permute-start(f32[2,10,128]{2,1,0:T(8,128)S(1)} %get-tuple-element.35), channel_id=1, source_target_pairs={{0,16},{16,32},{32,48},{48,64},{64,80},{80,96},{96,112},{112,128},... | collective-permute-start | bytes 30728 | tf_op jit(solution)/shard_map/ppermute | solution.py:55
  21.6 7.7 %collective-permute-start.2 = (f32[2,10,128]{2,1,0:T(8,128)S(1)}, f32[2,10,128]{2,1,0:T(8,128)S(1)}, u32[]{:S(2)}, u32[]{:S(2)}) collective-permute-start(f32[2,10,128]{2,1,0:T(8,128)S(1)} %get-tuple-element.36), channel_id=1, source_target_pairs={{16,0},{32,16},{48,32},{64,48},{80,64},{96,80},{112,96},{128,112},... | collective-permute-start | bytes 30728 | tf_op jit(solution)/shard_map/ppermute | solution.py:56
  41.8 6.8 %copy-start.1 = (f32[1,128,2048]{2,1,0:T(8,128)S(1)}, f32[1,128,2048]{2,1,0:T(8,128)}, u32[]{:S(2)}) copy-start(f32[1,128,2048]{2,1,0:T(8,128)} %param.14) | copy-start | bytes 3145732
  43.8 22.5 %all-to-all-start.1 = ((f32[8,2,128,148]{2,1,3,0:T(2,128)}), f32[8,2,128,148]{2,1,3,0:T(2,128)S(1)}, u32[]{:S(2)}, u32[]{:S(2)}) async-start(f32[8,2,128,148]{2,1,3,0:T(2,128)} %copy.79), calls=%async_computation.1 | async-start | bytes 2424832 | tf_op jit(solution)/shard_map/all_to_all | solution.py:74

commit v9 on v8

--- a/solution.py
+++ b/solution.py
@@ -21,7 +21,7 @@
     offset = lax.broadcasted_iota(jnp.int32, (rows, cols), 1) - lax.broadcasted_iota(jnp.int32, (rows, cols), 0)
     picks = (offset[None] == jnp.arange(row_taps.shape[1])[:, None, None]).astype(jnp.float32)
     taps = jnp.concatenate([row_taps, col_taps], axis=0)
-    return jnp.einsum("ka,arc->krc", taps, picks, precision=lax.Precision.HIGHEST)
+    return jnp.einsum("ka,arc->krc", taps, picks, precision=lax.Precision.HIGH)
 
 
 def separable(blocks, row_taps, col_taps, tile_rows, span):
@@ -63,14 +63,11 @@
     span = columns + 2 * half
     y_coord = coordinate(tile * tile_rows, tile_rows, total_rows)
     basis = separable(blocks, row_taps, col_taps, tile_rows, span)
-    models = []
-    y = y_coord[:, None]
-    for b in range(halves):
-        start = (b * group + place) * columns - half
-        x = coordinate(start, span, full_width)[None, :]
-        w = jnp.einsum("vkt,krc->tvrc", half_coeffs, basis[b], precision=lax.Precision.HIGH)
-        models.append(w[0] + x * w[1] + y * w[2] + (x * x) * w[3] + (x * y) * w[4] + (y * y) * w[5])
-    models = jnp.stack(models, axis=1)
+    y = y_coord[None, None, :, None]
+    starts = (jnp.arange(halves) * group + place) * columns - half
+    x = jnp.stack([coordinate(start, span, full_width) for start in starts])[None, :, None, :]
+    w = jnp.einsum("vkt,bkrc->tvbrc", half_coeffs, basis, precision=lax.Precision.HIGH)
+    models = w[0] + x * w[1] + y * w[2] + (x * x) * w[3] + (x * y) * w[4] + (y * y) * w[5]
     parts = lax.all_to_all(models, "xc", 0, 0, tiled=True)
     parts = jnp.swapaxes(parts, 0, 1).reshape((halves * group,) + parts.shape[2:])
     core = parts[:, :, half : half + columns]

time: 69.2 us -> 74.2 us (1.072)
  the two profiles are of different devices: /device:TPU:24 before, /device:TPU:32 now
where the time goes in v9:
time: 74.2 us; the launch traced here: 73.6 us
  starting transfers between devices  23.7 us (32%)
  local copies, waits for them, and re-layouts  16.7 us (23%)
  waiting for transfers between devices  14.8 us (20%)
  matrix products  13.5 us (18%)
  other arithmetic  3.41 us (5%)
  between operations  1.52 us (2%)
    all_to_all x1, waiting for transfers between devices, local(): parts = lax.all_to_all(models, 'xc', 0, 0, tiled=True)  14.8 us
    ppermute x1, starting transfers between devices, local(): pair = jnp.stack([template, lax.ppermute(template, 'zhi', swap)])  6.29 us
    slice x2, local copies, waits for them, and re-layouts, separable(): down = bands[:kernels, :tile_rows, :tile_rows + reach - 1]  5.92 us
    all_to_all x1, starting transfers between devices, local(): parts = lax.all_to_all(models, 'xc', 0, 0, tiled=True)  4.93 us
    dot_general x1, matrix products, local(): jnp.einsum('vkt,bkrc->tvbrc', half_coeffs, basis, precision=lax.Precision...  4.78 us
    unnamed x12, local copies, waits for them, and re-layouts  4.76 us
    ppermute x1, starting transfers between devices, local(): below = lax.ppermute(pair[:, :half], 'tile', up)  4.65 us
    dot_general x1, matrix products, separable(): jnp.einsum('bkrc,kcd->bkrd', passed, across, precision=lax.Precision.HIGH)  4.45 us
  transfers between devices with their start and end apart: 5, of which 1 were waited for; matrix products, arithmetic and copies ran while one was open for 29% of the time, Pallas kernels for 0%

profile of v9, /device:TPU:32, one launch (start us, length us, event | category | flops | bytes accessed | tf_op | source)
XLA Modules:
  0.0 73.6 jit_solution(6172602789778719196)
XLA Ops:
  0.0 0.0 copy-start
  0.0 6.3 %collective-permute-start = (f32[128,128]{1,0:T(8,128)}, f32[128,128]{1,0:T(8,128)S(1)}, u32[]{:S(2)}, u32[]{:S(2)}) collective-permute-start(f32[128,128]{1,0:T(8,128)} %param.10), channel_id=1, source_target_pairs={{0,8},{8,0},{1,9},{9,1},{2,10},{10,2},{3,11},{11,3},{4,12},{12,4},... | collective-permute-start | bytes 196616 | tf_op jit(solution)/shard_map/ppermute | solution.py:52
  6.3 0.7 copy.102
  7.0 0.6 broadcast_in_dim.14
  7.6 4.3 %all-to-all-start = ((f32[8,16,6]{1,2,0:T(8,128)}), f32[8,16,6]{1,2,0:T(8,128)S(1)}, u32[]{:S(2)}, u32[]{:S(2)}) async-start(f32[8,16,6]{1,2,0:T(8,128)} %broadcast_in_dim.14), calls=%async_computation | async-start | bytes 65536 | tf_op jit(solution)/shard_map/all_to_all | solution.py:49
  11.9 0.8 %copy.54 = f32[16,21]{0,1:T(8,128)S(1)} copy(f32[16,21]{1,0:T(8,128)} %param.11) | data formatting | bytes 2688 | tf_op args[1]
  12.7 0.8 %copy.55 = f32[16,21]{0,1:T(8,128)S(1)} copy(f32[16,21]{1,0:T(8,128)} %param.12) | data formatting | bytes 2688 | tf_op args[2]
  13.5 1.6 %fusion = f32[32,148,168]{2,0,1:T(8,128)S(1)} fusion(s32[148,168]{1,0:T(8,128)S(1)} %iota_subtract_fusion, f32[16,21]{0,1:T(8,128)S(1)} %copy.55, f32[16,21]{0,1:T(8,128)S(1)} %copy.54), kind=kOutput, calls=%fused_computation.1 | convolution fusion | flops 100774464 | bytes 3284736 | tf_op jit(solution)/shard_map/ka,arc->krc/dot_general | solution.py:24
  15.1 0.0 copy-start.1
  15.1 2.2 %copy-done.1 = f32[32,148,168]{2,0,1:T(8,128)} copy-done((f32[32,148,168]{2,0,1:T(8,128)}, f32[32,148,168]{2,0,1:T(8,128)S(1)}, u32[]{:S(2)}) %copy-start.1) | copy-done | bytes 3182616
  17.2 0.0 copy-start.3
  17.2 0.2 slice_bitcast_fusion
  17.5 0.6 fusion.48
  18.1 1.2 %multiply_add_fusion = (f32[1,148]{1,0:T(1,128)S(1)}, f32[1,148]{1,0:T(1,128)S(1)}) fusion(s32[]{:T(128)} %bitcast.16, s32[]{:T(128)} %bitcast.15), kind=kLoop, calls=%fused_computation.62 | loop fusion | flops 1480 | bytes 1192 | tf_op jit(solution)/shard_map/sub | solution.py:9
  19.4 0.0 collective-permute-done
  19.4 0.0 copy-done.3
  19.4 3.5 %collective-permute-start.1 = (f32[2,10,128]{2,1,0:T(8,128)S(1)}, f32[2,10,128]{2,1,0:T(8,128)S(1)}, u32[]{:S(2)}, u32[]{:S(2)}) collective-permute-start(f32[2,10,128]{2,1,0:T(8,128)S(1)} %get-tuple-element.33), channel_id=1, source_target_pairs={{0,16},{16,32},{32,48},{48,64},{64,80},{80,96},{96,112},{112,128},... | collective-permute-start | bytes 30728 | tf_op jit(solution)/shard_map/ppermute | solution.py:55
  22.9 4.6 %collective-permute-start.2 = (f32[2,10,128]{2,1,0:T(8,128)S(1)}, f32[2,10,128]{2,1,0:T(8,128)S(1)}, u32[]{:S(2)}, u32[]{:S(2)}) collective-permute-start(f32[2,10,128]{2,1,0:T(8,128)S(1)} %get-tuple-element.34), channel_id=1, source_target_pairs={{16,0},{32,16},{48,32},{64,48},{80,64},{96,80},{112,96},{128,112},... | collective-permute-start | bytes 30728 | tf_op jit(solution)/shard_map/ppermute | solution.py:56
  27.6 0.1 broadcast_multiply_fusion
  27.7 3.1 %slice.127 = f32[16,128,148]{2,0,1:T(8,128)} slice(f32[32,148,168]{2,0,1:T(8,128)} %copy-done.1), slice={[0:16], [0:128], [0:148]} | slice | bytes 2424832 | tf_op jit(solution)/shard_map/slice | solution.py:30
  30.8 2.8 %copy.56 = f32[16,128,148]{1,2,0:T(8,128)} copy(f32[16,128,148]{2,0,1:T(8,128)} %slice.127) | data formatting | bytes 2424832 | tf_op jit(solution)/shard_map/slice | solution.py:30
  33.6 0.0 collective-permute-done.1
  33.6 0.0 collective-permute-done.2
  33.7 2.7 %convolution_bitcast_fusion.1 = f32[2,16,128,168]{2,3,1,0:T(8,128)S(1)} fusion(f32[16,128,148]{1,2,0:T(8,128)} %copy.56, f32[1,148,128]{2,1,0:T(8,128)S(1)} %get-tuple-element.32, f32[1,148,128]{2,1,0:T(8,128)S(1)} %get-tuple-element.31), kind=kOutput, calls=%fused_computation.9 | convolution fusion | flops 611356032 | bytes 4116480 | tf_op jit(solution)/shard_map/kra,bac->bkrc/dot_general | solution.py:32
  36.4 4.5 %fusion.6 = f32[2,16,128,148,1]{2,3,0,1,4:T(8,128)} fusion(f32[2,16,128,168]{2,3,1,0:T(8,128)S(1)} %convolution_bitcast_fusion.1, f32[16,148,168,1]{2,0,1,3:T(8,128)S(1)} %slice_bitcast_fusion), kind=kOutput, calls=%fused_computation.10 | convolution fusion | flops 611057664 | bytes 6768640 | tf_op jit(solution)/shard_map/bkrc,kcd->bkrd/dot_general | solution.py:33
  40.9 0.0 all-to-all-done
  40.9 4.8 %convolution_bitcast_fusion = f32[6,8,2,128,148]{3,1,0,4,2:T(8,128)S(1)} fusion(f32[2,16,128,148,1]{2,3,0,1,4:T(8,128)} %fusion.6, f32[8,16,6,1,1]{1,2,0,4,3:T(8,128)S(1)} %bitcast.101), kind=kOutput, calls=%fused_computation.2 | convolution fusion | flops 174587904 | bytes 9702400 | tf_op jit(solution)/shard_map/vkt,bkrc->tvbrc/dot_general | solution.py:69
  45.7 0.9 %fusion.13 = f32[8,2,128,148]{2,0,3,1:T(8,128)S(1)} fusion(f32[6,8,2,128,148]{3,1,0,4,2:T(8,128)S(1)} %convolution_bitcast_fusion, f32[128]{0:T(128)S(1)} %get-tuple-element.42, f32[2,128,148]{1,2,0:T(8,128)S(1)} %broadcast_multiply_fusion, f32[2,148]{1,0:T(2,128)S(1)} %get-tuple-element.35, f32[128]{0:T(128)S(1)} %get-tuple-element.41, ...), kind=kLoop, calls=%fused_computation.14 | loop fusion | flops 3031040 | bytes 8641856 | tf_op jit(solution)/shard_map/add | solution.py:70
  46.6 2.0 %copy.66 = f32[8,2,128,148]{2,1,3,0:T(2,128)} copy(f32[8,2,128,148]{2,0,3,1:T(8,128)S(1)} %fusion.13) | data formatting | bytes 2424832 | tf_op jit(solution)/shard_map/add | solution.py:70
  48.6 0.0 copy-start.2
  48.6 4.9 %all-to-all-start.1 = ((f32[8,2,128,148]{2,1,3,0:T(2,128)}), f32[8,2,128,148]{2,1,3,0:T(2,128)S(1)}, u32[]{:S(2)}, u32[]{:S(2)}) async-start(f32[8,2,128,148]{2,1,3,0:T(2,128)} %copy.66), calls=%async_computation.1 | async-start | bytes 2424832 | tf_op jit(solution)/shard_map/all_to_all | solution.py:71
  53.5 0.0 copy-done.2
  53.5 0.3 copy.69
  53.8 0.0 copy-done
  53.9 0.1 constant_dynamic-slice_fusion
  53.9 0.5 fusion.47
  55.8 0.6 fusion.38
  56.4 14.8 %all-to-all-done.1 = f32[8,2,128,148]{2,1,3,0:T(2,128)S(1)} async-done(((f32[8,2,128,148]{2,1,3,0:T(2,128)}), f32[8,2,128,148]{2,1,3,0:T(2,128)S(1)}, u32[]{:S(2)}, u32[]{:S(2)}) %all-to-all-start.1) | async-done | bytes 1212448 | tf_op jit(solution)/shard_map/all_to_all | solution.py:71
  71.2 0.2 copy.101
  71.5 0.1 slice.134
  71.6 0.3 copy.68
  71.9 0.4 fusion.22
  72.3 1.3 %copy.70 = f32[1,128,2048]{2,1,0:T(8,128)} copy(f32[1,128,2048]{1,2,0:T(8,128)S(1)} %fusion.22) | data formatting | bytes 2097152 | tf_op jit(solution)/shard_map/jit(_where)/select_n | solution.py:87
  (10 shorter events, 0.1 us)
Async XLA Ops:
  0.0 53.8 %copy-start = (s32[16,2]{0,1:T(2,128)S(1)}, s32[16,2]{0,1:T(2,128)}, u32[]{:S(2)}) copy-start(s32[16,2]{0,1:T(2,128)} %param.15) | copy-start | bytes 388
  0.0 19.4 %collective-permute-start = (f32[128,128]{1,0:T(8,128)}, f32[128,128]{1,0:T(8,128)S(1)}, u32[]{:S(2)}, u32[]{:S(2)}) collective-permute-start(f32[128,128]{1,0:T(8,128)} %param.10), channel_id=1, source_target_pairs={{0,8},{8,0},{1,9},{9,1},{2,10},{10,2},{3,11},{11,3},{4,12},{12,4},... | collective-permute-start | bytes 196616 | tf_op jit(solution)/shard_map/ppermute | solution.py:52
  7.6 33.3 %all-to-all-start = ((f32[8,16,6]{1,2,0:T(8,128)}), f32[8,16,6]{1,2,0:T(8,128)S(1)}, u32[]{:S(2)}, u32[]{:S(2)}) async-start(f32[8,16,6]{1,2,0:T(8,128)} %broadcast_in_dim.14), calls=%async_computation | async-start | bytes 65536 | tf_op jit(solution)/shard_map/all_to_all | solution.py:49
  15.1 2.2 %copy-start.1 = (f32[32,148,168]{2,0,1:T(8,128)}, f32[32,148,168]{2,0,1:T(8,128)S(1)}, u32[]{:S(2)}) copy-start(f32[32,148,168]{2,0,1:T(8,128)S(1)} %fusion) | copy-start | bytes 9547780
  17.2 2.2 %copy-start.3 = (f32[128,128]{1,0:T(8,128)S(1)}, f32[128,128]{1,0:T(8,128)}, u32[]{:S(2)}) copy-start(f32[128,128]{1,0:T(8,128)} %param.10) | copy-start | bytes 196612
  19.4 14.2 %collective-permute-start.1 = (f32[2,10,128]{2,1,0:T(8,128)S(1)}, f32[2,10,128]{2,1,0:T(8,128)S(1)}, u32[]{:S(2)}, u32[]{:S(2)}) collective-permute-start(f32[2,10,128]{2,1,0:T(8,128)S(1)} %get-tuple-element.33), channel_id=1, source_target_pairs={{0,16},{16,32},{32,48},{48,64},{64,80},{80,96},{96,112},{112,128},... | collective-permute-start | bytes 30728 | tf_op jit(solution)/shard_map/ppermute | solution.py:55
  22.9 10.7 %collective-permute-start.2 = (f32[2,10,128]{2,1,0:T(8,128)S(1)}, f32[2,10,128]{2,1,0:T(8,128)S(1)}, u32[]{:S(2)}, u32[]{:S(2)}) collective-permute-start(f32[2,10,128]{2,1,0:T(8,128)S(1)} %get-tuple-element.34), channel_id=1, source_target_pairs={{16,0},{32,16},{48,32},{64,48},{80,64},{96,80},{112,96},{128,112},... | collective-permute-start | bytes 30728 | tf_op jit(solution)/shard_map/ppermute | solution.py:56
  48.6 4.9 %copy-start.2 = (f32[1,128,2048]{2,1,0:T(8,128)S(1)}, f32[1,128,2048]{2,1,0:T(8,128)}, u32[]{:S(2)}) copy-start(f32[1,128,2048]{2,1,0:T(8,128)} %param.14) | copy-start | bytes 3145732
  48.6 22.6 %all-to-all-start.1 = ((f32[8,2,128,148]{2,1,3,0:T(2,128)}), f32[8,2,128,148]{2,1,3,0:T(2,128)S(1)}, u32[]{:S(2)}, u32[]{:S(2)}) async-start(f32[8,2,128,148]{2,1,3,0:T(2,128)} %copy.66), calls=%async_computation.1 | async-start | bytes 2424832 | tf_op jit(solution)/shard_map/all_to_all | solution.py:71

commit v10 on v8

--- a/solution.py
+++ b/solution.py
@@ -17,18 +17,16 @@
     )
 
 
-def banded(row_taps, col_taps, rows, cols):
+def banded(taps, rows, cols):
     offset = lax.broadcasted_iota(jnp.int32, (rows, cols), 1) - lax.broadcasted_iota(jnp.int32, (rows, cols), 0)
-    picks = (offset[None] == jnp.arange(row_taps.shape[1])[:, None, None]).astype(jnp.float32)
-    taps = jnp.concatenate([row_taps, col_taps], axis=0)
+    picks = (offset[None] == jnp.arange(taps.shape[1])[:, None, None]).astype(jnp.float32)
     return jnp.einsum("ka,arc->krc", taps, picks, precision=lax.Precision.HIGHEST)
 
 
 def separable(blocks, row_taps, col_taps, tile_rows, span):
-    kernels, reach = row_taps.shape
-    bands = banded(row_taps, col_taps, span, span + reach - 1)
-    down = bands[:kernels, :tile_rows, : tile_rows + reach - 1]
-    across = jnp.swapaxes(bands[kernels:], 1, 2)
+    reach = row_taps.shape[1]
+    down = banded(row_taps, tile_rows, tile_rows + reach - 1)
+    across = jnp.swapaxes(banded(col_taps, span, span + reach - 1), 1, 2)
     passed = jnp.einsum("kra,bac->bkrc", down, blocks, precision=lax.Precision.HIGH)
     return jnp.einsum("bkrc,kcd->bkrd", passed, across, precision=lax.Precision.HIGH)
 

time: 69.2 us -> 65.1 us (0.941)
  the two profiles are of different devices: /device:TPU:24 before, /device:TPU:32 now
where the time goes in v10:
time: 65.1 us; the launch traced here: 64.3 us
  starting transfers between devices  23.7 us (36%)
  matrix products  15.7 us (24%)
  waiting for transfers between devices  15 us (23%)
  local copies, waits for them, and re-layouts  6.36 us (10%)
  other arithmetic  2.09 us (3%)
  between operations  1.5 us (2%)
    all_to_all x1, waiting for transfers between devices, local(): parts = lax.all_to_all(models, 'xc', 0, 0, tiled=True)  15 us
    ppermute x1, starting transfers between devices, local(): pair = jnp.stack([template, lax.ppermute(template, 'zhi', swap)])  6.38 us
    dot_general x1, matrix products, separable(): jnp.einsum('kra,bac->bkrc', down, blocks, precision=lax.Precision.HIGH)  5.15 us
    all_to_all x1, starting transfers between devices, local(): parts = lax.all_to_all(models, 'xc', 0, 0, tiled=True)  4.93 us
    ppermute x1, starting transfers between devices, local(): below = lax.ppermute(pair[:, :half], 'tile', up)  4.65 us
    dot_general x2, matrix products, banded(): jnp.einsum('ka,arc->krc', taps, picks, precision=lax.Precision.HIGHEST)  4.36 us
    all_to_all x1, starting transfers between devices, local(): half_coeffs = lax.all_to_all(copies, 'xc', 0, 0, tiled=True)  4.3 us
    ppermute x1, starting transfers between devices, local(): above = lax.ppermute(pair[:, tile_rows - half:], 'tile', down)  3.48 us
  transfers between devices with their start and end apart: 5, of which 1 were waited for; matrix products, arithmetic and copies ran while one was open for 24% of the time, Pallas kernels for 0%

profile of v10, /device:TPU:32, one launch (start us, length us, event | category | flops | bytes accessed | tf_op | source)
XLA Modules:
  0.0 64.3 jit_solution(2909745826646165799)
XLA Ops:
  0.0 0.0 copy-start
  0.0 0.0 copy-start.2
  0.0 0.0 copy-start.3
  0.0 6.4 %collective-permute-start = (f32[128,128]{1,0:T(8,128)}, f32[128,128]{1,0:T(8,128)S(1)}, u32[]{:S(2)}, u32[]{:S(2)}) collective-permute-start(f32[128,128]{1,0:T(8,128)} %param.10), channel_id=1, source_target_pairs={{0,8},{8,0},{1,9},{9,1},{2,10},{10,2},{3,11},{11,3},{4,12},{12,4},... | collective-permute-start | bytes 196616 | tf_op jit(solution)/shard_map/ppermute | solution.py:50
  6.4 0.7 %copy.112 = f32[1,16,6]{1,2,0:T(8,128)S(1)} copy(f32[1,16,6]{1,0,2:T(1,128)} %param.13) | data formatting | bytes 768
  7.1 0.6 broadcast_in_dim.14
  7.7 4.3 %all-to-all-start = ((f32[8,16,6]{1,2,0:T(8,128)}), f32[8,16,6]{1,2,0:T(8,128)S(1)}, u32[]{:S(2)}, u32[]{:S(2)}) async-start(f32[8,16,6]{1,2,0:T(8,128)} %broadcast_in_dim.14), calls=%async_computation | async-start | bytes 65536 | tf_op jit(solution)/shard_map/all_to_all | solution.py:47
  12.1 0.0 copy-done
  12.1 1.7 %fusion.13 = f32[16,148,168,1]{2,0,1,3:T(8,128)S(1)} fusion(s32[148,168]{1,0:T(8,128)S(1)} %iota_subtract_fusion, f32[16,21]{1,0:T(8,128)S(1)} %copy-done), kind=kOutput, calls=%fused_computation.13 | convolution fusion | flops 100773792 | bytes 1692096 | tf_op jit(solution)/shard_map/ka,arc->krc/dot_general | solution.py:23
  13.8 0.1 broadcast_multiply_fusion.1
  13.9 0.0 collective-permute-done
  13.9 0.0 copy-done.2
  13.9 3.5 %collective-permute-start.1 = (f32[2,10,128]{2,1,0:T(8,128)S(1)}, f32[2,10,128]{2,1,0:T(8,128)S(1)}, u32[]{:S(2)}, u32[]{:S(2)}) collective-permute-start(f32[2,10,128]{2,1,0:T(8,128)S(1)} %get-tuple-element.35), channel_id=1, source_target_pairs={{0,16},{16,32},{32,48},{48,64},{64,80},{80,96},{96,112},{112,128},... | collective-permute-start | bytes 30728 | tf_op jit(solution)/shard_map/ppermute | solution.py:53
  17.4 4.6 %collective-permute-start.2 = (f32[2,10,128]{2,1,0:T(8,128)S(1)}, f32[2,10,128]{2,1,0:T(8,128)S(1)}, u32[]{:S(2)}, u32[]{:S(2)}) collective-permute-start(f32[2,10,128]{2,1,0:T(8,128)S(1)} %get-tuple-element.36), channel_id=1, source_target_pairs={{16,0},{32,16},{48,32},{64,48},{80,64},{96,80},{112,96},{128,112},... | collective-permute-start | bytes 30728 | tf_op jit(solution)/shard_map/ppermute | solution.py:54
  22.1 0.0 copy-done.3
  22.1 2.7 %fusion.14 = f32[16,128,148,1]{2,0,1,3:T(8,128)} fusion(s32[128,148]{1,0:T(8,128)S(1)} %iota_subtract_fusion.1, f32[16,21]{1,0:T(8,128)S(1)} %copy-done.3), kind=kOutput, calls=%fused_computation.14 | convolution fusion | flops 76780032 | bytes 1289536 | tf_op jit(solution)/shard_map/ka,arc->krc/dot_general | solution.py:23
  24.8 0.0 collective-permute-done.1
  24.8 0.0 collective-permute-done.2
  24.8 5.2 %fusion.5 = f32[2,168,16,128]{3,1,0,2:T(8,128)S(1)} fusion(f32[16,128,148,1]{2,0,1,3:T(8,128)} %fusion.14, f32[1,148,128]{2,1,0:T(8,128)S(1)} %get-tuple-element.34, f32[1,148,128]{2,1,0:T(8,128)S(1)} %get-tuple-element.33), kind=kOutput, calls=%fused_computation.7 | convolution fusion | flops 611356032 | bytes 4116480 | tf_op jit(solution)/shard_map/kra,bac->bkrc/dot_general | solution.py:30
  30.0 3.0 %fusion.8 = f32[2,16,128,148]{2,3,0,1:T(8,128)S(1)} fusion(f32[2,168,16,128]{3,1,0,2:T(8,128)S(1)} %fusion.5, f32[16,148,168,1]{2,0,1,3:T(8,128)S(1)} %fusion.13), kind=kOutput, calls=%fused_computation.12 | convolution fusion | flops 611057664 | bytes 6768640 | tf_op jit(solution)/shard_map/bkrc,kcd->bkrd/dot_general | solution.py:31
  33.0 0.2 slice_bitcast_fusion.1
  33.2 0.0 all-to-all-done
  33.2 1.6 %convolution_bitcast_fusion = f32[6,8,128,148]{2,1,3,0:T(8,128)S(1)} fusion(f32[16,128,148]{1,2,0:T(8,128)S(1)} %get-tuple-element.30, f32[8,16,6,1]{1,2,0,3:T(8,128)S(1)} %bitcast.160), kind=kOutput, calls=%fused_computation.9 | convolution fusion | flops 87293952 | bytes 4852736 | tf_op jit(solution)/shard_map/vkt,krc->tvrc/dot_general | solution.py:69
  34.8 0.4 fusion.21
  35.2 1.6 %convolution_bitcast_fusion.1 = f32[6,8,128,148]{2,1,0,3:T(8,128)S(1)} fusion(f32[16,128,148,1]{1,2,0,3:T(8,128)S(1)} %get-tuple-element.29, f32[8,16,6]{1,2,0:T(8,128)S(1)} %all-to-all-done), kind=kOutput, calls=%fused_computation.10 | convolution fusion | flops 87293952 | bytes 4852736 | tf_op jit(solution)/shard_map/vkt,krc->tvrc/dot_general | solution.py:69
  36.8 0.4 fusion.31
  37.2 0.1 pad_maximum_fusion
  37.3 0.0 copy-start.1
  37.3 2.0 %copy.67 = f32[8,2,128,148]{2,1,3,0:T(2,128)} copy(f32[8,2,128,148]{2,0,3,1:T(8,128)S(1)} %pad_maximum_fusion) | data formatting | bytes 2424832 | tf_op jit(solution)/shard_map/stack | solution.py:71
  39.3 0.0 copy-start.4
  39.3 4.9 %all-to-all-start.1 = ((f32[8,2,128,148]{2,1,3,0:T(2,128)}), f32[8,2,128,148]{2,1,3,0:T(2,128)S(1)}, u32[]{:S(2)}, u32[]{:S(2)}) async-start(f32[8,2,128,148]{2,1,3,0:T(2,128)} %copy.67), calls=%async_computation.1 | async-start | bytes 2424832 | tf_op jit(solution)/shard_map/all_to_all | solution.py:72
  44.2 0.0 copy-done.1
  44.2 0.3 copy.70
  44.5 0.0 copy-done.4
  44.5 0.1 constant_dynamic-slice_fusion
  44.6 0.5 fusion.66
  46.4 0.6 fusion.57
  46.9 15.0 %all-to-all-done.1 = f32[8,2,128,148]{2,1,3,0:T(2,128)S(1)} async-done(((f32[8,2,128,148]{2,1,3,0:T(2,128)}), f32[8,2,128,148]{2,1,3,0:T(2,128)S(1)}, u32[]{:S(2)}, u32[]{:S(2)}) %all-to-all-start.1) | async-done | bytes 1212448 | tf_op jit(solution)/shard_map/all_to_all | solution.py:72
  61.9 0.2 copy.111
  62.1 0.1 slice.164
  62.3 0.3 copy.69
  62.6 0.4 fusion.19
  63.0 1.3 %copy.71 = f32[1,128,2048]{2,1,0:T(8,128)} copy(f32[1,128,2048]{1,2,0:T(8,128)S(1)} %fusion.19) | data formatting | bytes 2097152 | tf_op jit(solution)/shard_map/jit(_where)/select_n | solution.py:88
  (11 shorter events, 0.1 us)
Async XLA Ops:
  0.0 12.1 %copy-start = (f32[16,21]{1,0:T(8,128)S(1)}, f32[16,21]{1,0:T(8,128)}, u32[]{:S(2)}) copy-start(f32[16,21]{1,0:T(8,128)} %param.12) | copy-start | bytes 4036
  0.0 13.9 %copy-start.2 = (f32[128,128]{1,0:T(8,128)S(1)}, f32[128,128]{1,0:T(8,128)}, u32[]{:S(2)}) copy-start(f32[128,128]{1,0:T(8,128)} %param.10) | copy-start | bytes 196612
  0.0 22.1 %copy-start.3 = (f32[16,21]{1,0:T(8,128)S(1)}, f32[16,21]{1,0:T(8,128)}, u32[]{:S(2)}) copy-start(f32[16,21]{1,0:T(8,128)} %param.11) | copy-start | bytes 4036
  0.0 13.9 %collective-permute-start = (f32[128,128]{1,0:T(8,128)}, f32[128,128]{1,0:T(8,128)S(1)}, u32[]{:S(2)}, u32[]{:S(2)}) collective-permute-start(f32[128,128]{1,0:T(8,128)} %param.10), channel_id=1, source_target_pairs={{0,8},{8,0},{1,9},{9,1},{2,10},{10,2},{3,11},{11,3},{4,12},{12,4},... | collective-permute-start | bytes 196616 | tf_op jit(solution)/shard_map/ppermute | solution.py:50
  7.7 25.5 %all-to-all-start = ((f32[8,16,6]{1,2,0:T(8,128)}), f32[8,16,6]{1,2,0:T(8,128)S(1)}, u32[]{:S(2)}, u32[]{:S(2)}) async-start(f32[8,16,6]{1,2,0:T(8,128)} %broadcast_in_dim.14), calls=%async_computation | async-start | bytes 65536 | tf_op jit(solution)/shard_map/all_to_all | solution.py:47
  13.9 10.8 %collective-permute-start.1 = (f32[2,10,128]{2,1,0:T(8,128)S(1)}, f32[2,10,128]{2,1,0:T(8,128)S(1)}, u32[]{:S(2)}, u32[]{:S(2)}) collective-permute-start(f32[2,10,128]{2,1,0:T(8,128)S(1)} %get-tuple-element.35), channel_id=1, source_target_pairs={{0,16},{16,32},{32,48},{48,64},{64,80},{80,96},{96,112},{112,128},... | collective-permute-start | bytes 30728 | tf_op jit(solution)/shard_map/ppermute | solution.py:53
  17.4 7.3 %collective-permute-start.2 = (f32[2,10,128]{2,1,0:T(8,128)S(1)}, f32[2,10,128]{2,1,0:T(8,128)S(1)}, u32[]{:S(2)}, u32[]{:S(2)}) collective-permute-start(f32[2,10,128]{2,1,0:T(8,128)S(1)} %get-tuple-element.36), channel_id=1, source_target_pairs={{16,0},{32,16},{48,32},{64,48},{80,64},{96,80},{112,96},{128,112},... | collective-permute-start | bytes 30728 | tf_op jit(solution)/shard_map/ppermute | solution.py:54
  37.3 6.9 %copy-start.1 = (f32[1,128,2048]{2,1,0:T(8,128)S(1)}, f32[1,128,2048]{2,1,0:T(8,128)}, u32[]{:S(2)}) copy-start(f32[1,128,2048]{2,1,0:T(8,128)} %param.14) | copy-start | bytes 3145732
  39.3 5.3 %copy-start.4 = (s32[16,2]{0,1:T(2,128)S(1)}, s32[16,2]{0,1:T(2,128)}, u32[]{:S(2)}) copy-start(s32[16,2]{0,1:T(2,128)} %param.15) | copy-start | bytes 388
  39.3 22.6 %all-to-all-start.1 = ((f32[8,2,128,148]{2,1,3,0:T(2,128)}), f32[8,2,128,148]{2,1,3,0:T(2,128)S(1)}, u32[]{:S(2)}, u32[]{:S(2)}) async-start(f32[8,2,128,148]{2,1,3,0:T(2,128)} %copy.67), calls=%async_computation.1 | async-start | bytes 2424832 | tf_op jit(solution)/shard_map/all_to_all | solution.py:72

commit v11 on v10

--- a/solution.py
+++ b/solution.py
@@ -27,8 +27,8 @@
     reach = row_taps.shape[1]
     down = banded(row_taps, tile_rows, tile_rows + reach - 1)
     across = jnp.swapaxes(banded(col_taps, span, span + reach - 1), 1, 2)
-    passed = jnp.einsum("kra,bac->bkrc", down, blocks, precision=lax.Precision.HIGH)
-    return jnp.einsum("bkrc,kcd->bkrd", passed, across, precision=lax.Precision.HIGH)
+    passed = jnp.einsum("bac,kcd->bkad", blocks, across, precision=lax.Precision.HIGH)
+    return jnp.einsum("kra,bkad->bkrd", down, passed, precision=lax.Precision.HIGH)
 
 
 def local(template, row_taps, col_taps, coeffs, visits, boxes):

time: 65.1 us -> 62.6 us (0.962)
  the two profiles are of different devices: /device:TPU:32 before, /device:TPU:24 now
where the time goes in v11:
time: 62.6 us; the launch traced here: 62.2 us
  starting transfers between devices  22.5 us (36%)
  waiting for transfers between devices  17 us (27%)
  matrix products  12.5 us (20%)
  local copies, waits for them, and re-layouts  6.7 us (11%)
  other arithmetic  2.05 us (3%)
  between operations  1.57 us (3%)
    all_to_all x1, waiting for transfers between devices, local(): parts = lax.all_to_all(models, 'xc', 0, 0, tiled=True)  14.5 us
    ppermute x1, starting transfers between devices, local(): pair = jnp.stack([template, lax.ppermute(template, 'zhi', swap)])  7.19 us
    all_to_all x1, starting transfers between devices, local(): parts = lax.all_to_all(models, 'xc', 0, 0, tiled=True)  4.94 us
    all_to_all x1, starting transfers between devices, local(): half_coeffs = lax.all_to_all(copies, 'xc', 0, 0, tiled=True)  4.3 us
    dot_general x2, matrix products, banded(): jnp.einsum('ka,arc->krc', taps, picks, precision=lax.Precision.HIGHEST)  3.5 us
    ppermute x1, starting transfers between devices, local(): below = lax.ppermute(pair[:, :half], 'tile', up)  3.44 us
    dot_general x1, matrix products, separable(): jnp.einsum('bac,kcd->bkad', blocks, across, precision=lax.Precision.HIGH)  3.39 us
    dot_general x2, matrix products, local(): jnp.einsum('vkt,krc->tvrc', half_coeffs, basis[b], precision=lax.Precisio...  3.18 us
  transfers between devices with their start and end apart: 5, of which 2 were waited for; matrix products, arithmetic and copies ran while one was open for 20% of the time, Pallas kernels for 0%

profile of v11, /device:TPU:24, one launch (start us, length us, event | category | flops | bytes accessed | tf_op | source)
XLA Modules:
  0.0 62.2 jit_solution(13000797260148934143)
XLA Ops:
  0.0 0.0 copy-start
  0.0 7.2 %collective-permute-start = (f32[128,128]{1,0:T(8,128)}, f32[128,128]{1,0:T(8,128)S(1)}, u32[]{:S(2)}, u32[]{:S(2)}) collective-permute-start(f32[128,128]{1,0:T(8,128)} %param.10), channel_id=1, source_target_pairs={{0,8},{8,0},{1,9},{9,1},{2,10},{10,2},{3,11},{11,3},{4,12},{12,4},... | collective-permute-start | bytes 196616 | tf_op jit(solution)/shard_map/ppermute | solution.py:50
  7.2 0.7 %copy.110 = f32[1,16,6]{1,2,0:T(8,128)S(1)} copy(f32[1,16,6]{1,0,2:T(1,128)} %param.13) | data formatting | bytes 768
  7.9 0.6 broadcast_in_dim.14
  8.5 4.3 %all-to-all-start = ((f32[8,16,6]{1,2,0:T(8,128)}), f32[8,16,6]{1,2,0:T(8,128)S(1)}, u32[]{:S(2)}, u32[]{:S(2)}) async-start(f32[8,16,6]{1,2,0:T(8,128)} %broadcast_in_dim.14), calls=%async_computation | async-start | bytes 65536 | tf_op jit(solution)/shard_map/all_to_all | solution.py:47
  12.9 0.0 copy-done
  12.9 0.0 copy-start.3
  12.9 0.0 copy-start.4
  12.9 1.7 %fusion.10 = f32[16,168,148,1]{1,0,2,3:T(8,128)S(1)} fusion(s32[148,168]{1,0:T(8,128)S(1)} %iota_subtract_fusion, f32[16,21]{1,0:T(8,128)S(1)} %copy-done), kind=kOutput, calls=%fused_computation.12 | convolution fusion | flops 100773792 | bytes 1692096 | tf_op jit(solution)/shard_map/ka,arc->krc/dot_general | solution.py:23
  14.6 0.1 broadcast_multiply_fusion.1
  14.7 0.0 collective-permute-done
  14.7 0.0 copy-done.3
  14.8 2.6 %collective-permute-start.1 = (f32[2,10,128]{2,1,0:T(8,128)S(1)}, f32[2,10,128]{2,1,0:T(8,128)S(1)}, u32[]{:S(2)}, u32[]{:S(2)}) collective-permute-start(f32[2,10,128]{2,1,0:T(8,128)S(1)} %get-tuple-element.35), channel_id=1, source_target_pairs={{0,16},{16,32},{32,48},{48,64},{64,80},{80,96},{96,112},{112,128},... | collective-permute-start | bytes 30728 | tf_op jit(solution)/shard_map/ppermute | solution.py:53
  17.4 3.4 %collective-permute-start.2 = (f32[2,10,128]{2,1,0:T(8,128)S(1)}, f32[2,10,128]{2,1,0:T(8,128)S(1)}, u32[]{:S(2)}, u32[]{:S(2)}) collective-permute-start(f32[2,10,128]{2,1,0:T(8,128)S(1)} %get-tuple-element.36), channel_id=1, source_target_pairs={{16,0},{32,16},{48,32},{64,48},{80,64},{96,80},{112,96},{128,112},... | collective-permute-start | bytes 30728 | tf_op jit(solution)/shard_map/ppermute | solution.py:54
  20.8 0.0 copy-done.4
  20.8 1.8 %fusion.11 = f32[16,128,148,1]{1,0,2,3:T(8,128)} fusion(s32[128,148]{0,1:T(8,128)S(1)} %iota_subtract_fusion.1, f32[16,21]{1,0:T(8,128)S(1)} %copy-done.4), kind=kOutput, calls=%fused_computation.13 | convolution fusion | flops 76780032 | bytes 1289536 | tf_op jit(solution)/shard_map/ka,arc->krc/dot_general | solution.py:23
  22.6 0.0 collective-permute-done.1
  22.6 2.5 %collective-permute-done.2 = f32[2,10,128]{2,1,0:T(8,128)S(1)} collective-permute-done((f32[2,10,128]{2,1,0:T(8,128)S(1)}, f32[2,10,128]{2,1,0:T(8,128)S(1)}, u32[]{:S(2)}, u32[]{:S(2)}) %collective-permute-start.2) | collective-permute-done | bytes 10272 | tf_op jit(solution)/shard_map/ppermute | solution.py:54
  25.1 0.0 copy-start.1
  25.1 3.4 %fusion.3 = f32[16,148,2,148]{3,1,2,0:T(8,128)S(1)} fusion(f32[16,168,148,1]{1,0,2,3:T(8,128)S(1)} %fusion.10, f32[1,148,128]{2,1,0:T(8,128)S(1)} %get-tuple-element.34, f32[1,148,128]{2,1,0:T(8,128)S(1)} %get-tuple-element.33), kind=kOutput, calls=%fused_computation.4 | convolution fusion | flops 706833792 | bytes 4546560 | tf_op jit(solution)/shard_map/bac,kcd->bkad/dot_general | solution.py:30
  28.5 0.0 copy-done.1
  28.6 2.4 %fusion.7 = f32[2,16,128,148]{2,3,0,1:T(8,128)S(1)} fusion(f32[16,148,2,148]{3,1,2,0:T(8,128)S(1)} %fusion.3, f32[16,128,148,1]{1,0,2,3:T(8,128)S(1)} %copy-done.1), kind=kOutput, calls=%fused_computation.11 | convolution fusion | flops 538312704 | bytes 6440960 | tf_op jit(solution)/shard_map/kra,bkad->bkrd/dot_general | solution.py:31
  31.0 0.2 slice_bitcast_fusion.1
  31.1 0.0 all-to-all-done
  31.2 1.6 %convolution_bitcast_fusion = f32[6,8,128,148]{2,1,3,0:T(8,128)S(1)} fusion(f32[16,128,148]{1,2,0:T(8,128)S(1)} %get-tuple-element.30, f32[8,16,6,1]{1,2,0,3:T(8,128)S(1)} %bitcast.160), kind=kOutput, calls=%fused_computation.6 | convolution fusion | flops 87293952 | bytes 4852736 | tf_op jit(solution)/shard_map/vkt,krc->tvrc/dot_general | solution.py:69
  32.8 0.4 fusion.19
  33.2 1.6 %convolution_bitcast_fusion.1 = f32[6,8,128,148]{2,1,0,3:T(8,128)S(1)} fusion(f32[16,128,148,1]{1,2,0,3:T(8,128)S(1)} %get-tuple-element.29, f32[8,16,6]{1,2,0:T(8,128)S(1)} %all-to-all-done), kind=kOutput, calls=%fused_computation.7 | convolution fusion | flops 87293952 | bytes 4852736 | tf_op jit(solution)/shard_map/vkt,krc->tvrc/dot_general | solution.py:69
  34.8 0.4 fusion.29
  35.2 0.1 pad_maximum_fusion
  35.3 2.0 %copy.67 = f32[8,2,128,148]{2,1,3,0:T(2,128)} copy(f32[8,2,128,148]{2,0,3,1:T(8,128)S(1)} %pad_maximum_fusion) | data formatting | bytes 2424832 | tf_op jit(solution)/shard_map/stack | solution.py:71
  37.2 0.0 copy-start.2
  37.2 4.9 %all-to-all-start.1 = ((f32[8,2,128,148]{2,1,3,0:T(2,128)}), f32[8,2,128,148]{2,1,3,0:T(2,128)S(1)}, u32[]{:S(2)}, u32[]{:S(2)}) async-start(f32[8,2,128,148]{2,1,3,0:T(2,128)} %copy.67), calls=%async_computation.1 | async-start | bytes 2424832 | tf_op jit(solution)/shard_map/all_to_all | solution.py:72
  42.2 0.0 copy-start.5
  42.2 0.0 copy-done.2
  42.2 0.3 copy.70
  42.5 0.3 copy-done.5
  42.9 0.1 constant_dynamic-slice_fusion
  42.9 0.5 fusion.64
  44.7 0.6 fusion.55
  45.3 14.5 %all-to-all-done.1 = f32[8,2,128,148]{2,1,3,0:T(2,128)S(1)} async-done(((f32[8,2,128,148]{2,1,3,0:T(2,128)}), f32[8,2,128,148]{2,1,3,0:T(2,128)S(1)}, u32[]{:S(2)}, u32[]{:S(2)}) %all-to-all-start.1) | async-done | bytes 1212448 | tf_op jit(solution)/shard_map/all_to_all | solution.py:72
  59.9 0.2 copy.109
  60.1 0.1 slice.164
  60.3 0.3 copy.69
  60.6 0.3 fusion.16
  60.9 1.3 %copy.71 = f32[1,128,2048]{2,1,0:T(8,128)} copy(f32[1,128,2048]{1,2,0:T(8,128)S(1)} %fusion.16) | data formatting | bytes 2097152 | tf_op jit(solution)/shard_map/jit(_where)/select_n | solution.py:88
  (11 shorter events, 0.1 us)
Async XLA Ops:
  0.0 12.9 %copy-start = (f32[16,21]{1,0:T(8,128)S(1)}, f32[16,21]{1,0:T(8,128)}, u32[]{:S(2)}) copy-start(f32[16,21]{1,0:T(8,128)} %param.12) | copy-start | bytes 4036
  0.0 14.7 %collective-permute-start = (f32[128,128]{1,0:T(8,128)}, f32[128,128]{1,0:T(8,128)S(1)}, u32[]{:S(2)}, u32[]{:S(2)}) collective-permute-start(f32[128,128]{1,0:T(8,128)} %param.10), channel_id=1, source_target_pairs={{0,8},{8,0},{1,9},{9,1},{2,10},{10,2},{3,11},{11,3},{4,12},{12,4},... | collective-permute-start | bytes 196616 | tf_op jit(solution)/shard_map/ppermute | solution.py:50
  8.5 22.7 %all-to-all-start = ((f32[8,16,6]{1,2,0:T(8,128)}), f32[8,16,6]{1,2,0:T(8,128)S(1)}, u32[]{:S(2)}, u32[]{:S(2)}) async-start(f32[8,16,6]{1,2,0:T(8,128)} %broadcast_in_dim.14), calls=%async_computation | async-start | bytes 65536 | tf_op jit(solution)/shard_map/all_to_all | solution.py:47
  12.9 1.9 %copy-start.3 = (f32[128,128]{1,0:T(8,128)S(1)}, f32[128,128]{1,0:T(8,128)}, u32[]{:S(2)}) copy-start(f32[128,128]{1,0:T(8,128)} %param.10) | copy-start | bytes 196612
  12.9 7.9 %copy-start.4 = (f32[16,21]{1,0:T(8,128)S(1)}, f32[16,21]{1,0:T(8,128)}, u32[]{:S(2)}) copy-start(f32[16,21]{1,0:T(8,128)} %param.11) | copy-start | bytes 4036
  14.8 7.9 %collective-permute-start.1 = (f32[2,10,128]{2,1,0:T(8,128)S(1)}, f32[2,10,128]{2,1,0:T(8,128)S(1)}, u32[]{:S(2)}, u32[]{:S(2)}) collective-permute-start(f32[2,10,128]{2,1,0:T(8,128)S(1)} %get-tuple-element.35), channel_id=1, source_target_pairs={{0,16},{16,32},{32,48},{48,64},{64,80},{80,96},{96,112},{112,128},... | collective-permute-start | bytes 30728 | tf_op jit(solution)/shard_map/ppermute | solution.py:53
  17.4 7.7 %collective-permute-start.2 = (f32[2,10,128]{2,1,0:T(8,128)S(1)}, f32[2,10,128]{2,1,0:T(8,128)S(1)}, u32[]{:S(2)}, u32[]{:S(2)}) collective-permute-start(f32[2,10,128]{2,1,0:T(8,128)S(1)} %get-tuple-element.36), channel_id=1, source_target_pairs={{16,0},{32,16},{48,32},{64,48},{80,64},{96,80},{112,96},{128,112},... | collective-permute-start | bytes 30728 | tf_op jit(solution)/shard_map/ppermute | solution.py:54
  25.1 3.4 %copy-start.1 = (f32[16,128,148,1]{1,0,2,3:T(8,128)S(1)}, f32[16,128,148,1]{1,0,2,3:T(8,128)}, u32[]{:S(2)}) copy-start(f32[16,128,148,1]{1,0,2,3:T(8,128)} %fusion.11) | copy-start | bytes 3637252
  37.2 5.0 %copy-start.2 = (f32[1,128,2048]{2,1,0:T(8,128)S(1)}, f32[1,128,2048]{2,1,0:T(8,128)}, u32[]{:S(2)}) copy-start(f32[1,128,2048]{2,1,0:T(8,128)} %param.14) | copy-start | bytes 3145732
  37.2 22.6 %all-to-all-start.1 = ((f32[8,2,128,148]{2,1,3,0:T(2,128)}), f32[8,2,128,148]{2,1,3,0:T(2,128)S(1)}, u32[]{:S(2)}, u32[]{:S(2)}) async-start(f32[8,2,128,148]{2,1,3,0:T(2,128)} %copy.67), calls=%async_computation.1 | async-start | bytes 2424832 | tf_op jit(solution)/shard_map/all_to_all | solution.py:72
  42.2 0.7 %copy-start.5 = (s32[16,2]{0,1:T(2,128)S(1)}, s32[16,2]{0,1:T(2,128)}, u32[]{:S(2)}) copy-start(s32[16,2]{0,1:T(2,128)} %param.15) | copy-start | bytes 388

commit v12 on v11

--- a/solution.py
+++ b/solution.py
@@ -43,8 +43,6 @@
     full_width = columns * halves * group
     total_rows = tile_rows * tiles
 
-    copies = jnp.broadcast_to(coeffs, (group,) + coeffs.shape[1:])
-    half_coeffs = lax.all_to_all(copies, "xc", 0, 0, tiled=True)
 
     swap = [(h, halves - 1 - h) for h in range(halves)]
     pair = jnp.stack([template, lax.ppermute(template, "zhi", swap)])
@@ -52,6 +50,9 @@
     up = [(i + 1, i) for i in range(tiles - 1)]
     above = lax.ppermute(pair[:, tile_rows - half :], "tile", down)
     below = lax.ppermute(pair[:, :half], "tile", up)
+    copies = jnp.broadcast_to(coeffs, (group,) + coeffs.shape[1:])
+    copies, pair = lax.optimization_barrier((copies, pair))
+    half_coeffs = lax.all_to_all(copies, "xc", 0, 0, tiled=True)
     extended = jnp.concatenate([above, pair, below], axis=1)
     own = extended[0]
     other = extended[1]

time: 62.6 us -> 61.1 us (0.976)
  the two profiles are of different devices: /device:TPU:24 before, /device:TPU:32 now
where the time goes in v12:
time: 61.1 us; the launch traced here: 60.8 us
  starting transfers between devices  23.5 us (38%)
  waiting for transfers between devices  14.5 us (24%)
  matrix products  12.5 us (20%)
  local copies, waits for them, and re-layouts  6.7 us (11%)
  other arithmetic  2.06 us (3%)
  between operations  1.56 us (3%)
    all_to_all x1, waiting for transfers between devices, local(): parts = lax.all_to_all(models, 'xc', 0, 0, tiled=True)  14.5 us
    ppermute x1, starting transfers between devices, local(): pair = jnp.stack([template, lax.ppermute(template, 'zhi', swap)])  6.29 us
    all_to_all x1, starting transfers between devices, local(): parts = lax.all_to_all(models, 'xc', 0, 0, tiled=True)  4.92 us
    ppermute x1, starting transfers between devices, local(): below = lax.ppermute(pair[:, :half], 'tile', up)  4.47 us
    all_to_all x1, starting transfers between devices, local(): half_coeffs = lax.all_to_all(copies, 'xc', 0, 0, tiled=True)  4.3 us
    dot_general x2, matrix products, banded(): jnp.einsum('ka,arc->krc', taps, picks, precision=lax.Precision.HIGHEST)  3.5 us
    ppermute x1, starting transfers between devices, local(): above = lax.ppermute(pair[:, tile_rows - half:], 'tile', down)  3.48 us
    dot_general x1, matrix products, separable(): jnp.einsum('bac,kcd->bkad', blocks, across, precision=lax.Precision.HIGH)  3.39 us
  transfers between devices with their start and end apart: 5, of which 1 were waited for; matrix products, arithmetic and copies ran while one was open for 21% of the time, Pallas kernels for 0%

profile of v12, /device:TPU:32, one launch (start us, length us, event | category | flops | bytes accessed | tf_op | source)
XLA Modules:
  0.0 60.8 jit_solution(10230734531975390820)
XLA Ops:
  0.0 0.0 copy-start
  0.0 6.3 %collective-permute-start = (f32[128,128]{1,0:T(8,128)}, f32[128,128]{1,0:T(8,128)S(1)}, u32[]{:S(2)}, u32[]{:S(2)}) collective-permute-start(f32[128,128]{1,0:T(8,128)} %param.10), channel_id=1, source_target_pairs={{0,8},{8,0},{1,9},{9,1},{2,10},{10,2},{3,11},{11,3},{4,12},{12,4},... | collective-permute-start | bytes 196616 | tf_op jit(solution)/shard_map/ppermute | solution.py:48
  6.3 0.7 %copy.110 = f32[1,16,6]{1,2,0:T(8,128)S(1)} copy(f32[1,16,6]{1,0,2:T(1,128)} %param.13) | data formatting | bytes 768
  7.1 0.0 copy-done
  7.1 0.0 copy-start.4
  7.1 1.7 %fusion.10 = f32[16,168,148,1]{1,0,2,3:T(8,128)S(1)} fusion(s32[148,168]{1,0:T(8,128)S(1)} %iota_subtract_fusion, f32[16,21]{1,0:T(8,128)S(1)} %copy-done), kind=kOutput, calls=%fused_computation.12 | convolution fusion | flops 100773792 | bytes 1692096 | tf_op jit(solution)/shard_map/ka,arc->krc/dot_general | solution.py:23
  8.8 0.0 copy-start.3
  8.8 0.1 broadcast_multiply_fusion.1
  8.9 0.0 copy-done.4
  8.9 1.8 %fusion.11 = f32[16,128,148,1]{1,0,2,3:T(8,128)} fusion(s32[128,148]{0,1:T(8,128)S(1)} %iota_subtract_fusion.1, f32[16,21]{1,0:T(8,128)S(1)} %copy-done.4), kind=kOutput, calls=%fused_computation.13 | convolution fusion | flops 76780032 | bytes 1289536 | tf_op jit(solution)/shard_map/ka,arc->krc/dot_general | solution.py:23
  10.7 0.0 collective-permute-done
  10.7 0.0 copy-done.3
  10.7 3.5 %collective-permute-start.1 = (f32[2,10,128]{2,1,0:T(8,128)S(1)}, f32[2,10,128]{2,1,0:T(8,128)S(1)}, u32[]{:S(2)}, u32[]{:S(2)}) collective-permute-start(f32[2,10,128]{2,1,0:T(8,128)S(1)} %get-tuple-element.39), channel_id=1, source_target_pairs={{0,16},{16,32},{32,48},{48,64},{64,80},{80,96},{96,112},{112,128},... | collective-permute-start | bytes 30728 | tf_op jit(solution)/shard_map/ppermute | solution.py:51
  14.2 4.5 %collective-permute-start.2 = (f32[2,10,128]{2,1,0:T(8,128)S(1)}, f32[2,10,128]{2,1,0:T(8,128)S(1)}, u32[]{:S(2)}, u32[]{:S(2)}) collective-permute-start(f32[2,10,128]{2,1,0:T(8,128)S(1)} %get-tuple-element.40), channel_id=1, source_target_pairs={{16,0},{32,16},{48,32},{64,48},{80,64},{96,80},{112,96},{128,112},... | collective-permute-start | bytes 30728 | tf_op jit(solution)/shard_map/ppermute | solution.py:52
  18.7 0.6 %broadcast_in_dim.14 = f32[8,16,6]{1,2,0:T(8,128)} broadcast(f32[16,6]{0,1:T(8,128)S(1)} %bitcast.161), dimensions={1,2} | broadcast | bytes 3456 | tf_op jit(solution)/shard_map/broadcast_in_dim | solution.py:53
  19.3 4.3 %all-to-all-start = ((f32[8,16,6]{1,2,0:T(8,128)}), f32[8,16,6]{1,2,0:T(8,128)S(1)}, u32[]{:S(2)}, u32[]{:S(2)}) async-start(f32[8,16,6]{1,2,0:T(8,128)} %broadcast_in_dim.14), calls=%async_computation | async-start | bytes 65536 | tf_op jit(solution)/shard_map/all_to_all | solution.py:55
  23.6 0.0 collective-permute-done.1
  23.6 0.0 collective-permute-done.2
  23.7 0.0 copy-start.1
  23.7 3.4 %fusion.3 = f32[16,148,2,148]{3,1,2,0:T(8,128)S(1)} fusion(f32[16,168,148,1]{1,0,2,3:T(8,128)S(1)} %fusion.10, f32[1,148,128]{2,1,0:T(8,128)S(1)} %get-tuple-element.38, f32[1,148,128]{2,1,0:T(8,128)S(1)} %get-tuple-element.37), kind=kOutput, calls=%fused_computation.4 | convolution fusion | flops 706833792 | bytes 4546560 | tf_op jit(solution)/shard_map/bac,kcd->bkad/dot_general | solution.py:30
  27.1 0.0 copy-done.1
  27.1 2.4 %fusion.7 = f32[2,16,128,148]{2,3,0,1:T(8,128)S(1)} fusion(f32[16,148,2,148]{3,1,2,0:T(8,128)S(1)} %fusion.3, f32[16,128,148,1]{1,0,2,3:T(8,128)S(1)} %copy-done.1), kind=kOutput, calls=%fused_computation.11 | convolution fusion | flops 538312704 | bytes 6440960 | tf_op jit(solution)/shard_map/kra,bkad->bkrd/dot_general | solution.py:31
  29.5 0.2 slice_bitcast_fusion.1
  29.7 0.0 all-to-all-done
  29.7 1.6 %convolution_bitcast_fusion = f32[6,8,128,148]{2,1,3,0:T(8,128)S(1)} fusion(f32[16,128,148]{1,2,0:T(8,128)S(1)} %get-tuple-element.34, f32[8,16,6,1]{1,2,0,3:T(8,128)S(1)} %bitcast.160), kind=kOutput, calls=%fused_computation.6 | convolution fusion | flops 87293952 | bytes 4852736 | tf_op jit(solution)/shard_map/vkt,krc->tvrc/dot_general | solution.py:70
  31.3 1.6 %convolution_bitcast_fusion.1 = f32[6,8,128,148]{2,1,0,3:T(8,128)S(1)} fusion(f32[16,128,148,1]{1,2,0,3:T(8,128)S(1)} %get-tuple-element.33, f32[8,16,6]{1,2,0:T(8,128)S(1)} %all-to-all-done), kind=kOutput, calls=%fused_computation.7 | convolution fusion | flops 87293952 | bytes 4852736 | tf_op jit(solution)/shard_map/vkt,krc->tvrc/dot_general | solution.py:70
  32.9 0.4 fusion.29
  33.3 0.4 fusion.19
  33.7 0.1 pad_maximum_fusion
  33.8 2.0 %copy.67 = f32[8,2,128,148]{2,1,3,0:T(2,128)} copy(f32[8,2,128,148]{2,0,3,1:T(8,128)S(1)} %pad_maximum_fusion) | data formatting | bytes 2424832 | tf_op jit(solution)/shard_map/stack | solution.py:72
  35.8 0.0 copy-start.2
  35.8 4.9 %all-to-all-start.1 = ((f32[8,2,128,148]{2,1,3,0:T(2,128)}), f32[8,2,128,148]{2,1,3,0:T(2,128)S(1)}, u32[]{:S(2)}, u32[]{:S(2)}) async-start(f32[8,2,128,148]{2,1,3,0:T(2,128)} %copy.67), calls=%async_computation.1 | async-start | bytes 2424832 | tf_op jit(solution)/shard_map/all_to_all | solution.py:73
  40.7 0.0 copy-start.5
  40.7 0.0 copy-done.2
  40.8 0.3 copy.70
  41.1 0.3 copy-done.5
  41.4 0.1 constant_dynamic-slice_fusion
  41.5 0.5 fusion.66
  43.3 0.6 %fusion.57 = pred[2048]{0:T(1024)(128)(4,1)S(1)} fusion(s32[]{:T(128)} %bitcast.1, s32[]{:T(128)} %bitcast), kind=kLoop, calls=%fused_computation.93 | loop fusion | flops 6144 | bytes 2056 | tf_op jit(solution)/shard_map/and | solution.py:86
  43.9 14.5 %all-to-all-done.1 = f32[8,2,128,148]{2,1,3,0:T(2,128)S(1)} async-done(((f32[8,2,128,148]{2,1,3,0:T(2,128)}), f32[8,2,128,148]{2,1,3,0:T(2,128)S(1)}, u32[]{:S(2)}, u32[]{:S(2)}) %all-to-all-start.1) | async-done | bytes 1212448 | tf_op jit(solution)/shard_map/all_to_all | solution.py:73
  58.4 0.2 copy.109
  58.7 0.1 slice.168
  58.8 0.3 copy.69
  59.2 0.3 fusion.16
  59.5 1.3 %copy.71 = f32[1,128,2048]{2,1,0:T(8,128)} copy(f32[1,128,2048]{1,2,0:T(8,128)S(1)} %fusion.16) | data formatting | bytes 2097152 | tf_op jit(solution)/shard_map/jit(_where)/select_n | solution.py:89
  (12 shorter events, 0.1 us)
Async XLA Ops:
  0.0 7.1 %copy-start = (f32[16,21]{1,0:T(8,128)S(1)}, f32[16,21]{1,0:T(8,128)}, u32[]{:S(2)}) copy-start(f32[16,21]{1,0:T(8,128)} %param.12) | copy-start | bytes 4036
  0.0 10.7 %collective-permute-start = (f32[128,128]{1,0:T(8,128)}, f32[128,128]{1,0:T(8,128)S(1)}, u32[]{:S(2)}, u32[]{:S(2)}) collective-permute-start(f32[128,128]{1,0:T(8,128)} %param.10), channel_id=1, source_target_pairs={{0,8},{8,0},{1,9},{9,1},{2,10},{10,2},{3,11},{11,3},{4,12},{12,4},... | collective-permute-start | bytes 196616 | tf_op jit(solution)/shard_map/ppermute | solution.py:48
  7.1 1.8 %copy-start.4 = (f32[16,21]{1,0:T(8,128)S(1)}, f32[16,21]{1,0:T(8,128)}, u32[]{:S(2)}) copy-start(f32[16,21]{1,0:T(8,128)} %param.11) | copy-start | bytes 4036
  8.8 2.0 %copy-start.3 = (f32[128,128]{1,0:T(8,128)S(1)}, f32[128,128]{1,0:T(8,128)}, u32[]{:S(2)}) copy-start(f32[128,128]{1,0:T(8,128)} %param.10) | copy-start | bytes 196612
  10.7 12.9 %collective-permute-start.1 = (f32[2,10,128]{2,1,0:T(8,128)S(1)}, f32[2,10,128]{2,1,0:T(8,128)S(1)}, u32[]{:S(2)}, u32[]{:S(2)}) collective-permute-start(f32[2,10,128]{2,1,0:T(8,128)S(1)} %get-tuple-element.39), channel_id=1, source_target_pairs={{0,16},{16,32},{32,48},{48,64},{64,80},{80,96},{96,112},{112,128},... | collective-permute-start | bytes 30728 | tf_op jit(solution)/shard_map/ppermute | solution.py:51
  14.2 9.4 %collective-permute-start.2 = (f32[2,10,128]{2,1,0:T(8,128)S(1)}, f32[2,10,128]{2,1,0:T(8,128)S(1)}, u32[]{:S(2)}, u32[]{:S(2)}) collective-permute-start(f32[2,10,128]{2,1,0:T(8,128)S(1)} %get-tuple-element.40), channel_id=1, source_target_pairs={{16,0},{32,16},{48,32},{64,48},{80,64},{96,80},{112,96},{128,112},... | collective-permute-start | bytes 30728 | tf_op jit(solution)/shard_map/ppermute | solution.py:52
  19.3 10.4 %all-to-all-start = ((f32[8,16,6]{1,2,0:T(8,128)}), f32[8,16,6]{1,2,0:T(8,128)S(1)}, u32[]{:S(2)}, u32[]{:S(2)}) async-start(f32[8,16,6]{1,2,0:T(8,128)} %broadcast_in_dim.14), calls=%async_computation | async-start | bytes 65536 | tf_op jit(solution)/shard_map/all_to_all | solution.py:55
  23.7 3.4 %copy-start.1 = (f32[16,128,148,1]{1,0,2,3:T(8,128)S(1)}, f32[16,128,148,1]{1,0,2,3:T(8,128)}, u32[]{:S(2)}) copy-start(f32[16,128,148,1]{1,0,2,3:T(8,128)} %fusion.11) | copy-start | bytes 3637252
  35.8 4.9 %copy-start.2 = (f32[1,128,2048]{2,1,0:T(8,128)S(1)}, f32[1,128,2048]{2,1,0:T(8,128)}, u32[]{:S(2)}) copy-start(f32[1,128,2048]{2,1,0:T(8,128)} %param.14) | copy-start | bytes 3145732
  35.8 22.6 %all-to-all-start.1 = ((f32[8,2,128,148]{2,1,3,0:T(2,128)}), f32[8,2,128,148]{2,1,3,0:T(2,128)S(1)}, u32[]{:S(2)}, u32[]{:S(2)}) async-start(f32[8,2,128,148]{2,1,3,0:T(2,128)} %copy.67), calls=%async_computation.1 | async-start | bytes 2424832 | tf_op jit(solution)/shard_map/all_to_all | solution.py:73
  40.7 0.7 %copy-start.5 = (s32[16,2]{0,1:T(2,128)S(1)}, s32[16,2]{0,1:T(2,128)}, u32[]{:S(2)}) copy-start(s32[16,2]{0,1:T(2,128)} %param.15) | copy-start | bytes 388

commit v13 on v12

--- a/solution.py
+++ b/solution.py
@@ -76,8 +76,10 @@
     left = parts[:, :, :half]
     right = parts[:, :, half + columns :]
     edge = jnp.zeros_like(left[:1])
-    core = core.at[:, :, :half].add(jnp.concatenate([edge, right[:-1]], axis=0))
-    core = core.at[:, :, columns - half :].add(jnp.concatenate([left[1:], edge], axis=0))
+    spill = ((0, 0), (0, 0), (0, columns - half))
+    core = core + jnp.pad(jnp.concatenate([edge, right[:-1]], axis=0), spill)
+    spill = ((0, 0), (0, 0), (columns - half, 0))
+    core = core + jnp.pad(jnp.concatenate([left[1:], edge], axis=0), spill)
     model = jnp.swapaxes(core, 0, 1).reshape(1, tile_rows, full_width)
 
     visit = side * group + place

time: 61.1 us -> 61.1 us (level)
  no operation moved by 1% of the time
where the time goes in v13:
time: 61.1 us; the launch traced here: 60.8 us
  starting transfers between devices  23.5 us (38%)
  waiting for transfers between devices  14.5 us (24%)
  matrix products  12.5 us (20%)
  local copies, waits for them, and re-layouts  6.63 us (11%)
  other arithmetic  2.11 us (3%)
  between operations  1.54 us (3%)
    all_to_all x1, waiting for transfers between devices, local(): parts = lax.all_to_all(models, 'xc', 0, 0, tiled=True)  14.5 us
    ppermute x1, starting transfers between devices, local(): pair = jnp.stack([template, lax.ppermute(template, 'zhi', swap)])  6.29 us
    all_to_all x1, starting transfers between devices, local(): parts = lax.all_to_all(models, 'xc', 0, 0, tiled=True)  4.92 us
    ppermute x1, starting transfers between devices, local(): below = lax.ppermute(pair[:, :half], 'tile', up)  4.47 us
    all_to_all x1, starting transfers between devices, local(): half_coeffs = lax.all_to_all(copies, 'xc', 0, 0, tiled=True)  4.3 us
    dot_general x2, matrix products, banded(): jnp.einsum('ka,arc->krc', taps, picks, precision=lax.Precision.HIGHEST)  3.5 us
    ppermute x1, starting transfers between devices, local(): above = lax.ppermute(pair[:, tile_rows - half:], 'tile', down)  3.48 us
    dot_general x1, matrix products, separable(): jnp.einsum('bac,kcd->bkad', blocks, across, precision=lax.Precision.HIGH)  3.39 us
  transfers between devices with their start and end apart: 5, of which 1 were waited for; matrix products, arithmetic and copies ran while one was open for 21% of the time, Pallas kernels for 0%

profile of v13, /device:TPU:32, one launch (start us, length us, event | category | flops | bytes accessed | tf_op | source)
XLA Modules:
  0.0 60.8 jit_solution(5622046299702326123)
XLA Ops:
  0.0 0.0 copy-start
  0.0 6.3 %collective-permute-start = (f32[128,128]{1,0:T(8,128)}, f32[128,128]{1,0:T(8,128)S(1)}, u32[]{:S(2)}, u32[]{:S(2)}) collective-permute-start(f32[128,128]{1,0:T(8,128)} %param.6), channel_id=1, source_target_pairs={{0,8},{8,0},{1,9},{9,1},{2,10},{10,2},{3,11},{11,3},{4,12},{12,4},... | collective-permute-start | bytes 196616 | tf_op jit(solution)/shard_map/ppermute | solution.py:48
  6.3 0.7 %copy.110 = f32[1,16,6]{1,2,0:T(8,128)S(1)} copy(f32[1,16,6]{1,0,2:T(1,128)} %param.9) | data formatting | bytes 768
  7.1 0.0 copy-done
  7.1 0.0 copy-start.4
  7.1 1.7 %fusion.10 = f32[16,168,148,1]{1,0,2,3:T(8,128)S(1)} fusion(s32[148,168]{1,0:T(8,128)S(1)} %iota_subtract_fusion, f32[16,21]{1,0:T(8,128)S(1)} %copy-done), kind=kOutput, calls=%fused_computation.12 | convolution fusion | flops 100773792 | bytes 1692096 | tf_op jit(solution)/shard_map/ka,arc->krc/dot_general | solution.py:23
  8.8 0.0 copy-start.3
  8.8 0.1 broadcast_multiply_fusion.1
  8.9 0.0 copy-done.4
  8.9 1.8 %fusion.11 = f32[16,128,148,1]{1,0,2,3:T(8,128)} fusion(s32[128,148]{0,1:T(8,128)S(1)} %iota_subtract_fusion.1, f32[16,21]{1,0:T(8,128)S(1)} %copy-done.4), kind=kOutput, calls=%fused_computation.13 | convolution fusion | flops 76780032 | bytes 1289536 | tf_op jit(solution)/shard_map/ka,arc->krc/dot_general | solution.py:23
  10.7 0.0 collective-permute-done
  10.7 0.0 copy-done.3
  10.7 3.5 %collective-permute-start.1 = (f32[2,10,128]{2,1,0:T(8,128)S(1)}, f32[2,10,128]{2,1,0:T(8,128)S(1)}, u32[]{:S(2)}, u32[]{:S(2)}) collective-permute-start(f32[2,10,128]{2,1,0:T(8,128)S(1)} %get-tuple-element.15), channel_id=1, source_target_pairs={{0,16},{16,32},{32,48},{48,64},{64,80},{80,96},{96,112},{112,128},... | collective-permute-start | bytes 30728 | tf_op jit(solution)/shard_map/ppermute | solution.py:51
  14.2 4.5 %collective-permute-start.2 = (f32[2,10,128]{2,1,0:T(8,128)S(1)}, f32[2,10,128]{2,1,0:T(8,128)S(1)}, u32[]{:S(2)}, u32[]{:S(2)}) collective-permute-start(f32[2,10,128]{2,1,0:T(8,128)S(1)} %get-tuple-element.16), channel_id=1, source_target_pairs={{16,0},{32,16},{48,32},{64,48},{80,64},{96,80},{112,96},{128,112},... | collective-permute-start | bytes 30728 | tf_op jit(solution)/shard_map/ppermute | solution.py:52
  18.7 0.6 %broadcast_in_dim.14 = f32[8,16,6]{1,2,0:T(8,128)} broadcast(f32[16,6]{0,1:T(8,128)S(1)} %bitcast.160), dimensions={1,2} | broadcast | bytes 3456 | tf_op jit(solution)/shard_map/broadcast_in_dim | solution.py:53
  19.3 4.3 %all-to-all-start = ((f32[8,16,6]{1,2,0:T(8,128)}), f32[8,16,6]{1,2,0:T(8,128)S(1)}, u32[]{:S(2)}, u32[]{:S(2)}) async-start(f32[8,16,6]{1,2,0:T(8,128)} %broadcast_in_dim.14), calls=%async_computation | async-start | bytes 65536 | tf_op jit(solution)/shard_map/all_to_all | solution.py:55
  23.6 0.0 collective-permute-done.1
  23.6 0.0 collective-permute-done.2
  23.7 0.0 copy-start.1
  23.7 3.4 %fusion.3 = f32[16,148,2,148]{3,1,2,0:T(8,128)S(1)} fusion(f32[16,168,148,1]{1,0,2,3:T(8,128)S(1)} %fusion.10, f32[1,148,128]{2,1,0:T(8,128)S(1)} %get-tuple-element.14, f32[1,148,128]{2,1,0:T(8,128)S(1)} %get-tuple-element.13), kind=kOutput, calls=%fused_computation.4 | convolution fusion | flops 706833792 | bytes 4546560 | tf_op jit(solution)/shard_map/bac,kcd->bkad/dot_general | solution.py:30
  27.1 0.0 copy-done.1
  27.1 2.4 %fusion.7 = f32[2,16,128,148]{2,3,0,1:T(8,128)S(1)} fusion(f32[16,148,2,148]{3,1,2,0:T(8,128)S(1)} %fusion.3, f32[16,128,148,1]{1,0,2,3:T(8,128)S(1)} %copy-done.1), kind=kOutput, calls=%fused_computation.11 | convolution fusion | flops 538312704 | bytes 6440960 | tf_op jit(solution)/shard_map/kra,bkad->bkrd/dot_general | solution.py:31
  29.5 0.2 slice_bitcast_fusion.1
  29.7 0.0 all-to-all-done
  29.7 1.6 %convolution_bitcast_fusion = f32[6,8,128,148]{2,1,3,0:T(8,128)S(1)} fusion(f32[16,128,148]{1,2,0:T(8,128)S(1)} %get-tuple-element.10, f32[8,16,6,1]{1,2,0,3:T(8,128)S(1)} %bitcast.159), kind=kOutput, calls=%fused_computation.6 | convolution fusion | flops 87293952 | bytes 4852736 | tf_op jit(solution)/shard_map/vkt,krc->tvrc/dot_general | solution.py:70
  31.3 1.6 %convolution_bitcast_fusion.1 = f32[6,8,128,148]{2,1,0,3:T(8,128)S(1)} fusion(f32[16,128,148,1]{1,2,0,3:T(8,128)S(1)} %get-tuple-element.9, f32[8,16,6]{1,2,0:T(8,128)S(1)} %all-to-all-done), kind=kOutput, calls=%fused_computation.7 | convolution fusion | flops 87293952 | bytes 4852736 | tf_op jit(solution)/shard_map/vkt,krc->tvrc/dot_general | solution.py:70
  32.9 0.4 fusion.30
  33.3 0.4 fusion.20
  33.7 0.1 pad_maximum_fusion
  33.8 2.0 %copy.67 = f32[8,2,128,148]{2,1,3,0:T(2,128)} copy(f32[8,2,128,148]{2,0,3,1:T(8,128)S(1)} %pad_maximum_fusion) | data formatting | bytes 2424832 | tf_op jit(solution)/shard_map/stack | solution.py:72
  35.8 0.0 copy-start.2
  35.8 4.9 %all-to-all-start.1 = ((f32[8,2,128,148]{2,1,3,0:T(2,128)}), f32[8,2,128,148]{2,1,3,0:T(2,128)S(1)}, u32[]{:S(2)}, u32[]{:S(2)}) async-start(f32[8,2,128,148]{2,1,3,0:T(2,128)} %copy.67), calls=%async_computation.1 | async-start | bytes 2424832 | tf_op jit(solution)/shard_map/all_to_all | solution.py:73
  40.7 0.0 copy-start.5
  40.7 0.0 copy-done.2
  40.8 0.3 copy.70
  41.1 0.3 copy-done.5
  41.4 0.1 constant_dynamic-slice_fusion
  41.5 0.5 fusion.65
  43.3 0.6 %fusion.56 = pred[2048]{0:T(1024)(128)(4,1)S(1)} fusion(s32[]{:T(128)} %bitcast.1, s32[]{:T(128)} %bitcast), kind=kLoop, calls=%fused_computation.92 | loop fusion | flops 6144 | bytes 2056 | tf_op jit(solution)/shard_map/and | solution.py:88
  43.9 14.5 %all-to-all-done.1 = f32[8,2,128,148]{2,1,3,0:T(2,128)S(1)} async-done(((f32[8,2,128,148]{2,1,3,0:T(2,128)}), f32[8,2,128,148]{2,1,3,0:T(2,128)S(1)}, u32[]{:S(2)}, u32[]{:S(2)}) %all-to-all-start.1) | async-done | bytes 1212448 | tf_op jit(solution)/shard_map/all_to_all | solution.py:73
  58.4 0.2 copy.109
  58.7 0.1 fusion.16
  58.8 0.3 copy.69
  59.1 0.3 fusion.17
  59.5 1.3 %copy.71 = f32[1,128,2048]{2,1,0:T(8,128)} copy(f32[1,128,2048]{1,2,0:T(8,128)S(1)} %fusion.17) | data formatting | bytes 2097152 | tf_op jit(solution)/shard_map/jit(_where)/select_n | solution.py:91
  (10 shorter events, 0.1 us)
Async XLA Ops:
  0.0 7.1 %copy-start = (f32[16,21]{1,0:T(8,128)S(1)}, f32[16,21]{1,0:T(8,128)}, u32[]{:S(2)}) copy-start(f32[16,21]{1,0:T(8,128)} %param.8) | copy-start | bytes 4036
  0.0 10.7 %collective-permute-start = (f32[128,128]{1,0:T(8,128)}, f32[128,128]{1,0:T(8,128)S(1)}, u32[]{:S(2)}, u32[]{:S(2)}) collective-permute-start(f32[128,128]{1,0:T(8,128)} %param.6), channel_id=1, source_target_pairs={{0,8},{8,0},{1,9},{9,1},{2,10},{10,2},{3,11},{11,3},{4,12},{12,4},... | collective-permute-start | bytes 196616 | tf_op jit(solution)/shard_map/ppermute | solution.py:48
  7.1 1.8 %copy-start.4 = (f32[16,21]{1,0:T(8,128)S(1)}, f32[16,21]{1,0:T(8,128)}, u32[]{:S(2)}) copy-start(f32[16,21]{1,0:T(8,128)} %param.7) | copy-start | bytes 4036
  8.8 2.0 %copy-start.3 = (f32[128,128]{1,0:T(8,128)S(1)}, f32[128,128]{1,0:T(8,128)}, u32[]{:S(2)}) copy-start(f32[128,128]{1,0:T(8,128)} %param.6) | copy-start | bytes 196612
  10.7 12.9 %collective-permute-start.1 = (f32[2,10,128]{2,1,0:T(8,128)S(1)}, f32[2,10,128]{2,1,0:T(8,128)S(1)}, u32[]{:S(2)}, u32[]{:S(2)}) collective-permute-start(f32[2,10,128]{2,1,0:T(8,128)S(1)} %get-tuple-element.15), channel_id=1, source_target_pairs={{0,16},{16,32},{32,48},{48,64},{64,80},{80,96},{96,112},{112,128},... | collective-permute-start | bytes 30728 | tf_op jit(solution)/shard_map/ppermute | solution.py:51
  14.2 9.4 %collective-permute-start.2 = (f32[2,10,128]{2,1,0:T(8,128)S(1)}, f32[2,10,128]{2,1,0:T(8,128)S(1)}, u32[]{:S(2)}, u32[]{:S(2)}) collective-permute-start(f32[2,10,128]{2,1,0:T(8,128)S(1)} %get-tuple-element.16), channel_id=1, source_target_pairs={{16,0},{32,16},{48,32},{64,48},{80,64},{96,80},{112,96},{128,112},... | collective-permute-start | bytes 30728 | tf_op jit(solution)/shard_map/ppermute | solution.py:52
  19.3 10.4 %all-to-all-start = ((f32[8,16,6]{1,2,0:T(8,128)}), f32[8,16,6]{1,2,0:T(8,128)S(1)}, u32[]{:S(2)}, u32[]{:S(2)}) async-start(f32[8,16,6]{1,2,0:T(8,128)} %broadcast_in_dim.14), calls=%async_computation | async-start | bytes 65536 | tf_op jit(solution)/shard_map/all_to_all | solution.py:55
  23.7 3.4 %copy-start.1 = (f32[16,128,148,1]{1,0,2,3:T(8,128)S(1)}, f32[16,128,148,1]{1,0,2,3:T(8,128)}, u32[]{:S(2)}) copy-start(f32[16,128,148,1]{1,0,2,3:T(8,128)} %fusion.11) | copy-start | bytes 3637252
  35.8 4.9 %copy-start.2 = (f32[1,128,2048]{2,1,0:T(8,128)S(1)}, f32[1,128,2048]{2,1,0:T(8,128)}, u32[]{:S(2)}) copy-start(f32[1,128,2048]{2,1,0:T(8,128)} %param.10) | copy-start | bytes 3145732
  35.8 22.6 %all-to-all-start.1 = ((f32[8,2,128,148]{2,1,3,0:T(2,128)}), f32[8,2,128,148]{2,1,3,0:T(2,128)S(1)}, u32[]{:S(2)}, u32[]{:S(2)}) async-start(f32[8,2,128,148]{2,1,3,0:T(2,128)} %copy.67), calls=%async_computation.1 | async-start | bytes 2424832 | tf_op jit(solution)/shard_map/all_to_all | solution.py:73
  40.7 0.7 %copy-start.5 = (s32[16,2]{0,1:T(2,128)S(1)}, s32[16,2]{0,1:T(2,128)}, u32[]{:S(2)}) copy-start(s32[16,2]{0,1:T(2,128)} %param.11) | copy-start | bytes 388

commit v14 on v12

--- a/solution.py
+++ b/solution.py
@@ -27,8 +27,8 @@
     reach = row_taps.shape[1]
     down = banded(row_taps, tile_rows, tile_rows + reach - 1)
     across = jnp.swapaxes(banded(col_taps, span, span + reach - 1), 1, 2)
-    passed = jnp.einsum("bac,kcd->bkad", blocks, across, precision=lax.Precision.HIGH)
-    return jnp.einsum("kra,bkad->bkrd", down, passed, precision=lax.Precision.HIGH)
+    passed = jnp.einsum("bac,kcd->bkad", blocks, across, precision=lax.Precision.HIGHEST)
+    return jnp.einsum("kra,bkad->bkrd", down, passed, precision=lax.Precision.HIGHEST)
 
 
 def local(template, row_taps, col_taps, coeffs, visits, boxes):
@@ -67,7 +67,7 @@
     for b in range(halves):
         start = (b * group + place) * columns - half
         x = coordinate(start, span, full_width)[None, :]
-        w = jnp.einsum("vkt,krc->tvrc", half_coeffs, basis[b], precision=lax.Precision.HIGH)
+        w = jnp.einsum("vkt,krc->tvrc", half_coeffs, basis[b], precision=lax.Precision.HIGHEST)
         models.append(w[0] + x * w[1] + y * w[2] + (x * x) * w[3] + (x * y) * w[4] + (y * y) * w[5])
     models = jnp.stack(models, axis=1)
     parts = lax.all_to_all(models, "xc", 0, 0, tiled=True)

time: 61.1 us -> 69.2 us (1.13)
  matrix products: 12.5 us -> 20.5 us
    dot_general x2, matrix products: 5.81 us -> 10.7 us  [the longest x1 5.75 us: separable(): jnp.einsum('bac,kcd->bkad', blocks, across, precision=lax.Precision.HIGHEST)]
    dot_general x2, matrix products: 3.18 us -> 6.29 us  [local(): jnp.einsum('vkt,krc->tvrc', half_coeffs, basis[b], precision=lax.Precisio...]
  transfers between devices with their start and end apart: 5 -> 5, of which waited for: 1 -> 1; matrix products, arithmetic and copies ran while one was open for 21% -> 25% of each run, Pallas kernels for 0% -> 0%
where the time goes in v14:
time: 69.2 us; the launch traced here: 68.9 us
  starting transfers between devices  23.5 us (34%)
  matrix products  20.5 us (30%)
  waiting for transfers between devices  14.5 us (21%)
  local copies, waits for them, and re-layouts  6.7 us (10%)
  other arithmetic  2.06 us (3%)
  between operations  1.56 us (2%)
    all_to_all x1, waiting for transfers between devices, local(): parts = lax.all_to_all(models, 'xc', 0, 0, tiled=True)  14.5 us
    ppermute x1, starting transfers between devices, local(): pair = jnp.stack([template, lax.ppermute(template, 'zhi', swap)])  6.29 us
    dot_general x2, matrix products, local(): jnp.einsum('vkt,krc->tvrc', half_coeffs, basis[b], precision=lax.Precisio...  6.29 us
    dot_general x1, matrix products, separable(): jnp.einsum('bac,kcd->bkad', blocks, across, precision=lax.Precision.HIGHEST)  5.75 us
    dot_general x1, matrix products, separable(): jnp.einsum('kra,bkad->bkrd', down, passed, precision=lax.Precision.HIGHEST)  4.99 us
    all_to_all x1, starting transfers between devices, local(): parts = lax.all_to_all(models, 'xc', 0, 0, tiled=True)  4.93 us
    ppermute x1, starting transfers between devices, local(): below = lax.ppermute(pair[:, :half], 'tile', up)  4.47 us
    all_to_all x1, starting transfers between devices, local(): half_coeffs = lax.all_to_all(copies, 'xc', 0, 0, tiled=True)  4.3 us
  transfers between devices with their start and end apart: 5, of which 1 were waited for; matrix products, arithmetic and copies ran while one was open for 25% of the time, Pallas kernels for 0%

profile of v14, /device:TPU:32, one launch (start us, length us, event | category | flops | bytes accessed | tf_op | source)
XLA Modules:
  0.0 68.9 jit_solution(10565558432116131502)
XLA Ops:
  0.0 0.0 copy-start
  0.0 6.3 %collective-permute-start = (f32[128,128]{1,0:T(8,128)}, f32[128,128]{1,0:T(8,128)S(1)}, u32[]{:S(2)}, u32[]{:S(2)}) collective-permute-start(f32[128,128]{1,0:T(8,128)} %param.10), channel_id=1, source_target_pairs={{0,8},{8,0},{1,9},{9,1},{2,10},{10,2},{3,11},{11,3},{4,12},{12,4},... | collective-permute-start | bytes 196616 | tf_op jit(solution)/shard_map/ppermute | solution.py:48
  6.3 0.7 copy.110
  7.1 0.0 copy-done
  7.1 0.0 copy-start.4
  7.1 1.7 %fusion.10 = f32[16,168,148,1]{1,0,2,3:T(8,128)S(1)} fusion(s32[148,168]{1,0:T(8,128)S(1)} %iota_subtract_fusion, f32[16,21]{1,0:T(8,128)S(1)} %copy-done), kind=kOutput, calls=%fused_computation.12 | convolution fusion | flops 100773792 | bytes 1692096 | tf_op jit(solution)/shard_map/ka,arc->krc/dot_general | solution.py:23
  8.8 0.0 copy-start.3
  8.8 0.1 broadcast_multiply_fusion.1
  8.9 0.0 copy-done.4
  8.9 1.8 %fusion.11 = f32[16,128,148,1]{1,0,2,3:T(8,128)} fusion(s32[128,148]{0,1:T(8,128)S(1)} %iota_subtract_fusion.1, f32[16,21]{1,0:T(8,128)S(1)} %copy-done.4), kind=kOutput, calls=%fused_computation.13 | convolution fusion | flops 76780032 | bytes 1289536 | tf_op jit(solution)/shard_map/ka,arc->krc/dot_general | solution.py:23
  10.7 0.0 collective-permute-done
  10.7 0.0 copy-done.3
  10.7 3.5 %collective-permute-start.1 = (f32[2,10,128]{2,1,0:T(8,128)S(1)}, f32[2,10,128]{2,1,0:T(8,128)S(1)}, u32[]{:S(2)}, u32[]{:S(2)}) collective-permute-start(f32[2,10,128]{2,1,0:T(8,128)S(1)} %get-tuple-element.39), channel_id=1, source_target_pairs={{0,16},{16,32},{32,48},{48,64},{64,80},{80,96},{96,112},{112,128},... | collective-permute-start | bytes 30728 | tf_op jit(solution)/shard_map/ppermute | solution.py:51
  14.2 4.5 %collective-permute-start.2 = (f32[2,10,128]{2,1,0:T(8,128)S(1)}, f32[2,10,128]{2,1,0:T(8,128)S(1)}, u32[]{:S(2)}, u32[]{:S(2)}) collective-permute-start(f32[2,10,128]{2,1,0:T(8,128)S(1)} %get-tuple-element.40), channel_id=1, source_target_pairs={{16,0},{32,16},{48,32},{64,48},{80,64},{96,80},{112,96},{128,112},... | collective-permute-start | bytes 30728 | tf_op jit(solution)/shard_map/ppermute | solution.py:52
  18.7 0.6 broadcast_in_dim.14
  19.3 4.3 %all-to-all-start = ((f32[8,16,6]{1,2,0:T(8,128)}), f32[8,16,6]{1,2,0:T(8,128)S(1)}, u32[]{:S(2)}, u32[]{:S(2)}) async-start(f32[8,16,6]{1,2,0:T(8,128)} %broadcast_in_dim.14), calls=%async_computation | async-start | bytes 65536 | tf_op jit(solution)/shard_map/all_to_all | solution.py:55
  23.6 0.0 collective-permute-done.1
  23.6 0.0 collective-permute-done.2
  23.7 0.0 copy-start.1
  23.7 5.7 %fusion.3 = f32[16,148,2,148]{3,1,2,0:T(8,128)S(1)} fusion(f32[16,168,148,1]{1,0,2,3:T(8,128)S(1)} %fusion.10, f32[1,148,128]{2,1,0:T(8,128)S(1)} %get-tuple-element.38, f32[1,148,128]{2,1,0:T(8,128)S(1)} %get-tuple-element.37), kind=kOutput, calls=%fused_computation.4 | convolution fusion | flops 1413369216 | bytes 4546560 | tf_op jit(solution)/shard_map/bac,kcd->bkad/dot_general | solution.py:30
  29.5 0.0 copy-done.1
  29.5 5.0 %fusion.7 = f32[2,16,128,148]{2,3,0,1:T(8,128)S(1)} fusion(f32[16,148,2,148]{3,1,2,0:T(8,128)S(1)} %fusion.3, f32[16,128,148,1]{1,0,2,3:T(8,128)S(1)} %copy-done.1), kind=kOutput, calls=%fused_computation.11 | convolution fusion | flops 1076625408 | bytes 6440960 | tf_op jit(solution)/shard_map/kra,bkad->bkrd/dot_general | solution.py:31
  34.5 0.2 slice_bitcast_fusion.1
  34.6 0.0 all-to-all-done
  34.7 3.3 %convolution_bitcast_fusion = f32[6,8,128,148]{2,1,3,0:T(8,128)S(1)} fusion(f32[16,128,148]{1,2,0:T(8,128)S(1)} %get-tuple-element.34, f32[8,16,6,1]{1,2,0,3:T(8,128)S(1)} %bitcast.160), kind=kOutput, calls=%fused_computation.6 | convolution fusion | flops 174587904 | bytes 4852736 | tf_op jit(solution)/shard_map/vkt,krc->tvrc/dot_general | solution.py:70
  37.9 3.0 %convolution_bitcast_fusion.1 = f32[6,8,128,148]{2,1,0,3:T(8,128)S(1)} fusion(f32[16,128,148,1]{1,2,0,3:T(8,128)S(1)} %get-tuple-element.33, f32[8,16,6]{1,2,0:T(8,128)S(1)} %all-to-all-done), kind=kOutput, calls=%fused_computation.7 | convolution fusion | flops 174587904 | bytes 4852736 | tf_op jit(solution)/shard_map/vkt,krc->tvrc/dot_general | solution.py:70
  41.0 0.4 fusion.29
  41.4 0.4 fusion.19
  41.8 0.1 pad_maximum_fusion
  41.9 2.0 %copy.67 = f32[8,2,128,148]{2,1,3,0:T(2,128)} copy(f32[8,2,128,148]{2,0,3,1:T(8,128)S(1)} %pad_maximum_fusion) | data formatting | bytes 2424832 | tf_op jit(solution)/shard_map/stack | solution.py:72
  43.8 0.0 copy-start.2
  43.8 4.9 %all-to-all-start.1 = ((f32[8,2,128,148]{2,1,3,0:T(2,128)}), f32[8,2,128,148]{2,1,3,0:T(2,128)S(1)}, u32[]{:S(2)}, u32[]{:S(2)}) async-start(f32[8,2,128,148]{2,1,3,0:T(2,128)} %copy.67), calls=%async_computation.1 | async-start | bytes 2424832 | tf_op jit(solution)/shard_map/all_to_all | solution.py:73
  48.8 0.0 copy-start.5
  48.8 0.0 copy-done.2
  48.8 0.3 copy.70
  49.1 0.3 copy-done.5
  49.5 0.1 constant_dynamic-slice_fusion
  49.5 0.5 fusion.66
  51.3 0.6 fusion.57
  51.9 14.5 %all-to-all-done.1 = f32[8,2,128,148]{2,1,3,0:T(2,128)S(1)} async-done(((f32[8,2,128,148]{2,1,3,0:T(2,128)}), f32[8,2,128,148]{2,1,3,0:T(2,128)S(1)}, u32[]{:S(2)}, u32[]{:S(2)}) %all-to-all-start.1) | async-done | bytes 1212448 | tf_op jit(solution)/shard_map/all_to_all | solution.py:73
  66.5 0.2 copy.109
  66.7 0.1 slice.168
  66.9 0.3 copy.69
  67.2 0.3 fusion.16
  67.5 1.3 %copy.71 = f32[1,128,2048]{2,1,0:T(8,128)} copy(f32[1,128,2048]{1,2,0:T(8,128)S(1)} %fusion.16) | data formatting | bytes 2097152 | tf_op jit(solution)/shard_map/jit(_where)/select_n | solution.py:89
  (12 shorter events, 0.1 us)
Async XLA Ops:
  0.0 7.1 %copy-start = (f32[16,21]{1,0:T(8,128)S(1)}, f32[16,21]{1,0:T(8,128)}, u32[]{:S(2)}) copy-start(f32[16,21]{1,0:T(8,128)} %param.12) | copy-start | bytes 4036
  0.0 10.7 %collective-permute-start = (f32[128,128]{1,0:T(8,128)}, f32[128,128]{1,0:T(8,128)S(1)}, u32[]{:S(2)}, u32[]{:S(2)}) collective-permute-start(f32[128,128]{1,0:T(8,128)} %param.10), channel_id=1, source_target_pairs={{0,8},{8,0},{1,9},{9,1},{2,10},{10,2},{3,11},{11,3},{4,12},{12,4},... | collective-permute-start | bytes 196616 | tf_op jit(solution)/shard_map/ppermute | solution.py:48
  7.1 1.8 %copy-start.4 = (f32[16,21]{1,0:T(8,128)S(1)}, f32[16,21]{1,0:T(8,128)}, u32[]{:S(2)}) copy-start(f32[16,21]{1,0:T(8,128)} %param.11) | copy-start | bytes 4036
  8.8 2.0 %copy-start.3 = (f32[128,128]{1,0:T(8,128)S(1)}, f32[128,128]{1,0:T(8,128)}, u32[]{:S(2)}) copy-start(f32[128,128]{1,0:T(8,128)} %param.10) | copy-start | bytes 196612
  10.7 12.9 %collective-permute-start.1 = (f32[2,10,128]{2,1,0:T(8,128)S(1)}, f32[2,10,128]{2,1,0:T(8,128)S(1)}, u32[]{:S(2)}, u32[]{:S(2)}) collective-permute-start(f32[2,10,128]{2,1,0:T(8,128)S(1)} %get-tuple-element.39), channel_id=1, source_target_pairs={{0,16},{16,32},{32,48},{48,64},{64,80},{80,96},{96,112},{112,128},... | collective-permute-start | bytes 30728 | tf_op jit(solution)/shard_map/ppermute | solution.py:51
  14.2 9.4 %collective-permute-start.2 = (f32[2,10,128]{2,1,0:T(8,128)S(1)}, f32[2,10,128]{2,1,0:T(8,128)S(1)}, u32[]{:S(2)}, u32[]{:S(2)}) collective-permute-start(f32[2,10,128]{2,1,0:T(8,128)S(1)} %get-tuple-element.40), channel_id=1, source_target_pairs={{16,0},{32,16},{48,32},{64,48},{80,64},{96,80},{112,96},{128,112},... | collective-permute-start | bytes 30728 | tf_op jit(solution)/shard_map/ppermute | solution.py:52
  19.3 15.3 %all-to-all-start = ((f32[8,16,6]{1,2,0:T(8,128)}), f32[8,16,6]{1,2,0:T(8,128)S(1)}, u32[]{:S(2)}, u32[]{:S(2)}) async-start(f32[8,16,6]{1,2,0:T(8,128)} %broadcast_in_dim.14), calls=%async_computation | async-start | bytes 65536 | tf_op jit(solution)/shard_map/all_to_all | solution.py:55
  23.7 5.8 %copy-start.1 = (f32[16,128,148,1]{1,0,2,3:T(8,128)S(1)}, f32[16,128,148,1]{1,0,2,3:T(8,128)}, u32[]{:S(2)}) copy-start(f32[16,128,148,1]{1,0,2,3:T(8,128)} %fusion.11) | copy-start | bytes 3637252
  43.8 4.9 %copy-start.2 = (f32[1,128,2048]{2,1,0:T(8,128)S(1)}, f32[1,128,2048]{2,1,0:T(8,128)}, u32[]{:S(2)}) copy-start(f32[1,128,2048]{2,1,0:T(8,128)} %param.14) | copy-start | bytes 3145732
  43.8 22.6 %all-to-all-start.1 = ((f32[8,2,128,148]{2,1,3,0:T(2,128)}), f32[8,2,128,148]{2,1,3,0:T(2,128)S(1)}, u32[]{:S(2)}, u32[]{:S(2)}) async-start(f32[8,2,128,148]{2,1,3,0:T(2,128)} %copy.67), calls=%async_computation.1 | async-start | bytes 2424832 | tf_op jit(solution)/shard_map/all_to_all | solution.py:73
  48.8 0.7 copy-start.5

commit v15 on v12

--- a/solution.py
+++ b/solution.py
@@ -44,18 +44,16 @@
     total_rows = tile_rows * tiles
 
 
-    swap = [(h, halves - 1 - h) for h in range(halves)]
-    pair = jnp.stack([template, lax.ppermute(template, "zhi", swap)])
     down = [(i, i + 1) for i in range(tiles - 1)]
     up = [(i + 1, i) for i in range(tiles - 1)]
-    above = lax.ppermute(pair[:, tile_rows - half :], "tile", down)
-    below = lax.ppermute(pair[:, :half], "tile", up)
+    above = lax.ppermute(template[tile_rows - half :], "tile", down)
+    below = lax.ppermute(template[:half], "tile", up)
+    own = jnp.concatenate([above, template, below], axis=0)
+    swap = [(h, halves - 1 - h) for h in range(halves)]
+    other = lax.ppermute(own, "zhi", swap)
     copies = jnp.broadcast_to(coeffs, (group,) + coeffs.shape[1:])
-    copies, pair = lax.optimization_barrier((copies, pair))
+    copies, own = lax.optimization_barrier((copies, own))
     half_coeffs = lax.all_to_all(copies, "xc", 0, 0, tiled=True)
-    extended = jnp.concatenate([above, pair, below], axis=1)
-    own = extended[0]
-    other = extended[1]
     first = side == 0
     blocks = jnp.stack([jnp.where(first, own, other), jnp.where(first, other, own)])
     blocks = jnp.pad(blocks, ((0, 0), (0, 0), (2 * half, 2 * half)))

time: 61.1 us -> 62.5 us (1.023)
  the two profiles are of different devices: /device:TPU:32 before, /device:TPU:24 now
where the time goes in v15:
time: 62.5 us; the launch traced here: 62.1 us
  starting transfers between devices  21.4 us (34%)
  waiting for transfers between devices  17.7 us (28%)
  matrix products  12.5 us (20%)
  local copies, waits for them, and re-layouts  6.79 us (11%)
  other arithmetic  2.07 us (3%)
  between operations  1.62 us (3%)
    all_to_all x1, waiting for transfers between devices, local(): parts = lax.all_to_all(models, 'xc', 0, 0, tiled=True)  14.4 us
    ppermute x1, starting transfers between devices, local(): other = lax.ppermute(own, 'zhi', swap)  6.38 us
    all_to_all x1, starting transfers between devices, local(): parts = lax.all_to_all(models, 'xc', 0, 0, tiled=True)  4.93 us
    all_to_all x1, starting transfers between devices, local(): half_coeffs = lax.all_to_all(copies, 'xc', 0, 0, tiled=True)  4.3 us
    dot_general x2, matrix products, banded(): jnp.einsum('ka,arc->krc', taps, picks, precision=lax.Precision.HIGHEST)  3.5 us
    ppermute x1, starting transfers between devices, local(): above = lax.ppermute(template[tile_rows - half:], 'tile', down)  3.47 us
    dot_general x1, matrix products, separable(): jnp.einsum('bac,kcd->bkad', blocks, across, precision=lax.Precision.HIGH)  3.39 us
    ppermute x1, waiting for transfers between devices, local(): below = lax.ppermute(template[:half], 'tile', up)  3.3 us
  transfers between devices with their start and end apart: 5, of which 2 were waited for; matrix products, arithmetic and copies ran while one was open for 19% of the time, Pallas kernels for 0%

profile of v15, /device:TPU:24, one launch (start us, length us, event | category | flops | bytes accessed | tf_op | source)
XLA Modules:
  0.0 62.1 jit_solution(14326641393097014567)
XLA Ops:
  0.0 0.0 copy-start
  0.0 0.7 %fusion.64 = (f32[10,128]{1,0:T(8,128)S(1)}, f32[10,128]{1,0:T(8,128)S(1)}) fusion(f32[128,128]{1,0:T(8,128)} %param.10), kind=kLoop, calls=%fused_computation.100 | loop fusion | bytes 20480 | tf_op jit(solution)/shard_map/slice | solution.py:49
  0.7 3.5 %collective-permute-start = (f32[10,128]{1,0:T(8,128)S(1)}, f32[10,128]{1,0:T(8,128)S(1)}, u32[]{:S(2)}, u32[]{:S(2)}) collective-permute-start(f32[10,128]{1,0:T(8,128)S(1)} %get-tuple-element.39), channel_id=1, source_target_pairs={{0,16},{16,32},{32,48},{48,64},{64,80},{80,96},{96,112},{112,128},... | collective-permute-start | bytes 15368 | tf_op jit(solution)/shard_map/ppermute | solution.py:49
  4.2 2.4 %collective-permute-start.1 = (f32[10,128]{1,0:T(8,128)S(1)}, f32[10,128]{1,0:T(8,128)S(1)}, u32[]{:S(2)}, u32[]{:S(2)}) collective-permute-start(f32[10,128]{1,0:T(8,128)S(1)} %get-tuple-element.40), channel_id=1, source_target_pairs={{16,0},{32,16},{48,32},{64,48},{80,64},{96,80},{112,96},{128,112},... | collective-permute-start | bytes 15368 | tf_op jit(solution)/shard_map/ppermute | solution.py:50
  6.7 0.0 copy-done
  6.7 0.0 copy-start.5
  6.7 0.0 copy-start.3
  6.7 0.0 copy-start.4
  6.7 1.7 %fusion.10 = f32[16,168,148,1]{1,0,2,3:T(8,128)S(1)} fusion(s32[148,168]{1,0:T(8,128)S(1)} %iota_subtract_fusion, f32[16,21]{1,0:T(8,128)S(1)} %copy-done), kind=kOutput, calls=%fused_computation.12 | convolution fusion | flops 100773792 | bytes 1692096 | tf_op jit(solution)/shard_map/ka,arc->krc/dot_general | solution.py:23
  8.4 0.1 broadcast_multiply_fusion.1
  8.5 0.0 copy-done.5
  8.6 0.0 collective-permute-done
  8.6 3.3 %collective-permute-done.1 = f32[10,128]{1,0:T(8,128)S(1)} collective-permute-done((f32[10,128]{1,0:T(8,128)S(1)}, f32[10,128]{1,0:T(8,128)S(1)}, u32[]{:S(2)}, u32[]{:S(2)}) %collective-permute-start.1) | collective-permute-done | bytes 5152 | tf_op jit(solution)/shard_map/ppermute | solution.py:50
  11.9 0.0 copy-done.3
  11.9 6.4 %collective-permute-start.2 = (f32[148,128]{1,0:T(8,128)S(1)}, f32[148,128]{1,0:T(8,128)S(1)}, u32[]{:S(2)}, u32[]{:S(2)}) collective-permute-start(f32[148,128]{1,0:T(8,128)S(1)} %pad_maximum_fusion.1), channel_id=1, source_target_pairs={{0,8},{8,0},{1,9},{9,1},{2,10},{10,2},{3,11},{11,3},{4,12},{12,4},... | collective-permute-start | bytes 227336 | tf_op jit(solution)/shard_map/ppermute | solution.py:53
  18.3 0.0 copy-done.4
  18.3 1.8 %fusion.11 = f32[16,128,148,1]{1,0,2,3:T(8,128)} fusion(s32[128,148]{0,1:T(8,128)S(1)} %iota_subtract_fusion.1, f32[16,21]{1,0:T(8,128)S(1)} %copy-done.4), kind=kOutput, calls=%fused_computation.13 | convolution fusion | flops 76780032 | bytes 1289536 | tf_op jit(solution)/shard_map/ka,arc->krc/dot_general | solution.py:23
  20.1 0.6 broadcast_in_dim.14
  20.7 4.3 %all-to-all-start = ((f32[8,16,6]{1,2,0:T(8,128)}), f32[8,16,6]{1,2,0:T(8,128)S(1)}, u32[]{:S(2)}, u32[]{:S(2)}) async-start(f32[8,16,6]{1,2,0:T(8,128)} %broadcast_in_dim.14), calls=%async_computation | async-start | bytes 65536 | tf_op jit(solution)/shard_map/all_to_all | solution.py:56
  25.0 0.0 collective-permute-done.2
  25.0 0.0 copy-start.1
  25.0 3.4 %fusion.3 = f32[16,148,2,148]{3,1,2,0:T(8,128)S(1)} fusion(f32[16,168,148,1]{1,0,2,3:T(8,128)S(1)} %fusion.10, f32[1,148,128]{2,1,0:T(8,128)S(1)} %get-tuple-element.38, f32[1,148,128]{2,1,0:T(8,128)S(1)} %get-tuple-element.37), kind=kOutput, calls=%fused_computation.4 | convolution fusion | flops 706833792 | bytes 4546560 | tf_op jit(solution)/shard_map/bac,kcd->bkad/dot_general | solution.py:30
  28.4 0.0 copy-done.1
  28.4 2.4 %fusion.7 = f32[2,16,128,148]{2,3,0,1:T(8,128)S(1)} fusion(f32[16,148,2,148]{3,1,2,0:T(8,128)S(1)} %fusion.3, f32[16,128,148,1]{1,0,2,3:T(8,128)S(1)} %copy-done.1), kind=kOutput, calls=%fused_computation.11 | convolution fusion | flops 538312704 | bytes 6440960 | tf_op jit(solution)/shard_map/kra,bkad->bkrd/dot_general | solution.py:31
  30.9 0.2 slice_bitcast_fusion.1
  31.0 0.0 all-to-all-done
  31.1 1.6 %convolution_bitcast_fusion = f32[6,8,128,148]{2,1,3,0:T(8,128)S(1)} fusion(f32[16,128,148]{1,2,0:T(8,128)S(1)} %get-tuple-element.34, f32[8,16,6,1]{1,2,0,3:T(8,128)S(1)} %bitcast.158), kind=kOutput, calls=%fused_computation.6 | convolution fusion | flops 87293952 | bytes 4852736 | tf_op jit(solution)/shard_map/vkt,krc->tvrc/dot_general | solution.py:68
  32.7 0.4 fusion.19
  33.1 1.6 %convolution_bitcast_fusion.1 = f32[6,8,128,148]{2,1,0,3:T(8,128)S(1)} fusion(f32[16,128,148,1]{1,2,0,3:T(8,128)S(1)} %get-tuple-element.33, f32[8,16,6]{1,2,0:T(8,128)S(1)} %all-to-all-done), kind=kOutput, calls=%fused_computation.7 | convolution fusion | flops 87293952 | bytes 4852736 | tf_op jit(solution)/shard_map/vkt,krc->tvrc/dot_general | solution.py:68
  34.7 0.4 fusion.29
  35.1 0.1 pad_maximum_fusion
  35.1 2.0 %copy.67 = f32[8,2,128,148]{2,1,3,0:T(2,128)} copy(f32[8,2,128,148]{2,0,3,1:T(8,128)S(1)} %pad_maximum_fusion) | data formatting | bytes 2424832 | tf_op jit(solution)/shard_map/stack | solution.py:70
  37.1 0.0 copy-start.2
  37.1 4.9 %all-to-all-start.1 = ((f32[8,2,128,148]{2,1,3,0:T(2,128)}), f32[8,2,128,148]{2,1,3,0:T(2,128)S(1)}, u32[]{:S(2)}, u32[]{:S(2)}) async-start(f32[8,2,128,148]{2,1,3,0:T(2,128)} %copy.67), calls=%async_computation.1 | async-start | bytes 2424832 | tf_op jit(solution)/shard_map/all_to_all | solution.py:71
  42.0 0.0 copy-start.6
  42.1 0.0 copy-done.2
  42.1 0.3 copy.70
  42.4 0.3 copy-done.6
  42.7 0.1 constant_dynamic-slice_fusion
  42.8 0.6 fusion.65
  44.7 0.6 %fusion.55 = pred[2048]{0:T(1024)(128)(4,1)S(1)} fusion(s32[]{:T(128)} %bitcast.1, s32[]{:T(128)} %bitcast), kind=kLoop, calls=%fused_computation.86 | loop fusion | flops 6144 | bytes 2056 | tf_op jit(solution)/shard_map/and | solution.py:84
  45.3 14.4 %all-to-all-done.1 = f32[8,2,128,148]{2,1,3,0:T(2,128)S(1)} async-done(((f32[8,2,128,148]{2,1,3,0:T(2,128)}), f32[8,2,128,148]{2,1,3,0:T(2,128)S(1)}, u32[]{:S(2)}, u32[]{:S(2)}) %all-to-all-start.1) | async-done | bytes 1212448 | tf_op jit(solution)/shard_map/all_to_all | solution.py:71
  59.7 0.2 copy.109
  60.0 0.1 slice.154
  60.1 0.3 copy.69
  60.5 0.3 fusion.16
  60.8 1.3 %copy.71 = f32[1,128,2048]{2,1,0:T(8,128)} copy(f32[1,128,2048]{1,2,0:T(8,128)S(1)} %fusion.16) | data formatting | bytes 2097152 | tf_op jit(solution)/shard_map/jit(_where)/select_n | solution.py:87
  (11 shorter events, 0.1 us)
Async XLA Ops:
  0.0 6.7 %copy-start = (f32[16,21]{1,0:T(8,128)S(1)}, f32[16,21]{1,0:T(8,128)}, u32[]{:S(2)}) copy-start(f32[16,21]{1,0:T(8,128)} %param.12) | copy-start | bytes 4036
  0.7 7.8 %collective-permute-start = (f32[10,128]{1,0:T(8,128)S(1)}, f32[10,128]{1,0:T(8,128)S(1)}, u32[]{:S(2)}, u32[]{:S(2)}) collective-permute-start(f32[10,128]{1,0:T(8,128)S(1)} %get-tuple-element.39), channel_id=1, source_target_pairs={{0,16},{16,32},{32,48},{48,64},{64,80},{80,96},{96,112},{112,128},... | collective-permute-start | bytes 15368 | tf_op jit(solution)/shard_map/ppermute | solution.py:49
  4.2 7.7 %collective-permute-start.1 = (f32[10,128]{1,0:T(8,128)S(1)}, f32[10,128]{1,0:T(8,128)S(1)}, u32[]{:S(2)}, u32[]{:S(2)}) collective-permute-start(f32[10,128]{1,0:T(8,128)S(1)} %get-tuple-element.40), channel_id=1, source_target_pairs={{16,0},{32,16},{48,32},{64,48},{80,64},{96,80},{112,96},{128,112},... | collective-permute-start | bytes 15368 | tf_op jit(solution)/shard_map/ppermute | solution.py:50
  6.7 1.9 %copy-start.5 = (f32[1,16,6]{1,0,2:T(1,128)S(1)}, f32[1,16,6]{1,0,2:T(1,128)}, u32[]{:S(2)}) copy-start(f32[1,16,6]{1,0,2:T(1,128)} %param.13) | copy-start | bytes 1156
  6.7 5.2 %copy-start.3 = (f32[128,128]{1,0:T(8,128)S(1)}, f32[128,128]{1,0:T(8,128)}, u32[]{:S(2)}) copy-start(f32[128,128]{1,0:T(8,128)} %param.10) | copy-start | bytes 196612
  6.7 11.6 %copy-start.4 = (f32[16,21]{1,0:T(8,128)S(1)}, f32[16,21]{1,0:T(8,128)}, u32[]{:S(2)}) copy-start(f32[16,21]{1,0:T(8,128)} %param.11) | copy-start | bytes 4036
  11.9 13.1 %collective-permute-start.2 = (f32[148,128]{1,0:T(8,128)S(1)}, f32[148,128]{1,0:T(8,128)S(1)}, u32[]{:S(2)}, u32[]{:S(2)}) collective-permute-start(f32[148,128]{1,0:T(8,128)S(1)} %pad_maximum_fusion.1), channel_id=1, source_target_pairs={{0,8},{8,0},{1,9},{9,1},{2,10},{10,2},{3,11},{11,3},{4,12},{12,4},... | collective-permute-start | bytes 227336 | tf_op jit(solution)/shard_map/ppermute | solution.py:53
  20.7 10.3 %all-to-all-start = ((f32[8,16,6]{1,2,0:T(8,128)}), f32[8,16,6]{1,2,0:T(8,128)S(1)}, u32[]{:S(2)}, u32[]{:S(2)}) async-start(f32[8,16,6]{1,2,0:T(8,128)} %broadcast_in_dim.14), calls=%async_computation | async-start | bytes 65536 | tf_op jit(solution)/shard_map/all_to_all | solution.py:56
  25.0 3.4 %copy-start.1 = (f32[16,128,148,1]{1,0,2,3:T(8,128)S(1)}, f32[16,128,148,1]{1,0,2,3:T(8,128)}, u32[]{:S(2)}) copy-start(f32[16,128,148,1]{1,0,2,3:T(8,128)} %fusion.11) | copy-start | bytes 3637252
  37.1 4.9 %copy-start.2 = (f32[1,128,2048]{2,1,0:T(8,128)S(1)}, f32[1,128,2048]{2,1,0:T(8,128)}, u32[]{:S(2)}) copy-start(f32[1,128,2048]{2,1,0:T(8,128)} %param.14) | copy-start | bytes 3145732
  37.1 22.6 %all-to-all-start.1 = ((f32[8,2,128,148]{2,1,3,0:T(2,128)}), f32[8,2,128,148]{2,1,3,0:T(2,128)S(1)}, u32[]{:S(2)}, u32[]{:S(2)}) async-start(f32[8,2,128,148]{2,1,3,0:T(2,128)} %copy.67), calls=%async_computation.1 | async-start | bytes 2424832 | tf_op jit(solution)/shard_map/all_to_all | solution.py:71
  42.0 0.7 %copy-start.6 = (s32[16,2]{0,1:T(2,128)S(1)}, s32[16,2]{0,1:T(2,128)}, u32[]{:S(2)}) copy-start(s32[16,2]{0,1:T(2,128)} %param.15) | copy-start | bytes 388

commit v16 on v12

--- a/solution.py
+++ b/solution.py
@@ -20,7 +20,7 @@
 def banded(taps, rows, cols):
     offset = lax.broadcasted_iota(jnp.int32, (rows, cols), 1) - lax.broadcasted_iota(jnp.int32, (rows, cols), 0)
     picks = (offset[None] == jnp.arange(taps.shape[1])[:, None, None]).astype(jnp.float32)
-    return jnp.einsum("ka,arc->krc", taps, picks, precision=lax.Precision.HIGHEST)
+    return jnp.einsum("ka,arc->krc", taps, picks, precision=lax.Precision.HIGH)
 
 
 def separable(blocks, row_taps, col_taps, tile_rows, span):

time: 61.1 us -> 60.6 us (level)
  transfers between devices with their start and end apart: 5 -> 5, of which waited for: 1 -> 1; matrix products, arithmetic and copies ran while one was open for 21% -> 20% of each run, Pallas kernels for 0% -> 0%
where the time goes in v16:
time: 60.6 us; the launch traced here: 60.2 us
  starting transfers between devices  23.5 us (39%)
  waiting for transfers between devices  14.5 us (24%)
  matrix products  11.9 us (20%)
  local copies, waits for them, and re-layouts  6.7 us (11%)
  other arithmetic  2.06 us (3%)
  between operations  1.55 us (3%)
    all_to_all x1, waiting for transfers between devices, local(): parts = lax.all_to_all(models, 'xc', 0, 0, tiled=True)  14.5 us
    ppermute x1, starting transfers between devices, local(): pair = jnp.stack([template, lax.ppermute(template, 'zhi', swap)])  6.29 us
    all_to_all x1, starting transfers between devices, local(): parts = lax.all_to_all(models, 'xc', 0, 0, tiled=True)  4.92 us
    ppermute x1, starting transfers between devices, local(): below = lax.ppermute(pair[:, :half], 'tile', up)  4.47 us
    all_to_all x1, starting transfers between devices, local(): half_coeffs = lax.all_to_all(copies, 'xc', 0, 0, tiled=True)  4.3 us
    ppermute x1, starting transfers between devices, local(): above = lax.ppermute(pair[:, tile_rows - half:], 'tile', down)  3.48 us
    dot_general x1, matrix products, separable(): jnp.einsum('bac,kcd->bkad', blocks, across, precision=lax.Precision.HIGH)  3.39 us
    dot_general x2, matrix products, local(): jnp.einsum('vkt,krc->tvrc', half_coeffs, basis[b], precision=lax.Precisio...  3.18 us
  transfers between devices with their start and end apart: 5, of which 1 were waited for; matrix products, arithmetic and copies ran while one was open for 20% of the time, Pallas kernels for 0%

profile of v16, /device:TPU:32, one launch (start us, length us, event | category | flops | bytes accessed | tf_op | source)
XLA Modules:
  0.0 60.2 jit_solution(17546141409279051063)
XLA Ops:
  0.0 0.0 copy-start
  0.0 6.3 %collective-permute-start = (f32[128,128]{1,0:T(8,128)}, f32[128,128]{1,0:T(8,128)S(1)}, u32[]{:S(2)}, u32[]{:S(2)}) collective-permute-start(f32[128,128]{1,0:T(8,128)} %param.10), channel_id=1, source_target_pairs={{0,8},{8,0},{1,9},{9,1},{2,10},{10,2},{3,11},{11,3},{4,12},{12,4},... | collective-permute-start | bytes 196616 | tf_op jit(solution)/shard_map/ppermute | solution.py:48
  6.3 0.7 %copy.110 = f32[1,16,6]{1,2,0:T(8,128)S(1)} copy(f32[1,16,6]{1,0,2:T(1,128)} %param.13) | data formatting | bytes 768
  7.1 0.0 copy-done
  7.1 0.0 copy-start.4
  7.1 1.3 %fusion.10 = f32[16,168,148,1]{1,0,2,3:T(8,128)S(1)} fusion(s32[148,168]{1,0:T(8,128)S(1)} %iota_subtract_fusion, f32[16,21]{1,0:T(8,128)S(1)} %copy-done), kind=kOutput, calls=%fused_computation.12 | convolution fusion | flops 50647968 | bytes 1692096 | tf_op jit(solution)/shard_map/ka,arc->krc/dot_general | solution.py:23
  8.4 0.0 copy-start.3
  8.4 0.1 broadcast_multiply_fusion.1
  8.5 0.0 copy-done.4
  8.5 1.7 %fusion.11 = f32[16,128,148,1]{1,0,2,3:T(8,128)} fusion(s32[128,148]{0,1:T(8,128)S(1)} %iota_subtract_fusion.1, f32[16,21]{1,0:T(8,128)S(1)} %copy-done.4), kind=kOutput, calls=%fused_computation.13 | convolution fusion | flops 38588928 | bytes 1289536 | tf_op jit(solution)/shard_map/ka,arc->krc/dot_general | solution.py:23
  10.2 0.0 collective-permute-done
  10.2 0.0 copy-done.3
  10.2 3.5 %collective-permute-start.1 = (f32[2,10,128]{2,1,0:T(8,128)S(1)}, f32[2,10,128]{2,1,0:T(8,128)S(1)}, u32[]{:S(2)}, u32[]{:S(2)}) collective-permute-start(f32[2,10,128]{2,1,0:T(8,128)S(1)} %get-tuple-element.39), channel_id=1, source_target_pairs={{0,16},{16,32},{32,48},{48,64},{64,80},{80,96},{96,112},{112,128},... | collective-permute-start | bytes 30728 | tf_op jit(solution)/shard_map/ppermute | solution.py:51
  13.7 4.5 %collective-permute-start.2 = (f32[2,10,128]{2,1,0:T(8,128)S(1)}, f32[2,10,128]{2,1,0:T(8,128)S(1)}, u32[]{:S(2)}, u32[]{:S(2)}) collective-permute-start(f32[2,10,128]{2,1,0:T(8,128)S(1)} %get-tuple-element.40), channel_id=1, source_target_pairs={{16,0},{32,16},{48,32},{64,48},{80,64},{96,80},{112,96},{128,112},... | collective-permute-start | bytes 30728 | tf_op jit(solution)/shard_map/ppermute | solution.py:52
  18.2 0.6 %broadcast_in_dim.14 = f32[8,16,6]{1,2,0:T(8,128)} broadcast(f32[16,6]{0,1:T(8,128)S(1)} %bitcast.161), dimensions={1,2} | broadcast | bytes 3456 | tf_op jit(solution)/shard_map/broadcast_in_dim | solution.py:53
  18.8 4.3 %all-to-all-start = ((f32[8,16,6]{1,2,0:T(8,128)}), f32[8,16,6]{1,2,0:T(8,128)S(1)}, u32[]{:S(2)}, u32[]{:S(2)}) async-start(f32[8,16,6]{1,2,0:T(8,128)} %broadcast_in_dim.14), calls=%async_computation | async-start | bytes 65536 | tf_op jit(solution)/shard_map/all_to_all | solution.py:55
  23.1 0.0 collective-permute-done.1
  23.1 0.0 collective-permute-done.2
  23.1 0.0 copy-start.1
  23.1 3.4 %fusion.3 = f32[16,148,2,148]{3,1,2,0:T(8,128)S(1)} fusion(f32[16,168,148,1]{1,0,2,3:T(8,128)S(1)} %fusion.10, f32[1,148,128]{2,1,0:T(8,128)S(1)} %get-tuple-element.38, f32[1,148,128]{2,1,0:T(8,128)S(1)} %get-tuple-element.37), kind=kOutput, calls=%fused_computation.4 | convolution fusion | flops 706833792 | bytes 4546560 | tf_op jit(solution)/shard_map/bac,kcd->bkad/dot_general | solution.py:30
  26.6 0.0 copy-done.1
  26.6 2.4 %fusion.7 = f32[2,16,128,148]{2,3,0,1:T(8,128)S(1)} fusion(f32[16,148,2,148]{3,1,2,0:T(8,128)S(1)} %fusion.3, f32[16,128,148,1]{1,0,2,3:T(8,128)S(1)} %copy-done.1), kind=kOutput, calls=%fused_computation.11 | convolution fusion | flops 538312704 | bytes 6440960 | tf_op jit(solution)/shard_map/kra,bkad->bkrd/dot_general | solution.py:31
  29.0 0.2 slice_bitcast_fusion.1
  29.2 0.0 all-to-all-done
  29.2 1.6 %convolution_bitcast_fusion = f32[6,8,128,148]{2,1,3,0:T(8,128)S(1)} fusion(f32[16,128,148]{1,2,0:T(8,128)S(1)} %get-tuple-element.34, f32[8,16,6,1]{1,2,0,3:T(8,128)S(1)} %bitcast.160), kind=kOutput, calls=%fused_computation.6 | convolution fusion | flops 87293952 | bytes 4852736 | tf_op jit(solution)/shard_map/vkt,krc->tvrc/dot_general | solution.py:70
  30.8 1.6 %convolution_bitcast_fusion.1 = f32[6,8,128,148]{2,1,0,3:T(8,128)S(1)} fusion(f32[16,128,148,1]{1,2,0,3:T(8,128)S(1)} %get-tuple-element.33, f32[8,16,6]{1,2,0:T(8,128)S(1)} %all-to-all-done), kind=kOutput, calls=%fused_computation.7 | convolution fusion | flops 87293952 | bytes 4852736 | tf_op jit(solution)/shard_map/vkt,krc->tvrc/dot_general | solution.py:70
  32.4 0.4 fusion.29
  32.8 0.4 fusion.19
  33.2 0.1 pad_maximum_fusion
  33.3 2.0 %copy.67 = f32[8,2,128,148]{2,1,3,0:T(2,128)} copy(f32[8,2,128,148]{2,0,3,1:T(8,128)S(1)} %pad_maximum_fusion) | data formatting | bytes 2424832 | tf_op jit(solution)/shard_map/stack | solution.py:72
  35.2 0.0 copy-start.2
  35.2 4.9 %all-to-all-start.1 = ((f32[8,2,128,148]{2,1,3,0:T(2,128)}), f32[8,2,128,148]{2,1,3,0:T(2,128)S(1)}, u32[]{:S(2)}, u32[]{:S(2)}) async-start(f32[8,2,128,148]{2,1,3,0:T(2,128)} %copy.67), calls=%async_computation.1 | async-start | bytes 2424832 | tf_op jit(solution)/shard_map/all_to_all | solution.py:73
  40.2 0.0 copy-start.5
  40.2 0.0 copy-done.2
  40.2 0.3 copy.70
  40.5 0.3 copy-done.5
  40.8 0.1 constant_dynamic-slice_fusion
  40.9 0.5 fusion.66
  42.7 0.6 %fusion.57 = pred[2048]{0:T(1024)(128)(4,1)S(1)} fusion(s32[]{:T(128)} %bitcast.1, s32[]{:T(128)} %bitcast), kind=kLoop, calls=%fused_computation.93 | loop fusion | flops 6144 | bytes 2056 | tf_op jit(solution)/shard_map/and | solution.py:86
  43.3 14.5 %all-to-all-done.1 = f32[8,2,128,148]{2,1,3,0:T(2,128)S(1)} async-done(((f32[8,2,128,148]{2,1,3,0:T(2,128)}), f32[8,2,128,148]{2,1,3,0:T(2,128)S(1)}, u32[]{:S(2)}, u32[]{:S(2)}) %all-to-all-start.1) | async-done | bytes 1212448 | tf_op jit(solution)/shard_map/all_to_all | solution.py:73
  57.9 0.2 copy.109
  58.1 0.1 slice.168
  58.2 0.3 copy.69
  58.6 0.3 fusion.16
  58.9 1.3 %copy.71 = f32[1,128,2048]{2,1,0:T(8,128)} copy(f32[1,128,2048]{1,2,0:T(8,128)S(1)} %fusion.16) | data formatting | bytes 2097152 | tf_op jit(solution)/shard_map/jit(_where)/select_n | solution.py:89
  (12 shorter events, 0.1 us)
Async XLA Ops:
  0.0 7.1 %copy-start = (f32[16,21]{1,0:T(8,128)S(1)}, f32[16,21]{1,0:T(8,128)}, u32[]{:S(2)}) copy-start(f32[16,21]{1,0:T(8,128)} %param.12) | copy-start | bytes 4036
  0.0 10.2 %collective-permute-start = (f32[128,128]{1,0:T(8,128)}, f32[128,128]{1,0:T(8,128)S(1)}, u32[]{:S(2)}, u32[]{:S(2)}) collective-permute-start(f32[128,128]{1,0:T(8,128)} %param.10), channel_id=1, source_target_pairs={{0,8},{8,0},{1,9},{9,1},{2,10},{10,2},{3,11},{11,3},{4,12},{12,4},... | collective-permute-start | bytes 196616 | tf_op jit(solution)/shard_map/ppermute | solution.py:48
  7.1 1.4 %copy-start.4 = (f32[16,21]{1,0:T(8,128)S(1)}, f32[16,21]{1,0:T(8,128)}, u32[]{:S(2)}) copy-start(f32[16,21]{1,0:T(8,128)} %param.11) | copy-start | bytes 4036
  8.4 1.8 %copy-start.3 = (f32[128,128]{1,0:T(8,128)S(1)}, f32[128,128]{1,0:T(8,128)}, u32[]{:S(2)}) copy-start(f32[128,128]{1,0:T(8,128)} %param.10) | copy-start | bytes 196612
  10.2 12.9 %collective-permute-start.1 = (f32[2,10,128]{2,1,0:T(8,128)S(1)}, f32[2,10,128]{2,1,0:T(8,128)S(1)}, u32[]{:S(2)}, u32[]{:S(2)}) collective-permute-start(f32[2,10,128]{2,1,0:T(8,128)S(1)} %get-tuple-element.39), channel_id=1, source_target_pairs={{0,16},{16,32},{32,48},{48,64},{64,80},{80,96},{96,112},{112,128},... | collective-permute-start | bytes 30728 | tf_op jit(solution)/shard_map/ppermute | solution.py:51
  13.7 9.4 %collective-permute-start.2 = (f32[2,10,128]{2,1,0:T(8,128)S(1)}, f32[2,10,128]{2,1,0:T(8,128)S(1)}, u32[]{:S(2)}, u32[]{:S(2)}) collective-permute-start(f32[2,10,128]{2,1,0:T(8,128)S(1)} %get-tuple-element.40), channel_id=1, source_target_pairs={{16,0},{32,16},{48,32},{64,48},{80,64},{96,80},{112,96},{128,112},... | collective-permute-start | bytes 30728 | tf_op jit(solution)/shard_map/ppermute | solution.py:52
  18.8 10.4 %all-to-all-start = ((f32[8,16,6]{1,2,0:T(8,128)}), f32[8,16,6]{1,2,0:T(8,128)S(1)}, u32[]{:S(2)}, u32[]{:S(2)}) async-start(f32[8,16,6]{1,2,0:T(8,128)} %broadcast_in_dim.14), calls=%async_computation | async-start | bytes 65536 | tf_op jit(solution)/shard_map/all_to_all | solution.py:55
  23.1 3.4 %copy-start.1 = (f32[16,128,148,1]{1,0,2,3:T(8,128)S(1)}, f32[16,128,148,1]{1,0,2,3:T(8,128)}, u32[]{:S(2)}) copy-start(f32[16,128,148,1]{1,0,2,3:T(8,128)} %fusion.11) | copy-start | bytes 3637252
  35.2 4.9 %copy-start.2 = (f32[1,128,2048]{2,1,0:T(8,128)S(1)}, f32[1,128,2048]{2,1,0:T(8,128)}, u32[]{:S(2)}) copy-start(f32[1,128,2048]{2,1,0:T(8,128)} %param.14) | copy-start | bytes 3145732
  35.2 22.6 %all-to-all-start.1 = ((f32[8,2,128,148]{2,1,3,0:T(2,128)}), f32[8,2,128,148]{2,1,3,0:T(2,128)S(1)}, u32[]{:S(2)}, u32[]{:S(2)}) async-start(f32[8,2,128,148]{2,1,3,0:T(2,128)} %copy.67), calls=%async_computation.1 | async-start | bytes 2424832 | tf_op jit(solution)/shard_map/all_to_all | solution.py:73
  40.2 0.7 %copy-start.5 = (s32[16,2]{0,1:T(2,128)S(1)}, s32[16,2]{0,1:T(2,128)}, u32[]{:S(2)}) copy-start(s32[16,2]{0,1:T(2,128)} %param.15) | copy-start | bytes 388

commit v17 on v16

--- a/solution.py
+++ b/solution.py
@@ -46,13 +46,14 @@
 
     swap = [(h, halves - 1 - h) for h in range(halves)]
     pair = jnp.stack([template, lax.ppermute(template, "zhi", swap)])
+    copies = jnp.broadcast_to(coeffs, (group,) + coeffs.shape[1:])
+    copies, pair = lax.optimization_barrier((copies, pair))
+    half_coeffs = lax.all_to_all(copies, "xc", 0, 0, tiled=True)
+    half_coeffs, pair = lax.optimization_barrier((half_coeffs, pair))
     down = [(i, i + 1) for i in range(tiles - 1)]
     up = [(i + 1, i) for i in range(tiles - 1)]
     above = lax.ppermute(pair[:, tile_rows - half :], "tile", down)
     below = lax.ppermute(pair[:, :half], "tile", up)
-    copies = jnp.broadcast_to(coeffs, (group,) + coeffs.shape[1:])
-    copies, pair = lax.optimization_barrier((copies, pair))
-    half_coeffs = lax.all_to_all(copies, "xc", 0, 0, tiled=True)
     extended = jnp.concatenate([above, pair, below], axis=1)
     own = extended[0]
     other = extended[1]

time: 60.6 us -> 67.6 us (1.12)
  the two profiles are of different devices: /device:TPU:32 before, /device:TPU:24 now
where the time goes in v17:
time: 67.6 us; the launch traced here: 67.3 us
  waiting for transfers between devices  24.6 us (36%)
  starting transfers between devices  21 us (31%)
  matrix products  11.9 us (18%)
  local copies, waits for them, and re-layouts  6.06 us (9%)
  other arithmetic  2.12 us (3%)
  between operations  1.6 us (2%)
    all_to_all x1, waiting for transfers between devices, local(): parts = lax.all_to_all(models, 'xc', 0, 0, tiled=True)  14.3 us
    ppermute x1, starting transfers between devices, local(): pair = jnp.stack([template, lax.ppermute(template, 'zhi', swap)])  7.19 us
    all_to_all x1, waiting for transfers between devices, local(): half_coeffs = lax.all_to_all(copies, 'xc', 0, 0, tiled=True)  5.44 us
    all_to_all x1, starting transfers between devices, local(): half_coeffs = lax.all_to_all(copies, 'xc', 0, 0, tiled=True)  4.3 us
    all_to_all x1, starting transfers between devices, local(): parts = lax.all_to_all(models, 'xc', 0, 0, tiled=True)  3.7 us
    ppermute x1, waiting for transfers between devices, local(): below = lax.ppermute(pair[:, :half], 'tile', up)  3.57 us
    dot_general x1, matrix products, separable(): jnp.einsum('bac,kcd->bkad', blocks, across, precision=lax.Precision.HIGH)  3.4 us
    ppermute x1, starting transfers between devices, local(): above = lax.ppermute(pair[:, tile_rows - half:], 'tile', down)  3.34 us
  transfers between devices with their start and end apart: 5, of which 4 were waited for; matrix products, arithmetic and copies ran while one was open for 7% of the time, Pallas kernels for 0%

profile of v17, /device:TPU:24, one launch (start us, length us, event | category | flops | bytes accessed | tf_op | source)
XLA Modules:
  0.0 67.3 jit_solution(10404669748007111636)
XLA Ops:
  0.0 0.0 copy-start
  0.0 7.2 %collective-permute-start = (f32[128,128]{1,0:T(8,128)}, f32[128,128]{1,0:T(8,128)S(1)}, u32[]{:S(2)}, u32[]{:S(2)}) collective-permute-start(f32[128,128]{1,0:T(8,128)} %param.10), channel_id=1, source_target_pairs={{0,8},{8,0},{1,9},{9,1},{2,10},{10,2},{3,11},{11,3},{4,12},{12,4},... | collective-permute-start | bytes 196616 | tf_op jit(solution)/shard_map/ppermute | solution.py:48
  7.3 0.1 broadcast_multiply_fusion.1
  7.4 0.0 copy-done
  7.4 0.0 copy-start.5
  7.4 0.0 copy-start.3
  7.4 0.0 copy-start.4
  7.4 1.3 %fusion.10 = f32[16,168,148,1]{1,0,2,3:T(8,128)S(1)} fusion(s32[148,168]{1,0:T(8,128)S(1)} %iota_subtract_fusion, f32[16,21]{1,0:T(8,128)S(1)} %copy-done), kind=kOutput, calls=%fused_computation.12 | convolution fusion | flops 50647968 | bytes 1692096 | tf_op jit(solution)/shard_map/ka,arc->krc/dot_general | solution.py:23
  8.7 0.0 copy-done.5
  8.7 1.2 %collective-permute-done = f32[128,128]{1,0:T(8,128)S(1)} collective-permute-done((f32[128,128]{1,0:T(8,128)}, f32[128,128]{1,0:T(8,128)S(1)}, u32[]{:S(2)}, u32[]{:S(2)}) %collective-permute-start) | collective-permute-done | bytes 65568 | tf_op jit(solution)/shard_map/ppermute | solution.py:48
  9.9 0.0 copy-done.3
  10.0 0.6 broadcast_in_dim.14
  10.6 4.3 %all-to-all-start = ((f32[8,16,6]{1,2,0:T(8,128)}), f32[8,16,6]{1,2,0:T(8,128)S(1)}, u32[]{:S(2)}, u32[]{:S(2)}) async-start(f32[8,16,6]{1,2,0:T(8,128)} %broadcast_in_dim.14), calls=%async_computation | async-start | bytes 65536 | tf_op jit(solution)/shard_map/all_to_all | solution.py:51
  14.9 5.4 %all-to-all-done = f32[8,16,6]{1,2,0:T(8,128)S(1)} async-done(((f32[8,16,6]{1,2,0:T(8,128)}), f32[8,16,6]{1,2,0:T(8,128)S(1)}, u32[]{:S(2)}, u32[]{:S(2)}) %all-to-all-start) | async-done | bytes 3104 | tf_op jit(solution)/shard_map/all_to_all | solution.py:51
  20.3 3.3 %collective-permute-start.1 = (f32[2,10,128]{2,1,0:T(8,128)S(1)}, f32[2,10,128]{2,1,0:T(8,128)S(1)}, u32[]{:S(2)}, u32[]{:S(2)}) collective-permute-start(f32[2,10,128]{2,1,0:T(8,128)S(1)} %get-tuple-element.43), channel_id=1, source_target_pairs={{0,16},{16,32},{32,48},{48,64},{64,80},{80,96},{96,112},{112,128},... | collective-permute-start | bytes 30728 | tf_op jit(solution)/shard_map/ppermute | solution.py:55
  23.7 2.5 %collective-permute-start.2 = (f32[2,10,128]{2,1,0:T(8,128)S(1)}, f32[2,10,128]{2,1,0:T(8,128)S(1)}, u32[]{:S(2)}, u32[]{:S(2)}) collective-permute-start(f32[2,10,128]{2,1,0:T(8,128)S(1)} %get-tuple-element.44), channel_id=1, source_target_pairs={{16,0},{32,16},{48,32},{64,48},{80,64},{96,80},{112,96},{128,112},... | collective-permute-start | bytes 30728 | tf_op jit(solution)/shard_map/ppermute | solution.py:56
  26.2 0.0 copy-done.4
  26.2 1.7 %fusion.11 = f32[16,128,148,1]{1,0,2,3:T(8,128)} fusion(s32[128,148]{0,1:T(8,128)S(1)} %iota_subtract_fusion.1, f32[16,21]{1,0:T(8,128)S(1)} %copy-done.4), kind=kOutput, calls=%fused_computation.13 | convolution fusion | flops 38588928 | bytes 1289536 | tf_op jit(solution)/shard_map/ka,arc->krc/dot_general | solution.py:23
  27.8 0.0 collective-permute-done.1
  27.9 3.6 %collective-permute-done.2 = f32[2,10,128]{2,1,0:T(8,128)S(1)} collective-permute-done((f32[2,10,128]{2,1,0:T(8,128)S(1)}, f32[2,10,128]{2,1,0:T(8,128)S(1)}, u32[]{:S(2)}, u32[]{:S(2)}) %collective-permute-start.2) | collective-permute-done | bytes 10272 | tf_op jit(solution)/shard_map/ppermute | solution.py:56
  31.5 0.0 copy-start.1
  31.5 3.4 %fusion.3 = f32[16,148,2,148]{3,1,2,0:T(8,128)S(1)} fusion(f32[16,168,148,1]{1,0,2,3:T(8,128)S(1)} %fusion.10, f32[1,148,128]{2,1,0:T(8,128)S(1)} %get-tuple-element.42, f32[1,148,128]{2,1,0:T(8,128)S(1)} %get-tuple-element.41), kind=kOutput, calls=%fused_computation.4 | convolution fusion | flops 706833792 | bytes 4546560 | tf_op jit(solution)/shard_map/bac,kcd->bkad/dot_general | solution.py:30
  34.9 0.0 copy-done.1
  34.9 2.4 %fusion.7 = f32[2,16,128,148]{2,3,0,1:T(8,128)S(1)} fusion(f32[16,148,2,148]{3,1,2,0:T(8,128)S(1)} %fusion.3, f32[16,128,148,1]{1,0,2,3:T(8,128)S(1)} %copy-done.1), kind=kOutput, calls=%fused_computation.11 | convolution fusion | flops 538312704 | bytes 6440960 | tf_op jit(solution)/shard_map/kra,bkad->bkrd/dot_general | solution.py:31
  37.3 0.2 slice_bitcast_fusion.1
  37.5 1.6 %convolution_bitcast_fusion.1 = f32[6,8,128,148]{2,1,0,3:T(8,128)S(1)} fusion(f32[16,128,148,1]{1,2,0,3:T(8,128)S(1)} %get-tuple-element.37, f32[8,16,6]{1,2,0:T(8,128)S(1)} %all-to-all-done), kind=kOutput, calls=%fused_computation.7 | convolution fusion | flops 87293952 | bytes 4852736 | tf_op jit(solution)/shard_map/vkt,krc->tvrc/dot_general | solution.py:71
  39.1 1.6 %convolution_bitcast_fusion = f32[6,8,128,148]{2,1,3,0:T(8,128)S(1)} fusion(f32[16,128,148]{1,2,0:T(8,128)S(1)} %get-tuple-element.38, f32[8,16,6,1]{1,2,0,3:T(8,128)S(1)} %bitcast.156), kind=kOutput, calls=%fused_computation.6 | convolution fusion | flops 87293952 | bytes 4852736 | tf_op jit(solution)/shard_map/vkt,krc->tvrc/dot_general | solution.py:71
  40.7 0.4 fusion.29
  41.1 0.4 fusion.19
  41.5 0.1 pad_maximum_fusion
  41.6 2.0 %copy.67 = f32[8,2,128,148]{2,1,3,0:T(2,128)} copy(f32[8,2,128,148]{2,0,3,1:T(8,128)S(1)} %pad_maximum_fusion) | data formatting | bytes 2424832 | tf_op jit(solution)/shard_map/stack | solution.py:73
  43.6 0.0 copy-start.2
  43.6 3.7 %all-to-all-start.1 = ((f32[8,2,128,148]{2,1,3,0:T(2,128)}), f32[8,2,128,148]{2,1,3,0:T(2,128)S(1)}, u32[]{:S(2)}, u32[]{:S(2)}) async-start(f32[8,2,128,148]{2,1,3,0:T(2,128)} %copy.67), calls=%async_computation.1 | async-start | bytes 2424832 | tf_op jit(solution)/shard_map/all_to_all | solution.py:74
  47.3 0.0 copy-start.6
  47.3 0.0 copy-done.2
  47.3 0.3 copy.70
  47.6 0.3 copy-done.6
  48.0 0.1 constant_dynamic-slice_fusion
  48.0 0.6 fusion.65
  49.9 0.6 fusion.55
  50.6 14.3 %all-to-all-done.1 = f32[8,2,128,148]{2,1,3,0:T(2,128)S(1)} async-done(((f32[8,2,128,148]{2,1,3,0:T(2,128)}), f32[8,2,128,148]{2,1,3,0:T(2,128)S(1)}, u32[]{:S(2)}, u32[]{:S(2)}) %all-to-all-start.1) | async-done | bytes 1212448 | tf_op jit(solution)/shard_map/all_to_all | solution.py:74
  64.9 0.2 copy.109
  65.1 0.1 slice.164
  65.3 0.3 copy.69
  65.6 0.3 fusion.16
  66.0 1.3 %copy.71 = f32[1,128,2048]{2,1,0:T(8,128)} copy(f32[1,128,2048]{1,2,0:T(8,128)S(1)} %fusion.16) | data formatting | bytes 2097152 | tf_op jit(solution)/shard_map/jit(_where)/select_n | solution.py:90
  (13 shorter events, 0.1 us)
Async XLA Ops:
  0.0 7.4 %copy-start = (f32[16,21]{1,0:T(8,128)S(1)}, f32[16,21]{1,0:T(8,128)}, u32[]{:S(2)}) copy-start(f32[16,21]{1,0:T(8,128)} %param.12) | copy-start | bytes 4036
  0.0 9.9 %collective-permute-start = (f32[128,128]{1,0:T(8,128)}, f32[128,128]{1,0:T(8,128)S(1)}, u32[]{:S(2)}, u32[]{:S(2)}) collective-permute-start(f32[128,128]{1,0:T(8,128)} %param.10), channel_id=1, source_target_pairs={{0,8},{8,0},{1,9},{9,1},{2,10},{10,2},{3,11},{11,3},{4,12},{12,4},... | collective-permute-start | bytes 196616 | tf_op jit(solution)/shard_map/ppermute | solution.py:48
  7.4 1.3 %copy-start.5 = (f32[1,16,6]{1,0,2:T(1,128)S(1)}, f32[1,16,6]{1,0,2:T(1,128)}, u32[]{:S(2)}) copy-start(f32[1,16,6]{1,0,2:T(1,128)} %param.13) | copy-start | bytes 1156
  7.4 2.5 %copy-start.3 = (f32[128,128]{1,0:T(8,128)S(1)}, f32[128,128]{1,0:T(8,128)}, u32[]{:S(2)}) copy-start(f32[128,128]{1,0:T(8,128)} %param.10) | copy-start | bytes 196612
  7.4 18.8 %copy-start.4 = (f32[16,21]{1,0:T(8,128)S(1)}, f32[16,21]{1,0:T(8,128)}, u32[]{:S(2)}) copy-start(f32[16,21]{1,0:T(8,128)} %param.11) | copy-start | bytes 4036
  10.6 9.7 %all-to-all-start = ((f32[8,16,6]{1,2,0:T(8,128)}), f32[8,16,6]{1,2,0:T(8,128)S(1)}, u32[]{:S(2)}, u32[]{:S(2)}) async-start(f32[8,16,6]{1,2,0:T(8,128)} %broadcast_in_dim.14), calls=%async_computation | async-start | bytes 65536 | tf_op jit(solution)/shard_map/all_to_all | solution.py:51
  20.3 7.5 %collective-permute-start.1 = (f32[2,10,128]{2,1,0:T(8,128)S(1)}, f32[2,10,128]{2,1,0:T(8,128)S(1)}, u32[]{:S(2)}, u32[]{:S(2)}) collective-permute-start(f32[2,10,128]{2,1,0:T(8,128)S(1)} %get-tuple-element.43), channel_id=1, source_target_pairs={{0,16},{16,32},{32,48},{48,64},{64,80},{80,96},{96,112},{112,128},... | collective-permute-start | bytes 30728 | tf_op jit(solution)/shard_map/ppermute | solution.py:55
  23.7 7.7 %collective-permute-start.2 = (f32[2,10,128]{2,1,0:T(8,128)S(1)}, f32[2,10,128]{2,1,0:T(8,128)S(1)}, u32[]{:S(2)}, u32[]{:S(2)}) collective-permute-start(f32[2,10,128]{2,1,0:T(8,128)S(1)} %get-tuple-element.44), channel_id=1, source_target_pairs={{16,0},{32,16},{48,32},{64,48},{80,64},{96,80},{112,96},{128,112},... | collective-permute-start | bytes 30728 | tf_op jit(solution)/shard_map/ppermute | solution.py:56
  31.5 3.4 %copy-start.1 = (f32[16,128,148,1]{1,0,2,3:T(8,128)S(1)}, f32[16,128,148,1]{1,0,2,3:T(8,128)}, u32[]{:S(2)}) copy-start(f32[16,128,148,1]{1,0,2,3:T(8,128)} %fusion.11) | copy-start | bytes 3637252
  43.6 3.7 %copy-start.2 = (f32[1,128,2048]{2,1,0:T(8,128)S(1)}, f32[1,128,2048]{2,1,0:T(8,128)}, u32[]{:S(2)}) copy-start(f32[1,128,2048]{2,1,0:T(8,128)} %param.14) | copy-start | bytes 3145732
  43.6 21.3 %all-to-all-start.1 = ((f32[8,2,128,148]{2,1,3,0:T(2,128)}), f32[8,2,128,148]{2,1,3,0:T(2,128)S(1)}, u32[]{:S(2)}, u32[]{:S(2)}) async-start(f32[8,2,128,148]{2,1,3,0:T(2,128)} %copy.67), calls=%async_computation.1 | async-start | bytes 2424832 | tf_op jit(solution)/shard_map/all_to_all | solution.py:74
  47.3 0.7 %copy-start.6 = (s32[16,2]{0,1:T(2,128)S(1)}, s32[16,2]{0,1:T(2,128)}, u32[]{:S(2)}) copy-start(s32[16,2]{0,1:T(2,128)} %param.15) | copy-start | bytes 388
